TPU v7x, 256 devices: a whole 4x4x8 slice. The times are simulated.
256 devices in a mesh: wide: 16 (over z, core), narrow: 16 (over y, x).
Axes of the slice: x: 4, y: 4, z: 8, core: 2. Of those that a mesh axis runs over, the one named last changes fastest.
Arguments:
- screens: bfloat16 [4, 4096, 4096], P(None, 'wide'), may hold values from -3 to 3
- offsets: int32 [2, 128, 4], replicated, may hold values from 0 to 2752, as said below
- valid: int32 [2, 80, 80], P(None, 'narrow'), may hold values from 0 to 1, as said below
- recon: bfloat16 [25600, 5120], P('narrow', 'wide'), may hold values from -0.0390625 to 0.0390625
Outputs:
- slopes: float32 [2, 64, 2, 80, 80], P(None, 'wide', None, 'narrow')
- commands: float32 [64, 5120], P('narrow', 'wide')
Inputs may be any that keep to these rules, and one draw needn't show every extreme that they name: For each coordinate and each layer, the offsets of all items lie within 64 of the smallest, and the largest is exactly 64 above the smallest. In the 5 subaperture rows of one index of narrow, each sensor has at most 300 valid subapertures; in every draw one index of narrow holds exactly 300 for each sensor.
All inputs are finite; a program needn't handle non-finite values.
Results may differ from a plain program's by a relative error of at most 0.0043.
Values may be sent and summed in bfloat16 or wider, within the bound.
No kernel may reach another device: no remote copies, remote signals or barrier semaphores. Data moves between devices by JAX's collectives and lax.ppermute only.
A program may use at most 128 MiB of HBM per device.

v0:
```python
import math

import jax
import jax.numpy as jnp
from jax import lax
from jax.sharding import PartitionSpec as P

L = 4
NSUB = 80
SAMP = 16
NPIX = 32
NSENS = 2
SPREAD = 64
FR_DEV = 4
PUP = 1280


def broadcast(block, axis, source):
    block = jnp.where(lax.axis_index(axis) == source, block, jnp.zeros_like(block))
    return lax.psum(block, axis)


def dft_table(samp, npix):
    sample_ids = jnp.arange(samp * samp, dtype=jnp.int32)
    pixel_ids = jnp.arange(npix * npix, dtype=jnp.int32)
    sample_row = sample_ids // samp
    sample_col = sample_ids % samp
    pixel_row = pixel_ids // npix - npix // 2
    pixel_col = pixel_ids % npix - npix // 2
    phase_turns = jnp.mod(
        sample_row[:, None] * pixel_row[None, :] + sample_col[:, None] * pixel_col[None, :], npix
    )
    angles = phase_turns.astype(jnp.float32) * jnp.float32(-2.0 * math.pi / npix)
    cosine = jnp.cos(angles).astype(jnp.bfloat16)
    sine_part = jnp.sin(angles).astype(jnp.bfloat16)
    top_rows = jnp.concatenate([cosine, sine_part], axis=1)
    bottom_rows = jnp.concatenate([-sine_part, cosine], axis=1)
    return jnp.concatenate([top_rows, bottom_rows], axis=0)


def subaperture_fields(pupil_phase, samp):
    sub_rows = pupil_phase.shape[0] // samp
    sub_cols = pupil_phase.shape[1] // samp
    samples = (
        pupil_phase.reshape(sub_rows, samp, sub_cols, samp)
        .transpose(0, 2, 1, 3)
        .reshape(sub_rows * sub_cols, samp * samp)
    )
    return jnp.concatenate([jnp.cos(samples), jnp.sin(samples)], axis=1).astype(jnp.bfloat16)


def centroids(fields, transform, npix):
    spectrum = jnp.dot(fields, transform, preferred_element_type=jnp.float32)
    pixel_count = npix * npix
    real_part = spectrum[:, :pixel_count]
    imag_part = spectrum[:, pixel_count:]
    intensity = real_part * real_part + imag_part * imag_part
    pixel_ids = jnp.arange(pixel_count, dtype=jnp.int32)
    along_x = (pixel_ids % npix - npix // 2).astype(jnp.float32)
    along_y = (pixel_ids // npix - npix // 2).astype(jnp.float32)
    flux_total = jnp.sum(intensity, axis=1)
    centre_x = jnp.sum(intensity * along_x[None, :], axis=1) / flux_total
    centre_y = jnp.sum(intensity * along_y[None, :], axis=1) / flux_total
    return jnp.stack([centre_x, centre_y], axis=1)


def cut_windows(rows_block, row_first, col_first, pixel_rows):

    def cut_one(row_at, col_at):
        return lax.dynamic_slice(rows_block, (row_at, col_at), (pixel_rows, PUP))

    return jax.vmap(cut_one)(row_first, col_first).astype(jnp.float32)


def body(screens, offsets, valid, recon):
    wide_count = lax.axis_size("wide")
    wide_index = lax.axis_index("wide")
    narrow_index = lax.axis_index("narrow")
    band_rows = screens.shape[1]
    sub_rows = valid.shape[1]
    pixel_rows = sub_rows * SAMP
    union_cols = PUP + SPREAD
    local_items = FR_DEV * NSENS
    own_offsets = lax.dynamic_slice_in_dim(offsets, wide_index * local_items, local_items, 1)
    lowest = jnp.min(offsets, axis=1)
    band_blocks = [
        lax.dynamic_slice_in_dim(screens[which_layer], lowest[1, which_layer], union_cols, 1)
        for which_layer in range(L)
    ]
    pupil_phase = jnp.zeros((local_items, pixel_rows, PUP), jnp.float32)
    for which_layer in range(L):
        group_start = lowest[0, which_layer] + pixel_rows * narrow_index
        root_upper = group_start // band_rows
        root_lower = jnp.minimum(root_upper + 1, wide_count - 1)
        upper_rows = broadcast(band_blocks[which_layer], "wide", root_upper)
        lower_rows = broadcast(band_blocks[which_layer], "wide", root_lower)
        joined_rows = jnp.concatenate([upper_rows, lower_rows], axis=0)
        row_first = (
            own_offsets[0, :, which_layer] + pixel_rows * narrow_index - root_upper * band_rows
        )
        col_first = own_offsets[1, :, which_layer] - lowest[1, which_layer]
        pupil_phase = pupil_phase + cut_windows(joined_rows, row_first, col_first, pixel_rows)
    transform = dft_table(SAMP, NPIX)
    frame_phase = pupil_phase.reshape(FR_DEV, NSENS, pixel_rows, PUP)
    valid_flags = valid.reshape(-1)

    def frame_fields(frame_block):
        return jnp.concatenate(
            [subaperture_fields(frame_block[sensor_index], SAMP) for sensor_index in range(NSENS)],
            axis=0,
        )

    def one_frame(frame_block):
        return centroids(frame_fields(frame_block), transform, NPIX) * valid_flags[:, None].astype(
            jnp.float32
        )

    measured = lax.map(one_frame, frame_phase)
    measured = measured.reshape(FR_DEV, NSENS, sub_rows, NSUB, 2)
    slopes = measured.transpose(4, 0, 1, 2, 3)
    slope_vector = (
        measured.transpose(0, 2, 1, 3, 4)
        .reshape(FR_DEV, sub_rows * NSENS * NSUB * 2)
        .astype(jnp.bfloat16)
    )
    partial_commands = jnp.dot(
        lax.all_gather(slope_vector, "wide", axis=0, tiled=True),
        recon,
        preferred_element_type=jnp.float32,
    )
    commands = lax.psum_scatter(partial_commands, "narrow", scatter_dimension=0, tiled=True)
    return (slopes, commands)


def solution(mesh):
    return jax.shard_map(
        body,
        mesh=mesh,
        in_specs=(P(None, "wide", None), P(), P(None, "narrow", None), P("narrow", "wide")),
        out_specs=(P(None, "wide", None, "narrow", None), P("narrow", "wide")),
        check_vma=False,
    )
```

profile of v0, /device:TPU:1, one launch (start us, length us, event | category | flops | bytes accessed | tf_op | source)
XLA Modules:
  0.0 496.1 jit_solution(6549098456706438841)
XLA Ops:
  16.5 5.7 %fusion.54 = (bf16[1,256,4096]{2,1,0:T(8,128)(2,1)}, bf16[1,256,4096]{2,1,0:T(8,128)(2,1)}, bf16[1,256,4096]{2,1,0:T(8,128)(2,1)S(1)}, bf16[1,256,4096]{2,1,0:T(8,128)(2,1)}) fusion(bf16[4,256,4096]{2,1,0:T(8,128)(2,1)} %param.6), kind=kLoop, calls=%fused_computation.126 | loop fusion | bytes 16777216 | tf_op jit(solution)/shard_map/slice | solution.py:87
  24.7 4.1 select_bitcast_fusion.5
  28.8 3.9 select_bitcast_fusion.1
  33.4 2.6 compare_select_fusion.7
  36.1 4.3 fusion.48
  40.4 4.6 sine_convert_fusion.2
  46.6 116.4 %all-reduce.7.cloned.1.call-done = (bf16[256,1344]{1,0:T(8,128)(2,1)}, bf16[256,1344]{1,0:T(8,128)(2,1)}, bf16[256,1344]{1,0:T(8,128)(2,1)}, bf16[256,1344]{1,0:...) async-done(((bf16[256,1344]{1,0:T(8,128)(2,1)}, bf16[256,1344]{1,0:T(8,128)(2,1)}, ...) | async-done | bytes 5505040 | tf_op jit(solution)/shard_map/psum | solution.py:20
  163.0 2.6 pad_maximum_fusion
  165.7 24.3 %while.18 = (s32[]{:T(128)}, bf16[512,1344]{1,0:T(8,128)(2,1)}, s32[8,2]{0,1:T(2,128)S(1)}, bf16[8,80,1280]{2,1,0:T(8,128)(2,1)S(1)}, s32[]{:T(128)}) while((s32[]{:T(128)}, bf16[512,1344]{1,0:T(8,128)(2,1)}, s32[8,2]{0,1:T(2,128)S(1)}, bf16[8,80,1280]{2,1,0:T(8,128)(2,1)S(1)}, s32[]{:T(128)}) %tuple.146), condition=%wide.while_cond, body=%wide.while_body.sunk | while | flops 2 | bytes 409709 | solution.py:70
  166.4 2.4 bitcast_dynamic-update-slice_fusion.8
  169.5 2.4 bitcast_dynamic-update-slice_fusion.8
  172.5 2.4 bitcast_dynamic-update-slice_fusion.8
  175.6 2.4 bitcast_dynamic-update-slice_fusion.8
  178.6 2.4 bitcast_dynamic-update-slice_fusion.8
  181.7 2.4 bitcast_dynamic-update-slice_fusion.8
  184.7 2.4 bitcast_dynamic-update-slice_fusion.8
  187.7 2.4 bitcast_dynamic-update-slice_fusion.8
  190.1 2.9 pad_maximum_fusion.1
  194.4 28.6 %while.19 = (s32[]{:T(128)}, bf16[512,1344]{1,0:T(8,128)(2,1)}, s32[8,2]{0,1:T(2,128)S(1)}, bf16[8,80,1280]{2,1,0:T(8,128)(2,1)}, s32[]{:T(128)}) while((s32[]{:T(128)}, bf16[512,1344]{1,0:T(8,128)(2,1)}, s32[8,2]{0,1:T(2,128)S(1)}, bf16[8,80,1280]{2,1,0:T(8,128)(2,1)}, s32[]{:T(128)}) %tuple.143), condition=%wide.while_cond.1, body=%wide.while_body.1.sunk | while | flops 2 | bytes 411233 | solution.py:70
  195.0 3.0 bitcast_dynamic-update-slice_fusion.9
  198.6 3.0 bitcast_dynamic-update-slice_fusion.9
  202.1 3.0 bitcast_dynamic-update-slice_fusion.9
  205.7 3.0 bitcast_dynamic-update-slice_fusion.9
  209.3 3.0 bitcast_dynamic-update-slice_fusion.9
  212.9 3.0 bitcast_dynamic-update-slice_fusion.9
  216.4 3.0 bitcast_dynamic-update-slice_fusion.9
  220.0 3.0 bitcast_dynamic-update-slice_fusion.9
  223.0 2.4 pad_maximum_fusion.2
  225.5 23.4 %while.20 = (s32[]{:T(128)}, bf16[512,1344]{1,0:T(8,128)(2,1)}, s32[8,2]{0,1:T(2,128)S(1)}, bf16[8,80,1280]{2,1,0:T(8,128)(2,1)S(1)}, s32[]{:T(128)}) while((s32[]{:T(128)}, bf16[512,1344]{1,0:T(8,128)(2,1)}, s32[8,2]{0,1:T(2,128)S(1)}, bf16[8,80,1280]{2,1,0:T(8,128)(2,1)S(1)}, s32[]{:T(128)}) %tuple.140), condition=%wide.while_cond.2, body=%wide.while_body.2.sunk | while | flops 2 | bytes 409709 | solution.py:70
  226.2 2.3 bitcast_dynamic-update-slice_fusion.10
  229.1 2.3 bitcast_dynamic-update-slice_fusion.10
  232.0 2.3 bitcast_dynamic-update-slice_fusion.10
  235.0 2.3 bitcast_dynamic-update-slice_fusion.10
  237.9 2.3 bitcast_dynamic-update-slice_fusion.10
  240.8 2.3 bitcast_dynamic-update-slice_fusion.10
  243.7 2.3 bitcast_dynamic-update-slice_fusion.10
  246.7 2.3 bitcast_dynamic-update-slice_fusion.10
  248.9 2.9 pad_maximum_fusion.3
  251.9 24.1 %while.21 = (s32[]{:T(128)}, bf16[512,1344]{1,0:T(8,128)(2,1)}, s32[8,2]{0,1:T(2,128)S(1)}, bf16[8,80,1280]{2,1,0:T(8,128)(2,1)S(1)}, s32[]{:T(128)}) while((s32[]{:T(128)}, bf16[512,1344]{1,0:T(8,128)(2,1)}, s32[8,2]{0,1:T(2,128)S(1)}, bf16[8,80,1280]{2,1,0:T(8,128)(2,1)S(1)}, s32[]{:T(128)}) %tuple.137), condition=%wide.while_cond.3, body=%wide.while_body.3.sunk | while | flops 2 | bytes 409709 | solution.py:70
  252.6 2.3 bitcast_dynamic-update-slice_fusion.11
  255.6 2.3 bitcast_dynamic-update-slice_fusion.11
  258.6 2.3 bitcast_dynamic-update-slice_fusion.11
  261.6 2.3 bitcast_dynamic-update-slice_fusion.11
  264.7 2.3 bitcast_dynamic-update-slice_fusion.11
  267.7 2.3 bitcast_dynamic-update-slice_fusion.11
  270.7 2.3 bitcast_dynamic-update-slice_fusion.11
  273.7 2.3 bitcast_dynamic-update-slice_fusion.11
  276.0 4.9 convert_add_fusion
  280.9 98.5 %while.17 = (s32[]{:T(128)}, f32[4,800,2]{1,2,0:T(2,128)S(1)}, f32[4,2,80,1280]{3,2,1,0:T(8,128)}, bf16[512,2048]{1,0:T(8,128)(2,1)}, f32[800,1]{0,1:T(1,128)S(1)}, /*index=5*/s32[]{:T(128)}, s32[]{:T(128)}, s32[]{}, f32[]{:T(128)}) while((s32[]{:T(128)}, f32[4,800,2]{1,2,0:T(2,128)S(1)}, f32[4,2,80,1280]{3,2,1,0:T(8,128)}, ...), condition=%wide.region_13.14_spmd, body=%wide.region_9.13_spmd.sunk | while | flops 1687980416 | bytes 22656888 | solution.py:118
  280.9 5.2 %cosine_convert_fusion.4 = (bf16[1,1,80,1280]{3,2,1,0:T(8,128)(2,1)}, bf16[1,1,80,1280]{3,2,1,0:T(8,128)(2,1)}, bf16[1,1,80,1280]{3,2,1,0:T(8,128)(2,1)S(1)}, bf16[1,1,80,1280]{3,2,1,0:T(8,128)(2,1)S(1)}) fusion(f32[4,2,80,1280]{3,2,1,0:T(8,128)} %get-tuple-element.498, s32[]{:T(128)} %get-tuple-element.487, s32[]{:T(128)S(6)} %add.480), kind=kLoop, calls=%fused_computation.24.clone.1 | loop fusion | flops 409600 | bytes 1638408 | tf_op jit(solution)/shard_map/convert.15
  289.4 2.2 cos.49
  293.7 2.2 sin.47
  300.5 3.9 fusion.73
  305.6 5.2 %cosine_convert_fusion.4 = (bf16[1,1,80,1280]{3,2,1,0:T(8,128)(2,1)}, bf16[1,1,80,1280]{3,2,1,0:T(8,128)(2,1)}, bf16[1,1,80,1280]{3,2,1,0:T(8,128)(2,1)S(1)}, bf16[1,1,80,1280]{3,2,1,0:T(8,128)(2,1)S(1)}) fusion(f32[4,2,80,1280]{3,2,1,0:T(8,128)} %get-tuple-element.498, s32[]{:T(128)} %get-tuple-element.487, s32[]{:T(128)S(6)} %add.480), kind=kLoop, calls=%fused_computation.24.clone.1 | loop fusion | flops 409600 | bytes 1638408 | tf_op jit(solution)/shard_map/convert.15
  314.0 2.2 cos.49
  318.3 2.2 sin.47
  325.1 3.9 fusion.73
  330.2 5.2 %cosine_convert_fusion.4 = (bf16[1,1,80,1280]{3,2,1,0:T(8,128)(2,1)}, bf16[1,1,80,1280]{3,2,1,0:T(8,128)(2,1)}, bf16[1,1,80,1280]{3,2,1,0:T(8,128)(2,1)S(1)}, bf16[1,1,80,1280]{3,2,1,0:T(8,128)(2,1)S(1)}) fusion(f32[4,2,80,1280]{3,2,1,0:T(8,128)} %get-tuple-element.498, s32[]{:T(128)} %get-tuple-element.487, s32[]{:T(128)S(6)} %add.480), kind=kLoop, calls=%fused_computation.24.clone.1 | loop fusion | flops 409600 | bytes 1638408 | tf_op jit(solution)/shard_map/convert.15
  338.7 2.2 cos.49
  349.7 3.9 fusion.73
  354.8 5.2 %cosine_convert_fusion.4 = (bf16[1,1,80,1280]{3,2,1,0:T(8,128)(2,1)}, bf16[1,1,80,1280]{3,2,1,0:T(8,128)(2,1)}, bf16[1,1,80,1280]{3,2,1,0:T(8,128)(2,1)S(1)}, bf16[1,1,80,1280]{3,2,1,0:T(8,128)(2,1)S(1)}) fusion(f32[4,2,80,1280]{3,2,1,0:T(8,128)} %get-tuple-element.498, s32[]{:T(128)} %get-tuple-element.487, s32[]{:T(128)S(6)} %add.480), kind=kLoop, calls=%fused_computation.24.clone.1 | loop fusion | flops 409600 | bytes 1638408 | tf_op jit(solution)/shard_map/convert.15
  374.4 3.9 fusion.73
  380.2 16.5 %all-gather = bf16[16,4,1600]{2,1,0:T(4,128)(2,1)S(1)} all-gather(bf16[1,4,1600]{2,1,0:T(4,128)(2,1)S(1)} %copy.28), channel_id=1, replica_groups=mesh['wide'=16,'narrow'=16] {'wide'}, dimensions={0}, use_global_device_ids=true | all-gather | bytes 217600 | tf_op jit(solution)/shard_map/all_gather | solution.py:127
  399.7 88.3 %all-reduce.5.cloned.1.call-done = f32[64,320]{1,0:T(8,128)} async-done(((f32[64,320]{1,0:T(8,128)}), f32[64,320]{1,0:T(8,128)}) %all-reduce.5.cloned.1.call-update) | async-done | bytes 81936
  (181 shorter events, 81.5 us)
Async XLA Ops:
  7.2 389.6 %copy-start = (bf16[1600,320]{0,1:T(8,128)(2,1)S(1)}, bf16[1600,320]{0,1:T(8,128)(2,1)}, u32[]{:S(2)}) copy-start(bf16[1600,320]{0,1:T(8,128)(2,1)} %param.9) | copy-start | bytes 3072004
  7.2 155.8 %all-reduce.7.cloned.1.call-start = ((), (), s32[]{:S(2)}) async-start(), calls=%async_computation.1 | async-start | bytes 11534336 | tf_op jit(solution)/shard_map/psum | solution.py:20
  32.6 0.7 copy-start.7
  32.6 0.8 copy-start.6
  32.7 455.3 %all-reduce.5.cloned.1.call-start = ((), (), s32[]{:S(2)}) async-start(), calls=%async_computation | async-start | bytes 196608
  165.6 24.5 %copy-start.5 = (bf16[256,1344]{1,0:T(8,128)(2,1)S(1)}, bf16[256,1344]{1,0:T(8,128)(2,1)}, u32[]{:S(2)}) copy-start(bf16[256,1344]{1,0:T(8,128)(2,1)} %get-tuple-element.187) | copy-start | bytes 2064388
  190.1 4.3 copy-start.1
  193.1 29.9 %copy-start.4 = (bf16[256,1344]{1,0:T(8,128)(2,1)S(1)}, bf16[256,1344]{1,0:T(8,128)(2,1)}, u32[]{:S(2)}) copy-start(bf16[256,1344]{1,0:T(8,128)(2,1)} %get-tuple-element.185) | copy-start | bytes 2064388
  225.4 23.5 %copy-start.3 = (bf16[256,1344]{1,0:T(8,128)(2,1)S(1)}, bf16[256,1344]{1,0:T(8,128)(2,1)}, u32[]{:S(2)}) copy-start(bf16[256,1344]{1,0:T(8,128)(2,1)} %get-tuple-element.183) | copy-start | bytes 2064388
  248.9 2.9 copy-start.2
  379.4 18.4 %copy-start.8 = (u32[256]{0:T(256)S(1)}, u32[256]{0:T(256)}, u32[]{:S(2)}) copy-start(u32[256]{0:T(256)} %constant.269) | copy-start | bytes 3076
Sparse Core Ops, SparseCore 0:
  32.8 130.1 all-reduce.6
  398.0 89.9 all-reduce.4
where the time goes:
time: 500 us; the launch traced here: 496 us
  waiting for transfers between devices  205 us (41%)
  local copies, waits for them, and re-layouts  169 us (34%)
  other arithmetic  63.1 us (13%)
  between operations  25.2 us (5%)
  matrix products  16.5 us (3%)
  blocking collectives  16.5 us (3%)
    psum x1, waiting for transfers between devices, broadcast(): return lax.psum(block, axis)  116 us
    gather x96, local copies, waits for them, and re-layouts  100 us
    unnamed x3, waiting for transfers between devices  88.3 us
    cos x24, local copies, waits for them, and re-layouts, subaperture_fields(): jnp.cos(samples)  29.9 us
    sin x24, local copies, waits for them, and re-layouts, subaperture_fields(): jnp.sin(samples)  27.2 us
    another operation x8, other arithmetic  20.9 us
    all_gather x1, blocking collectives, body(): lax.all_gather(slope_vector, 'wide', axis=0, tiled=True)  16.5 us
    dot_general x4, matrix products, centroids(): spectrum = jnp.dot(fields, transform, preferred_element_type=jnp.float32)  15.4 us
  transfers between devices with their start and end apart: 2, of which 2 were waited for; matrix products, arithmetic and copies ran while one was open for 3% of the time, Pallas kernels for 0%

commit v1 on v0

--- a/solution.py
+++ b/solution.py
@@ -64,42 +64,37 @@
     return jnp.stack([centre_x, centre_y], axis=1)
 
 
-def cut_windows(rows_block, row_first, col_first, pixel_rows):
-
-    def cut_one(row_at, col_at):
-        return lax.dynamic_slice(rows_block, (row_at, col_at), (pixel_rows, PUP))
-
-    return jax.vmap(cut_one)(row_first, col_first).astype(jnp.float32)
-
-
 def body(screens, offsets, valid, recon):
-    wide_count = lax.axis_size("wide")
     wide_index = lax.axis_index("wide")
     narrow_index = lax.axis_index("narrow")
     band_rows = screens.shape[1]
     sub_rows = valid.shape[1]
     pixel_rows = sub_rows * SAMP
+    slab_rows = pixel_rows + SPREAD
     union_cols = PUP + SPREAD
     local_items = FR_DEV * NSENS
     own_offsets = lax.dynamic_slice_in_dim(offsets, wide_index * local_items, local_items, 1)
     lowest = jnp.min(offsets, axis=1)
-    band_blocks = [
-        lax.dynamic_slice_in_dim(screens[which_layer], lowest[1, which_layer], union_cols, 1)
-        for which_layer in range(L)
-    ]
-    pupil_phase = jnp.zeros((local_items, pixel_rows, PUP), jnp.float32)
+    pad = jnp.zeros((slab_rows, union_cols), screens.dtype)
+    slabs = []
     for which_layer in range(L):
+        band = lax.dynamic_slice_in_dim(screens[which_layer], lowest[1, which_layer], union_cols, 1)
+        padded = jnp.concatenate([pad, band, pad], axis=0)
         group_start = lowest[0, which_layer] + pixel_rows * narrow_index
-        root_upper = group_start // band_rows
-        root_lower = jnp.minimum(root_upper + 1, wide_count - 1)
-        upper_rows = broadcast(band_blocks[which_layer], "wide", root_upper)
-        lower_rows = broadcast(band_blocks[which_layer], "wide", root_lower)
-        joined_rows = jnp.concatenate([upper_rows, lower_rows], axis=0)
-        row_first = (
-            own_offsets[0, :, which_layer] + pixel_rows * narrow_index - root_upper * band_rows
-        )
-        col_first = own_offsets[1, :, which_layer] - lowest[1, which_layer]
-        pupil_phase = pupil_phase + cut_windows(joined_rows, row_first, col_first, pixel_rows)
+        row_at = jnp.clip(group_start - wide_index * band_rows + slab_rows, 0, band_rows + slab_rows)
+        slabs.append(lax.dynamic_slice_in_dim(padded, row_at, slab_rows, 0))
+    slabs = lax.psum(jnp.stack(slabs), "wide")
+    rel = own_offsets - lowest[:, None, :]
+    phases = []
+    for item in range(local_items):
+        acc = jnp.zeros((pixel_rows, PUP), jnp.float32)
+        for which_layer in range(L):
+            window = lax.dynamic_slice(
+                slabs[which_layer], (rel[0, item, which_layer], rel[1, item, which_layer]), (pixel_rows, PUP)
+            )
+            acc = acc + window.astype(jnp.float32)
+        phases.append(acc)
+    pupil_phase = jnp.stack(phases)
     transform = dft_table(SAMP, NPIX)
     frame_phase = pupil_phase.reshape(FR_DEV, NSENS, pixel_rows, PUP)
     valid_flags = valid.reshape(-1)

time: 500 us -> 396 us (0.79)
  between operations: 25.2 us -> 144 us
  waiting for transfers between devices: 205 us -> 86.4 us
  local copies, waits for them, and re-layouts: 169 us -> 77.4 us
  other arithmetic: 63.1 us -> 45.3 us
  blocking collectives: 16.5 us -> 21.9 us
    psum x1, waiting for transfers between devices: 116 us -> 0.01 us  [body(): slabs = lax.psum(jnp.stack(slabs), 'wide')]
    gather x96 -> x0, local copies, waits for them, and re-layouts: 100 us -> none
    concatenate x6 -> x0, other arithmetic: 10.9 us -> none  [the longest x4 10.9 us: body(): joined_rows = jnp.concatenate([upper_rows, lower_rows], axis=0)]
    select_n x3 -> x0, other arithmetic: 10.5 us -> none  [the longest x2 7.92 us: broadcast(): jnp.where(lax.axis_index(axis) == source, block, jnp.zeros_like(block))]
    all_gather x1, blocking collectives: 16.5 us -> 21.9 us  [body(): lax.all_gather(slope_vector, 'wide', axis=0, tiled=True)]
    another operation x8 -> x11, other arithmetic: 20.9 us -> 26 us
  transfers between devices with their start and end apart: 2 -> 2, of which waited for: 2 -> 1; matrix products, arithmetic and copies ran while one was open for 3% -> 4% of each run, Pallas kernels for 0% -> 0%
where the time goes in v1:
time: 396 us; the launch traced here: 392 us
  between operations  144 us (36%)
  waiting for transfers between devices  86.4 us (22%)
  local copies, waits for them, and re-layouts  77.4 us (20%)
  other arithmetic  45.3 us (11%)
  blocking collectives  21.9 us (6%)
  matrix products  16.5 us (4%)
    unnamed x3, waiting for transfers between devices  86.4 us
    cos x24, local copies, waits for them, and re-layouts, subaperture_fields(): jnp.cos(samples)  30.1 us
    sin x24, local copies, waits for them, and re-layouts, subaperture_fields(): jnp.sin(samples)  27.2 us
    all_gather x1, blocking collectives, body(): lax.all_gather(slope_vector, 'wide', axis=0, tiled=True)  21.9 us
    another operation x8, other arithmetic  20.9 us
    dot_general x4, matrix products, centroids(): spectrum = jnp.dot(fields, transform, preferred_element_type=jnp.float32)  15.4 us
  transfers between devices with their start and end apart: 2, of which 1 were waited for; matrix products, arithmetic and copies ran while one was open for 4% of the time, Pallas kernels for 0%

profile of v1, /device:TPU:1, one launch (start us, length us, event | category | flops | bytes accessed | tf_op | source)
XLA Modules:
  0.0 392.3 jit_solution(16243066642801625289)
XLA Ops:
  13.8 5.6 %fusion.50 = (bf16[1,256,4096]{2,1,0:T(8,128)(2,1)S(1)}, bf16[1,256,4096]{2,1,0:T(8,128)(2,1)}, bf16[1,256,4096]{2,1,0:T(8,128)(2,1)}, bf16[1,256,4096]{2,1,0:T(8,128)(2,1)}) fusion(bf16[4,256,4096]{2,1,0:T(8,128)(2,1)} %param.6), kind=kLoop, calls=%fused_computation.107 | loop fusion | bytes 16777216 | tf_op jit(solution)/shard_map/slice | solution.py:81
  24.6 2.3 dynamic-slice_bitcast_fusion
  26.9 2.0 dynamic-slice_bitcast_fusion.2
  29.0 3.2 fusion.35
  32.2 1.4 pad_maximum_fusion
  156.0 4.3 %fusion.48 = bf16[256,1024]{1,0:T(8,128)(2,1)S(1)} fusion(s32[1024]{0:T(1024)S(1)} %get-tuple-element.214, s32[256]{0:T(256)S(1)} %get-tuple-element.215, s32[1024]{0:T(1024)S(1)} %get-tuple-element.213, s32[256]{0:T(256)S(1)} %get-tuple-element.216), kind=kLoop, calls=%fused_computation.105 | loop fusion | flops 5242880 | bytes 534528 | tf_op jit(solution)/shard_map/neg | solution.py:37
  160.3 4.6 %sine_convert_fusion.2 = (bf16[256,1024]{1,0:T(8,128)(2,1)S(1)}, bf16[256,1024]{1,0:T(8,128)(2,1)S(1)}) fusion(s32[1024]{0:T(1024)S(1)} %get-tuple-element.214, s32[256]{0:T(256)S(1)} %get-tuple-element.215, s32[1024]{0:T(1024)S(1)} %get-tuple-element.213, s32[256]{0:T(256)S(1)} %get-tuple-element.216), kind=kLoop, calls=%fused_computation.55 | loop fusion | flops 4718592 | bytes 1058816 | tf_op jit(solution)/shard_map/convert_element_type | solution.py:35
  164.9 1.5 maximum_maximum_fusion
  166.5 1.5 fusion.51
  171.7 1.7 copy-done.1
  173.4 98.6 %while.13 = (s32[]{:T(128)}, f32[4,800,2]{1,2,0:T(2,128)S(1)}, f32[4,2,80,1280]{3,2,1,0:T(8,128)}, bf16[512,2048]{1,0:T(8,128)(2,1)}, f32[800,1]{0,1:T(1,128)S(1)}, /*index=5*/s32[]{:T(128)}, s32[]{:T(128)}, s32[]{}, f32[]{:T(128)}) while((s32[]{:T(128)}, f32[4,800,2]{1,2,0:T(2,128)S(1)}, f32[4,2,80,1280]{3,2,1,0:T(8,128)}, ...), condition=%wide.region_6.7_spmd, body=%wide.region_2.6_spmd.sunk | while | flops 1687980416 | bytes 22656888 | solution.py:113
  173.4 5.2 %cosine_convert_fusion.4 = (bf16[1,1,80,1280]{3,2,1,0:T(8,128)(2,1)}, bf16[1,1,80,1280]{3,2,1,0:T(8,128)(2,1)}, bf16[1,1,80,1280]{3,2,1,0:T(8,128)(2,1)S(1)}, bf16[1,1,80,1280]{3,2,1,0:T(8,128)(2,1)S(1)}) fusion(f32[4,2,80,1280]{3,2,1,0:T(8,128)} %get-tuple-element.294, s32[]{:T(128)} %get-tuple-element.283, s32[]{:T(128)S(6)} %add.641), kind=kLoop, calls=%fused_computation.16.clone.1 | loop fusion | flops 409600 | bytes 1638408 | tf_op jit(solution)/shard_map/convert.15
  178.6 1.2 cos.47
  179.9 1.1 copy.35
  181.9 2.2 cos.49
  184.1 1.1 copy.37
  185.2 1.0 cos.50
  186.2 2.2 sin.47
  188.4 1.1 copy.34
  189.5 1.0 sin.48
  190.5 1.2 sin.49
  191.7 1.1 copy.36
  193.0 3.9 fusion.70
  196.9 1.1 multiply_reduce_fusion.3
  198.1 5.2 %cosine_convert_fusion.4 = (bf16[1,1,80,1280]{3,2,1,0:T(8,128)(2,1)}, bf16[1,1,80,1280]{3,2,1,0:T(8,128)(2,1)}, bf16[1,1,80,1280]{3,2,1,0:T(8,128)(2,1)S(1)}, bf16[1,1,80,1280]{3,2,1,0:T(8,128)(2,1)S(1)}) fusion(f32[4,2,80,1280]{3,2,1,0:T(8,128)} %get-tuple-element.294, s32[]{:T(128)} %get-tuple-element.283, s32[]{:T(128)S(6)} %add.641), kind=kLoop, calls=%fused_computation.16.clone.1 | loop fusion | flops 409600 | bytes 1638408 | tf_op jit(solution)/shard_map/convert.15
  203.3 1.2 cos.47
  204.5 1.1 copy.35
  206.6 2.2 cos.49
  208.8 1.1 copy.37
  209.9 1.0 cos.50
  210.9 2.2 sin.47
  213.1 1.1 copy.34
  215.1 1.2 sin.49
  216.4 1.1 copy.36
  217.7 3.9 fusion.70
  221.6 1.1 multiply_reduce_fusion.3
  222.7 5.2 %cosine_convert_fusion.4 = (bf16[1,1,80,1280]{3,2,1,0:T(8,128)(2,1)}, bf16[1,1,80,1280]{3,2,1,0:T(8,128)(2,1)}, bf16[1,1,80,1280]{3,2,1,0:T(8,128)(2,1)S(1)}, bf16[1,1,80,1280]{3,2,1,0:T(8,128)(2,1)S(1)}) fusion(f32[4,2,80,1280]{3,2,1,0:T(8,128)} %get-tuple-element.294, s32[]{:T(128)} %get-tuple-element.283, s32[]{:T(128)S(6)} %add.641), kind=kLoop, calls=%fused_computation.16.clone.1 | loop fusion | flops 409600 | bytes 1638408 | tf_op jit(solution)/shard_map/convert.15
  228.0 1.2 cos.47
  229.2 1.1 copy.35
  231.2 2.2 cos.49
  233.5 1.1 copy.37
  234.5 1.0 cos.50
  235.5 2.2 sin.47
  237.7 1.1 copy.34
  239.8 1.2 sin.49
  241.0 1.1 copy.36
  242.4 3.9 fusion.70
  246.2 1.1 multiply_reduce_fusion.3
  247.4 5.2 %cosine_convert_fusion.4 = (bf16[1,1,80,1280]{3,2,1,0:T(8,128)(2,1)}, bf16[1,1,80,1280]{3,2,1,0:T(8,128)(2,1)}, bf16[1,1,80,1280]{3,2,1,0:T(8,128)(2,1)S(1)}, bf16[1,1,80,1280]{3,2,1,0:T(8,128)(2,1)S(1)}) fusion(f32[4,2,80,1280]{3,2,1,0:T(8,128)} %get-tuple-element.294, s32[]{:T(128)} %get-tuple-element.283, s32[]{:T(128)S(6)} %add.641), kind=kLoop, calls=%fused_computation.16.clone.1 | loop fusion | flops 409600 | bytes 1638408 | tf_op jit(solution)/shard_map/convert.15
  252.6 1.2 cos.47
  253.9 1.1 copy.35
  255.9 2.2 cos.49
  258.1 1.1 copy.37
  259.2 1.0 cos.50
  260.2 2.2 sin.47
  262.4 1.1 copy.34
  264.5 1.2 sin.49
  265.7 1.1 copy.36
  267.0 3.8 fusion.70
  270.9 1.1 multiply_reduce_fusion.3
  272.8 21.9 %all-gather = bf16[16,4,1600]{2,1,0:T(4,128)(2,1)S(1)} all-gather(bf16[1,4,1600]{2,1,0:T(4,128)(2,1)S(1)} %copy.28), channel_id=1, replica_groups=mesh['wide'=16,'narrow'=16] {'wide'}, dimensions={0}, use_global_device_ids=true | all-gather | bytes 217600 | tf_op jit(solution)/shard_map/all_gather | solution.py:122
  294.8 1.1 fusion.57
  297.8 86.3 %all-reduce.6.cloned.1.call-done = f32[64,320]{1,0:T(8,128)} async-done(((f32[64,320]{1,0:T(8,128)}), f32[64,320]{1,0:T(8,128)}) %all-reduce.6.cloned.1.call-update) | async-done | bytes 81936
  384.2 1.3 constant_dynamic-slice_fusion.1
  (78 shorter events, 18.9 us)
Async XLA Ops:
  7.2 287.7 %copy-start = (bf16[1600,320]{0,1:T(8,128)(2,1)S(1)}, bf16[1600,320]{0,1:T(8,128)(2,1)}, u32[]{:S(2)}) copy-start(bf16[1600,320]{0,1:T(8,128)(2,1)} %param.9) | copy-start | bytes 3072004
  7.2 159.3 %all-reduce.4.cloned.1.call-start = ((), (), s32[]{:S(2)}) async-start(), calls=%async_computation | async-start | bytes 3244032 | tf_op jit(solution)/shard_map/psum | solution.py:86
  32.2 1.7 copy-start.2
  32.2 84.0 %copy-start.3 = (s32[2,5,80]{2,0,1:T(2,128)S(1)}, s32[2,5,80]{2,0,1:T(2,128)}, u32[]{:S(2)}) copy-start(s32[2,5,80]{2,0,1:T(2,128)} %param.8) | copy-start | bytes 9604
  33.7 350.5 %all-reduce.6.cloned.1.call-start = ((), (), s32[]{:S(2)}) async-start(), calls=%async_computation.1 | async-start | bytes 196608
  171.7 1.7 copy-start.1
  272.1 23.9 %copy-start.4 = (u32[256]{0:T(256)S(1)}, u32[256]{0:T(256)}, u32[]{:S(2)}) copy-start(u32[256]{0:T(256)} %constant.217) | copy-start | bytes 3076
Sparse Core Ops, SparseCore 0:
  33.8 116.7 all-reduce.3
  296.0 88.0 all-reduce.5

commit v2 on v1

--- a/solution.py
+++ b/solution.py
@@ -65,6 +65,8 @@
 
 
 def body(screens, offsets, valid, recon):
+    wide_count = lax.axis_size("wide")
+    narrow_count = lax.axis_size("narrow")
     wide_index = lax.axis_index("wide")
     narrow_index = lax.axis_index("narrow")
     band_rows = screens.shape[1]
@@ -83,7 +85,9 @@
         group_start = lowest[0, which_layer] + pixel_rows * narrow_index
         row_at = jnp.clip(group_start - wide_index * band_rows + slab_rows, 0, band_rows + slab_rows)
         slabs.append(lax.dynamic_slice_in_dim(padded, row_at, slab_rows, 0))
-    slabs = lax.psum(jnp.stack(slabs), "wide")
+    slabs = jnp.stack(slabs).reshape(wide_count, L * slab_rows // wide_count, union_cols)
+    slabs = jnp.sum(lax.all_to_all(slabs, "wide", 0, 0), axis=0, dtype=slabs.dtype)
+    slabs = lax.all_gather(slabs, "wide", axis=0, tiled=True).reshape(L, slab_rows, union_cols)
     rel = own_offsets - lowest[:, None, :]
     phases = []
     for item in range(local_items):
@@ -123,7 +127,8 @@
         recon,
         preferred_element_type=jnp.float32,
     )
-    commands = lax.psum_scatter(partial_commands, "narrow", scatter_dimension=0, tiled=True)
+    partial_commands = partial_commands.reshape(narrow_count, -1, partial_commands.shape[1])
+    commands = jnp.sum(lax.all_to_all(partial_commands, "narrow", 0, 0), axis=0)
     return (slopes, commands)
 
 

time: 396 us -> 373 us (0.942)
  waiting for transfers between devices: 86.4 us -> 6.04 us
  blocking collectives: 21.9 us -> 69.9 us
  starting transfers between devices: 0.26 us -> 6.79 us
    unnamed x3 -> x1, waiting for transfers between devices: 86.4 us -> 0.02 us
    all_to_all x0 -> x1, blocking collectives: none -> 54.8 us  [body(): lax.all_to_all(slabs, 'wide', 0, 0)]
    all_gather x1, blocking collectives: 21.9 us -> 15 us  [body(): lax.all_gather(slope_vector, 'wide', axis=0, tiled=True)]
    all_to_all x0 -> x1, starting transfers between devices: none -> 6.75 us  [body(): commands = jnp.sum(lax.all_to_all(partial_commands, 'narrow', 0, 0), axis=0)]
    all_to_all x0 -> x1, waiting for transfers between devices: none -> 6.02 us  [body(): commands = jnp.sum(lax.all_to_all(partial_commands, 'narrow', 0, 0), axis=0)]
where the time goes in v2:
time: 373 us; the launch traced here: 369 us
  between operations  144 us (39%)
  local copies, waits for them, and re-layouts  81 us (22%)
  blocking collectives  69.9 us (19%)
  other arithmetic  45.7 us (12%)
  matrix products  15.9 us (4%)
  starting transfers between devices  6.79 us (2%)
  waiting for transfers between devices  6.04 us (2%)
    all_to_all x1, blocking collectives, body(): lax.all_to_all(slabs, 'wide', 0, 0)  54.8 us
    cos x24, local copies, waits for them, and re-layouts, subaperture_fields(): jnp.cos(samples)  30.1 us
    sin x24, local copies, waits for them, and re-layouts, subaperture_fields(): jnp.sin(samples)  27.1 us
    another operation x8, other arithmetic  20.9 us
    dot_general x4, matrix products, centroids(): spectrum = jnp.dot(fields, transform, preferred_element_type=jnp.float32)  15.4 us
    all_gather x1, blocking collectives, body(): lax.all_gather(slope_vector, 'wide', axis=0, tiled=True)  15 us
  transfers between devices with their start and end apart: 2, of which 1 were waited for; matrix products, arithmetic and copies ran while one was open for 4% of the time, Pallas kernels for 0%

profile of v2, /device:TPU:1, one launch (start us, length us, event | category | flops | bytes accessed | tf_op | source)
XLA Modules:
  0.0 369.2 jit_solution(8961222747041907362)
XLA Ops:
  13.8 5.6 %fusion.50 = (bf16[1,256,4096]{2,1,0:T(8,128)(2,1)S(1)}, bf16[1,256,4096]{2,1,0:T(8,128)(2,1)}, bf16[1,256,4096]{2,1,0:T(8,128)(2,1)}, bf16[1,256,4096]{2,1,0:T(8,128)(2,1)}) fusion(bf16[4,256,4096]{2,1,0:T(8,128)(2,1)} %param.6), kind=kLoop, calls=%fused_computation.106 | loop fusion | bytes 16777216 | tf_op jit(solution)/shard_map/slice | solution.py:83
  24.4 2.3 dynamic-slice_bitcast_fusion
  26.7 2.0 dynamic-slice_bitcast_fusion.2
  28.8 3.2 fusion.35
  32.3 1.5 reshape.287
  33.8 54.8 %all_to_all.10 = bf16[16,36,1344]{2,1,0:T(8,128)(2,1)S(1)} all-to-all(bf16[16,36,1344]{2,1,0:T(8,128)(2,1)} %reshape.287), channel_id=1, replica_groups=mesh['wide'=16,'narrow'=16] {'wide'}, dimensions={0} | all-to-all | bytes 3096576 | tf_op jit(solution)/shard_map/all_to_all | solution.py:89
  88.6 1.0 reduce_sum.57
  211.9 4.3 %fusion.48 = bf16[256,1024]{1,0:T(8,128)(2,1)S(1)} fusion(s32[1024]{0:T(1024)S(1)} %get-tuple-element.214, s32[256]{0:T(256)S(1)} %get-tuple-element.215, s32[1024]{0:T(1024)S(1)} %get-tuple-element.213, s32[256]{0:T(256)S(1)} %get-tuple-element.216), kind=kLoop, calls=%fused_computation.104 | loop fusion | flops 5242880 | bytes 534528 | tf_op jit(solution)/shard_map/neg | solution.py:37
  216.2 4.6 %sine_convert_fusion.2 = (bf16[256,1024]{1,0:T(8,128)(2,1)S(1)}, bf16[256,1024]{1,0:T(8,128)(2,1)S(1)}) fusion(s32[1024]{0:T(1024)S(1)} %get-tuple-element.214, s32[256]{0:T(256)S(1)} %get-tuple-element.215, s32[1024]{0:T(1024)S(1)} %get-tuple-element.213, s32[256]{0:T(256)S(1)} %get-tuple-element.216), kind=kLoop, calls=%fused_computation.55 | loop fusion | flops 4718592 | bytes 1058816 | tf_op jit(solution)/shard_map/convert_element_type | solution.py:35
  220.8 1.6 maximum_maximum_fusion
  222.4 2.5 fusion.51
  224.9 1.1 reshape.295
  226.1 1.1 reshape.297
  231.1 1.7 copy-done.1
  232.8 98.5 %while.13 = (s32[]{:T(128)}, f32[4,800,2]{1,2,0:T(2,128)S(1)}, f32[4,2,80,1280]{3,2,1,0:T(8,128)}, bf16[512,2048]{1,0:T(8,128)(2,1)}, f32[800,1]{0,1:T(1,128)S(1)}, /*index=5*/s32[]{:T(128)}, s32[]{:T(128)}, s32[]{}, f32[]{:T(128)}) while((s32[]{:T(128)}, f32[4,800,2]{1,2,0:T(2,128)S(1)}, f32[4,2,80,1280]{3,2,1,0:T(8,128)}, ...), condition=%wide.region_6.7_spmd, body=%wide.region_2.6_spmd.sunk | while | flops 1687980416 | bytes 22656888 | solution.py:117
  232.8 5.2 %cosine_convert_fusion.4 = (bf16[1,1,80,1280]{3,2,1,0:T(8,128)(2,1)}, bf16[1,1,80,1280]{3,2,1,0:T(8,128)(2,1)}, bf16[1,1,80,1280]{3,2,1,0:T(8,128)(2,1)S(1)}, bf16[1,1,80,1280]{3,2,1,0:T(8,128)(2,1)S(1)}) fusion(f32[4,2,80,1280]{3,2,1,0:T(8,128)} %get-tuple-element.294, s32[]{:T(128)} %get-tuple-element.283, s32[]{:T(128)S(6)} %add.620), kind=kLoop, calls=%fused_computation.16.clone.1 | loop fusion | flops 409600 | bytes 1638408 | tf_op jit(solution)/shard_map/convert.15
  238.0 1.2 cos.47
  239.2 1.1 copy.35
  240.3 1.0 cos.48
  241.3 2.2 cos.49
  243.5 1.1 copy.37
  245.5 2.2 sin.47
  247.8 1.1 copy.34
  249.8 1.2 sin.49
  251.0 1.1 copy.36
  252.4 3.9 %fusion.70 = f32[800,2048]{1,0:T(8,128)S(1)} fusion(bf16[512,2048]{1,0:T(8,128)(2,1)} %get-tuple-element.295, bf16[400,256]{0,1:T(8,128)(2,1)} %sin.48, bf16[400,256]{0,1:T(8,128)(2,1)} %cos.48, bf16[400,256]{0,1:T(8,128)(2,1)S(1)} %sin.50, bf16[400,256]{0,1:T(8,128)(2,1)} %cos.50), kind=kOutput, calls=%fused_computation.5.clone.1 | convolution fusion | flops 1680998400 | bytes 9469952 | tf_op jit(solution)/shard_map/while/body/eval_jaxpr/dot_general | solution.py:53
  256.3 1.1 multiply_reduce_fusion.3
  257.4 5.2 %cosine_convert_fusion.4 = (bf16[1,1,80,1280]{3,2,1,0:T(8,128)(2,1)}, bf16[1,1,80,1280]{3,2,1,0:T(8,128)(2,1)}, bf16[1,1,80,1280]{3,2,1,0:T(8,128)(2,1)S(1)}, bf16[1,1,80,1280]{3,2,1,0:T(8,128)(2,1)S(1)}) fusion(f32[4,2,80,1280]{3,2,1,0:T(8,128)} %get-tuple-element.294, s32[]{:T(128)} %get-tuple-element.283, s32[]{:T(128)S(6)} %add.620), kind=kLoop, calls=%fused_computation.16.clone.1 | loop fusion | flops 409600 | bytes 1638408 | tf_op jit(solution)/shard_map/convert.15
  262.6 1.2 cos.47
  263.9 1.1 copy.35
  264.9 1.0 cos.48
  265.9 2.2 cos.49
  268.2 1.1 copy.37
  270.2 2.2 sin.47
  272.4 1.1 copy.34
  274.5 1.2 sin.49
  275.7 1.1 copy.36
  277.0 3.9 %fusion.70 = f32[800,2048]{1,0:T(8,128)S(1)} fusion(bf16[512,2048]{1,0:T(8,128)(2,1)} %get-tuple-element.295, bf16[400,256]{0,1:T(8,128)(2,1)} %sin.48, bf16[400,256]{0,1:T(8,128)(2,1)} %cos.48, bf16[400,256]{0,1:T(8,128)(2,1)S(1)} %sin.50, bf16[400,256]{0,1:T(8,128)(2,1)} %cos.50), kind=kOutput, calls=%fused_computation.5.clone.1 | convolution fusion | flops 1680998400 | bytes 9469952 | tf_op jit(solution)/shard_map/while/body/eval_jaxpr/dot_general | solution.py:53
  280.9 1.1 multiply_reduce_fusion.3
  282.1 5.2 %cosine_convert_fusion.4 = (bf16[1,1,80,1280]{3,2,1,0:T(8,128)(2,1)}, bf16[1,1,80,1280]{3,2,1,0:T(8,128)(2,1)}, bf16[1,1,80,1280]{3,2,1,0:T(8,128)(2,1)S(1)}, bf16[1,1,80,1280]{3,2,1,0:T(8,128)(2,1)S(1)}) fusion(f32[4,2,80,1280]{3,2,1,0:T(8,128)} %get-tuple-element.294, s32[]{:T(128)} %get-tuple-element.283, s32[]{:T(128)S(6)} %add.620), kind=kLoop, calls=%fused_computation.16.clone.1 | loop fusion | flops 409600 | bytes 1638408 | tf_op jit(solution)/shard_map/convert.15
  287.3 1.2 cos.47
  288.5 1.1 copy.35
  290.6 2.2 cos.49
  292.8 1.1 copy.37
  294.8 2.2 sin.47
  297.1 1.1 copy.34
  299.1 1.2 sin.49
  300.3 1.1 copy.36
  301.7 3.8 %fusion.70 = f32[800,2048]{1,0:T(8,128)S(1)} fusion(bf16[512,2048]{1,0:T(8,128)(2,1)} %get-tuple-element.295, bf16[400,256]{0,1:T(8,128)(2,1)} %sin.48, bf16[400,256]{0,1:T(8,128)(2,1)} %cos.48, bf16[400,256]{0,1:T(8,128)(2,1)S(1)} %sin.50, bf16[400,256]{0,1:T(8,128)(2,1)} %cos.50), kind=kOutput, calls=%fused_computation.5.clone.1 | convolution fusion | flops 1680998400 | bytes 9469952 | tf_op jit(solution)/shard_map/while/body/eval_jaxpr/dot_general | solution.py:53
  305.5 1.1 multiply_reduce_fusion.3
  306.7 5.2 %cosine_convert_fusion.4 = (bf16[1,1,80,1280]{3,2,1,0:T(8,128)(2,1)}, bf16[1,1,80,1280]{3,2,1,0:T(8,128)(2,1)}, bf16[1,1,80,1280]{3,2,1,0:T(8,128)(2,1)S(1)}, bf16[1,1,80,1280]{3,2,1,0:T(8,128)(2,1)S(1)}) fusion(f32[4,2,80,1280]{3,2,1,0:T(8,128)} %get-tuple-element.294, s32[]{:T(128)} %get-tuple-element.283, s32[]{:T(128)S(6)} %add.620), kind=kLoop, calls=%fused_computation.16.clone.1 | loop fusion | flops 409600 | bytes 1638408 | tf_op jit(solution)/shard_map/convert.15
  311.9 1.2 cos.47
  313.1 1.1 copy.35
  315.2 2.2 cos.49
  317.4 1.1 copy.37
  319.5 2.2 sin.47
  321.7 1.1 copy.34
  323.7 1.2 sin.49
  325.0 1.1 copy.36
  326.3 3.9 %fusion.70 = f32[800,2048]{1,0:T(8,128)S(1)} fusion(bf16[512,2048]{1,0:T(8,128)(2,1)} %get-tuple-element.295, bf16[400,256]{0,1:T(8,128)(2,1)} %sin.48, bf16[400,256]{0,1:T(8,128)(2,1)} %cos.48, bf16[400,256]{0,1:T(8,128)(2,1)S(1)} %sin.50, bf16[400,256]{0,1:T(8,128)(2,1)} %cos.50), kind=kOutput, calls=%fused_computation.5.clone.1 | convolution fusion | flops 1680998400 | bytes 9469952 | tf_op jit(solution)/shard_map/while/body/eval_jaxpr/dot_general | solution.py:53
  330.2 1.1 multiply_reduce_fusion.3
  332.1 15.0 %all-gather.1 = bf16[16,4,1600]{2,1,0:T(4,128)(2,1)S(1)} all-gather(bf16[1,4,1600]{2,1,0:T(4,128)(2,1)S(1)} %copy.28), channel_id=1, replica_groups=mesh['wide'=16,'narrow'=16] {'wide'}, dimensions={0}, use_global_device_ids=true | all-gather | bytes 217600 | tf_op jit(solution)/shard_map/all_gather | solution.py:126
  348.3 6.8 %all-to-all-start.1 = ((f32[16,4,320]{2,1,0:T(4,128)}), f32[16,4,320]{2,1,0:T(4,128)S(1)}, u32[]{:S(2)}, u32[]{:S(2)}) async-start(f32[16,4,320]{2,1,0:T(4,128)} %reshape.290), calls=%async_computation.1 | async-start | bytes 196608 | tf_op jit(solution)/shard_map/all_to_all | solution.py:131
  355.7 6.0 %all-to-all-done.1 = f32[16,4,320]{2,1,0:T(4,128)S(1)} async-done(((f32[16,4,320]{2,1,0:T(4,128)}), f32[16,4,320]{2,1,0:T(4,128)S(1)}, u32[]{:S(2)}, u32[]{:S(2)}) %all-to-all-start.1) | async-done | bytes 81952 | tf_op jit(solution)/shard_map/all_to_all | solution.py:131
  (82 shorter events, 23.1 us)
Async XLA Ops:
  7.2 340.1 %copy-start = (bf16[1600,320]{0,1:T(8,128)(2,1)S(1)}, bf16[1600,320]{0,1:T(8,128)(2,1)}, u32[]{:S(2)}) copy-start(bf16[1600,320]{0,1:T(8,128)(2,1)} %param.9) | copy-start | bytes 3072004
  7.2 215.2 %all-gather.4.cloned.1.call-start = ((), (), s32[]{:S(2)}) async-start(), calls=%async_computation.2 | async-start | bytes 1914880 | tf_op jit(solution)/shard_map/all_gather | solution.py:90
  33.8 55.9 %copy-start.2 = (s32[2,128,4]{1,2,0:T(4,128)S(1)}, s32[2,128,4]{1,2,0:T(4,128)}, u32[]{:S(2)}) copy-start(s32[2,128,4]{1,2,0:T(4,128)} %param.7) | copy-start | bytes 12292
  88.6 83.4 %copy-start.3 = (s32[2,5,80]{2,0,1:T(2,128)S(1)}, s32[2,5,80]{2,0,1:T(2,128)}, u32[]{:S(2)}) copy-start(s32[2,5,80]{2,0,1:T(2,128)} %param.8) | copy-start | bytes 9604
  231.1 1.7 copy-start.1
  348.3 13.4 %all-to-all-start.1 = ((f32[16,4,320]{2,1,0:T(4,128)}), f32[16,4,320]{2,1,0:T(4,128)S(1)}, u32[]{:S(2)}, u32[]{:S(2)}) async-start(f32[16,4,320]{2,1,0:T(4,128)} %reshape.290), calls=%async_computation.1 | async-start | bytes 196608 | tf_op jit(solution)/shard_map/all_to_all | solution.py:131
Sparse Core Ops, SparseCore 0:
  89.7 36.6 all-gather.3

commit v3 on v2

--- a/solution.py
+++ b/solution.py
@@ -87,7 +87,8 @@
         slabs.append(lax.dynamic_slice_in_dim(padded, row_at, slab_rows, 0))
     slabs = jnp.stack(slabs).reshape(wide_count, L * slab_rows // wide_count, union_cols)
     slabs = jnp.sum(lax.all_to_all(slabs, "wide", 0, 0), axis=0, dtype=slabs.dtype)
-    slabs = lax.all_gather(slabs, "wide", axis=0, tiled=True).reshape(L, slab_rows, union_cols)
+    slabs = jnp.broadcast_to(slabs[None], (wide_count,) + slabs.shape)
+    slabs = lax.all_to_all(slabs, "wide", 0, 0).reshape(L, slab_rows, union_cols)
     rel = own_offsets - lowest[:, None, :]
     phases = []
     for item in range(local_items):

time: 373 us -> 366 us (0.981)
  between operations: 144 us -> 131 us
  starting transfers between devices: 6.79 us -> 10.7 us
    all_to_all x0 -> x1, starting transfers between devices: none -> 3.92 us  [body(): lax.all_to_all(slabs, 'wide', 0, 0).reshape(L, slab_rows, union_cols)]
    slice x5 -> x1, local copies, waits for them, and re-layouts: 4.99 us -> 1.11 us  [body(): slabs[which_layer]]
where the time goes in v3:
time: 366 us; the launch traced here: 362 us
  between operations  131 us (36%)
  local copies, waits for them, and re-layouts  82 us (22%)
  blocking collectives  71.7 us (20%)
  other arithmetic  45 us (12%)
  matrix products  15.8 us (4%)
  starting transfers between devices  10.7 us (3%)
  waiting for transfers between devices  6.03 us (2%)
    all_to_all x1, blocking collectives, body(): lax.all_to_all(slabs, 'wide', 0, 0)  54.7 us
    cos x24, local copies, waits for them, and re-layouts, subaperture_fields(): jnp.cos(samples)  30 us
    sin x24, local copies, waits for them, and re-layouts, subaperture_fields(): jnp.sin(samples)  27.2 us
    another operation x8, other arithmetic  20.9 us
    all_gather x1, blocking collectives, body(): lax.all_gather(slope_vector, 'wide', axis=0, tiled=True)  17 us
    dot_general x4, matrix products, centroids(): spectrum = jnp.dot(fields, transform, preferred_element_type=jnp.float32)  15.4 us
  transfers between devices with their start and end apart: 2, of which 1 were waited for; matrix products, arithmetic and copies ran while one was open for 4% of the time, Pallas kernels for 0%

profile of v3, /device:TPU:1, one launch (start us, length us, event | category | flops | bytes accessed | tf_op | source)
XLA Modules:
  0.0 362.2 jit_solution(14334888834747050914)
XLA Ops:
  7.1 5.6 %fusion.50 = (bf16[1,256,4096]{2,1,0:T(8,128)(2,1)S(1)}, bf16[1,256,4096]{2,1,0:T(8,128)(2,1)}, bf16[1,256,4096]{2,1,0:T(8,128)(2,1)}, bf16[1,256,4096]{2,1,0:T(8,128)(2,1)}) fusion(bf16[4,256,4096]{2,1,0:T(8,128)(2,1)} %param.6), kind=kLoop, calls=%fused_computation.106 | loop fusion | bytes 16777216 | tf_op jit(solution)/shard_map/slice | solution.py:83
  17.7 2.3 dynamic-slice_bitcast_fusion
  20.0 2.0 dynamic-slice_bitcast_fusion.2
  22.1 3.2 fusion.35
  25.6 1.5 reshape.273
  27.1 54.7 %all_to_all.15 = bf16[16,36,1344]{2,1,0:T(8,128)(2,1)S(1)} all-to-all(bf16[16,36,1344]{2,1,0:T(8,128)(2,1)} %reshape.273), channel_id=1, replica_groups=mesh['wide'=16,'narrow'=16] {'wide'}, dimensions={0} | all-to-all | bytes 3096576 | tf_op jit(solution)/shard_map/all_to_all | solution.py:89
  82.1 1.4 broadcast_in_dim.9
  83.4 3.9 %all-to-all-start.1 = ((bf16[16,36,1344]{2,1,0:T(8,128)(2,1)}), bf16[16,36,1344]{2,1,0:T(8,128)(2,1)S(1)}, u32[]{:S(2)}, u32[]{:S(2)}) async-start(bf16[16,36,1344]{2,1,0:T(8,128)(2,1)} %broadcast_in_dim.9), calls=%async_computation.1 | async-start | bytes 3604480 | tf_op jit(solution)/shard_map/all_to_all | solution.py:91
  210.2 4.3 %fusion.48 = bf16[256,1024]{1,0:T(8,128)(2,1)S(1)} fusion(s32[1024]{0:T(1024)S(1)} %get-tuple-element.214, s32[256]{0:T(256)S(1)} %get-tuple-element.215, s32[1024]{0:T(1024)S(1)} %get-tuple-element.213, s32[256]{0:T(256)S(1)} %get-tuple-element.216), kind=kLoop, calls=%fused_computation.104 | loop fusion | flops 5242880 | bytes 534528 | tf_op jit(solution)/shard_map/neg | solution.py:37
  214.5 4.6 %sine_convert_fusion.2 = (bf16[256,1024]{1,0:T(8,128)(2,1)S(1)}, bf16[256,1024]{1,0:T(8,128)(2,1)S(1)}) fusion(s32[1024]{0:T(1024)S(1)} %get-tuple-element.214, s32[256]{0:T(256)S(1)} %get-tuple-element.215, s32[1024]{0:T(1024)S(1)} %get-tuple-element.213, s32[256]{0:T(256)S(1)} %get-tuple-element.216), kind=kLoop, calls=%fused_computation.55 | loop fusion | flops 4718592 | bytes 1058816 | tf_op jit(solution)/shard_map/convert_element_type | solution.py:35
  219.1 1.6 maximum_maximum_fusion
  220.7 1.1 fusion.51
  221.8 1.1 squeeze.280
  222.9 1.1 squeeze.283
  224.0 1.1 squeeze.286
  229.1 1.7 copy-done.1
  230.7 98.5 %while.13 = (s32[]{:T(128)}, f32[4,800,2]{1,2,0:T(2,128)S(1)}, f32[4,2,80,1280]{3,2,1,0:T(8,128)}, bf16[512,2048]{1,0:T(8,128)(2,1)}, f32[800,1]{0,1:T(1,128)S(1)}, /*index=5*/s32[]{:T(128)}, s32[]{:T(128)}, s32[]{}, f32[]{:T(128)}) while((s32[]{:T(128)}, f32[4,800,2]{1,2,0:T(2,128)S(1)}, f32[4,2,80,1280]{3,2,1,0:T(8,128)}, ...), condition=%wide.region_6.7_spmd, body=%wide.region_2.6_spmd.sunk | while | flops 1687980416 | bytes 22656888 | solution.py:118
  230.7 5.2 %cosine_convert_fusion.4 = (bf16[1,1,80,1280]{3,2,1,0:T(8,128)(2,1)}, bf16[1,1,80,1280]{3,2,1,0:T(8,128)(2,1)}, bf16[1,1,80,1280]{3,2,1,0:T(8,128)(2,1)S(1)}, bf16[1,1,80,1280]{3,2,1,0:T(8,128)(2,1)S(1)}) fusion(f32[4,2,80,1280]{3,2,1,0:T(8,128)} %get-tuple-element.294, s32[]{:T(128)} %get-tuple-element.283, s32[]{:T(128)S(6)} %add.611), kind=kLoop, calls=%fused_computation.16.clone.1 | loop fusion | flops 409600 | bytes 1638408 | tf_op jit(solution)/shard_map/convert.15
  235.9 1.2 cos.47
  237.2 1.1 copy.35
  239.2 2.2 cos.49
  241.4 1.1 copy.37
  243.5 2.2 sin.47
  245.7 1.1 copy.34
  247.7 1.2 sin.49
  248.9 1.1 copy.36
  250.3 3.9 %fusion.70 = f32[800,2048]{1,0:T(8,128)S(1)} fusion(bf16[512,2048]{1,0:T(8,128)(2,1)} %get-tuple-element.295, bf16[400,256]{0,1:T(8,128)(2,1)} %sin.48, bf16[400,256]{0,1:T(8,128)(2,1)} %cos.48, bf16[400,256]{0,1:T(8,128)(2,1)S(1)} %sin.50, bf16[400,256]{0,1:T(8,128)(2,1)} %cos.50), kind=kOutput, calls=%fused_computation.5.clone.1 | convolution fusion | flops 1680998400 | bytes 9469952 | tf_op jit(solution)/shard_map/while/body/eval_jaxpr/dot_general | solution.py:53
  254.2 1.1 multiply_reduce_fusion.3
  255.3 5.2 %cosine_convert_fusion.4 = (bf16[1,1,80,1280]{3,2,1,0:T(8,128)(2,1)}, bf16[1,1,80,1280]{3,2,1,0:T(8,128)(2,1)}, bf16[1,1,80,1280]{3,2,1,0:T(8,128)(2,1)S(1)}, bf16[1,1,80,1280]{3,2,1,0:T(8,128)(2,1)S(1)}) fusion(f32[4,2,80,1280]{3,2,1,0:T(8,128)} %get-tuple-element.294, s32[]{:T(128)} %get-tuple-element.283, s32[]{:T(128)S(6)} %add.611), kind=kLoop, calls=%fused_computation.16.clone.1 | loop fusion | flops 409600 | bytes 1638408 | tf_op jit(solution)/shard_map/convert.15
  260.5 1.2 cos.47
  261.8 1.1 copy.35
  263.8 2.2 cos.49
  266.0 1.1 copy.37
  268.1 2.2 sin.47
  270.3 1.1 copy.34
  272.3 1.2 sin.49
  273.6 1.1 copy.36
  274.9 3.8 %fusion.70 = f32[800,2048]{1,0:T(8,128)S(1)} fusion(bf16[512,2048]{1,0:T(8,128)(2,1)} %get-tuple-element.295, bf16[400,256]{0,1:T(8,128)(2,1)} %sin.48, bf16[400,256]{0,1:T(8,128)(2,1)} %cos.48, bf16[400,256]{0,1:T(8,128)(2,1)S(1)} %sin.50, bf16[400,256]{0,1:T(8,128)(2,1)} %cos.50), kind=kOutput, calls=%fused_computation.5.clone.1 | convolution fusion | flops 1680998400 | bytes 9469952 | tf_op jit(solution)/shard_map/while/body/eval_jaxpr/dot_general | solution.py:53
  278.8 1.1 multiply_reduce_fusion.3
  280.0 5.2 %cosine_convert_fusion.4 = (bf16[1,1,80,1280]{3,2,1,0:T(8,128)(2,1)}, bf16[1,1,80,1280]{3,2,1,0:T(8,128)(2,1)}, bf16[1,1,80,1280]{3,2,1,0:T(8,128)(2,1)S(1)}, bf16[1,1,80,1280]{3,2,1,0:T(8,128)(2,1)S(1)}) fusion(f32[4,2,80,1280]{3,2,1,0:T(8,128)} %get-tuple-element.294, s32[]{:T(128)} %get-tuple-element.283, s32[]{:T(128)S(6)} %add.611), kind=kLoop, calls=%fused_computation.16.clone.1 | loop fusion | flops 409600 | bytes 1638408 | tf_op jit(solution)/shard_map/convert.15
  285.2 1.2 cos.47
  286.4 1.1 copy.35
  288.4 2.2 cos.49
  290.7 1.1 copy.37
  292.7 2.2 sin.47
  294.9 1.1 copy.34
  297.0 1.2 sin.49
  298.2 1.1 copy.36
  299.5 3.9 %fusion.70 = f32[800,2048]{1,0:T(8,128)S(1)} fusion(bf16[512,2048]{1,0:T(8,128)(2,1)} %get-tuple-element.295, bf16[400,256]{0,1:T(8,128)(2,1)} %sin.48, bf16[400,256]{0,1:T(8,128)(2,1)} %cos.48, bf16[400,256]{0,1:T(8,128)(2,1)S(1)} %sin.50, bf16[400,256]{0,1:T(8,128)(2,1)} %cos.50), kind=kOutput, calls=%fused_computation.5.clone.1 | convolution fusion | flops 1680998400 | bytes 9469952 | tf_op jit(solution)/shard_map/while/body/eval_jaxpr/dot_general | solution.py:53
  303.4 1.1 multiply_reduce_fusion.3
  304.6 5.2 %cosine_convert_fusion.4 = (bf16[1,1,80,1280]{3,2,1,0:T(8,128)(2,1)}, bf16[1,1,80,1280]{3,2,1,0:T(8,128)(2,1)}, bf16[1,1,80,1280]{3,2,1,0:T(8,128)(2,1)S(1)}, bf16[1,1,80,1280]{3,2,1,0:T(8,128)(2,1)S(1)}) fusion(f32[4,2,80,1280]{3,2,1,0:T(8,128)} %get-tuple-element.294, s32[]{:T(128)} %get-tuple-element.283, s32[]{:T(128)S(6)} %add.611), kind=kLoop, calls=%fused_computation.16.clone.1 | loop fusion | flops 409600 | bytes 1638408 | tf_op jit(solution)/shard_map/convert.15
  309.8 1.2 cos.47
  311.0 1.1 copy.35
  313.1 2.2 cos.49
  315.3 1.1 copy.37
  317.3 2.2 sin.47
  319.5 1.1 copy.34
  321.6 1.2 sin.49
  322.8 1.1 copy.36
  324.2 3.9 %fusion.70 = f32[800,2048]{1,0:T(8,128)S(1)} fusion(bf16[512,2048]{1,0:T(8,128)(2,1)} %get-tuple-element.295, bf16[400,256]{0,1:T(8,128)(2,1)} %sin.48, bf16[400,256]{0,1:T(8,128)(2,1)} %cos.48, bf16[400,256]{0,1:T(8,128)(2,1)S(1)} %sin.50, bf16[400,256]{0,1:T(8,128)(2,1)} %cos.50), kind=kOutput, calls=%fused_computation.5.clone.1 | convolution fusion | flops 1680998400 | bytes 9469952 | tf_op jit(solution)/shard_map/while/body/eval_jaxpr/dot_general | solution.py:53
  328.0 1.1 multiply_reduce_fusion.3
  329.9 17.0 %all-gather = bf16[16,4,1600]{2,1,0:T(4,128)(2,1)S(1)} all-gather(bf16[1,4,1600]{2,1,0:T(4,128)(2,1)S(1)} %copy.28), channel_id=1, replica_groups=mesh['wide'=16,'narrow'=16] {'wide'}, dimensions={0}, use_global_device_ids=true | all-gather | bytes 217600 | tf_op jit(solution)/shard_map/all_gather | solution.py:127
  348.2 6.7 %all-to-all-start.2 = ((f32[16,4,320]{2,1,0:T(4,128)}), f32[16,4,320]{2,1,0:T(4,128)S(1)}, u32[]{:S(2)}, u32[]{:S(2)}) async-start(f32[16,4,320]{2,1,0:T(4,128)} %reshape.276), calls=%async_computation.2 | async-start | bytes 196608 | tf_op jit(solution)/shard_map/all_to_all | solution.py:132
  355.6 6.0 %all-to-all-done.2 = f32[16,4,320]{2,1,0:T(4,128)S(1)} async-done(((f32[16,4,320]{2,1,0:T(4,128)}), f32[16,4,320]{2,1,0:T(4,128)S(1)}, u32[]{:S(2)}, u32[]{:S(2)}) %all-to-all-start.2) | async-done | bytes 81952 | tf_op jit(solution)/shard_map/all_to_all | solution.py:132
  (82 shorter events, 25.2 us)
Async XLA Ops:
  0.6 346.4 %copy-start = (bf16[1600,320]{0,1:T(8,128)(2,1)S(1)}, bf16[1600,320]{0,1:T(8,128)(2,1)}, u32[]{:S(2)}) copy-start(bf16[1600,320]{0,1:T(8,128)(2,1)} %param.9) | copy-start | bytes 3072004
  83.4 3.9 %copy-start.2 = (s32[2,128,4]{1,2,0:T(4,128)S(1)}, s32[2,128,4]{1,2,0:T(4,128)}, u32[]{:S(2)}) copy-start(s32[2,128,4]{1,2,0:T(4,128)} %param.7) | copy-start | bytes 12292
  83.4 86.7 %copy-start.3 = (s32[2,5,80]{2,0,1:T(2,128)S(1)}, s32[2,5,80]{2,0,1:T(2,128)}, u32[]{:S(2)}) copy-start(s32[2,5,80]{2,0,1:T(2,128)} %param.8) | copy-start | bytes 9604
  83.4 137.2 %all-to-all-start.1 = ((bf16[16,36,1344]{2,1,0:T(8,128)(2,1)}), bf16[16,36,1344]{2,1,0:T(8,128)(2,1)S(1)}, u32[]{:S(2)}, u32[]{:S(2)}) async-start(bf16[16,36,1344]{2,1,0:T(8,128)(2,1)} %broadcast_in_dim.9), calls=%async_computation.1 | async-start | bytes 3604480 | tf_op jit(solution)/shard_map/all_to_all | solution.py:91
  229.1 1.7 copy-start.1
  348.2 13.4 %all-to-all-start.2 = ((f32[16,4,320]{2,1,0:T(4,128)}), f32[16,4,320]{2,1,0:T(4,128)S(1)}, u32[]{:S(2)}, u32[]{:S(2)}) async-start(f32[16,4,320]{2,1,0:T(4,128)} %reshape.276), calls=%async_computation.2 | async-start | bytes 196608 | tf_op jit(solution)/shard_map/all_to_all | solution.py:132

commit v4 on v1

--- a/solution.py
+++ b/solution.py
@@ -65,6 +65,7 @@
 
 
 def body(screens, offsets, valid, recon):
+    narrow_count = lax.axis_size("narrow")
     wide_index = lax.axis_index("wide")
     narrow_index = lax.axis_index("narrow")
     band_rows = screens.shape[1]
@@ -123,7 +124,8 @@
         recon,
         preferred_element_type=jnp.float32,
     )
-    commands = lax.psum_scatter(partial_commands, "narrow", scatter_dimension=0, tiled=True)
+    partial_commands = partial_commands.reshape(narrow_count, -1, partial_commands.shape[1])
+    commands = jnp.sum(lax.all_to_all(partial_commands, "narrow", 0, 0), axis=0)
     return (slopes, commands)
 
 

time: 396 us -> 320 us (0.81)
  waiting for transfers between devices: 86.4 us -> 6.04 us
  starting transfers between devices: 0.26 us -> 6.81 us
    unnamed x3 -> x1, waiting for transfers between devices: 86.4 us -> 0.02 us
    all_to_all x0 -> x1, starting transfers between devices: none -> 6.77 us  [body(): commands = jnp.sum(lax.all_to_all(partial_commands, 'narrow', 0, 0), axis=0)]
    all_to_all x0 -> x1, waiting for transfers between devices: none -> 6.02 us  [body(): commands = jnp.sum(lax.all_to_all(partial_commands, 'narrow', 0, 0), axis=0)]
  transfers between devices with their start and end apart: 2 -> 2, of which waited for: 1 -> 1; matrix products, arithmetic and copies ran while one was open for 4% -> 5% of each run, Pallas kernels for 0% -> 0%
where the time goes in v4:
time: 320 us; the launch traced here: 316 us
  between operations  143 us (45%)
  local copies, waits for them, and re-layouts  76 us (24%)
  other arithmetic  46 us (14%)
  blocking collectives  21.9 us (7%)
  matrix products  15.8 us (5%)
  starting transfers between devices  6.81 us (2%)
  waiting for transfers between devices  6.04 us (2%)
    cos x24, local copies, waits for them, and re-layouts, subaperture_fields(): jnp.cos(samples)  30.1 us
    sin x24, local copies, waits for them, and re-layouts, subaperture_fields(): jnp.sin(samples)  27.1 us
    all_gather x1, blocking collectives, body(): lax.all_gather(slope_vector, 'wide', axis=0, tiled=True)  21.9 us
    another operation x8, other arithmetic  20.9 us
    dot_general x4, matrix products, centroids(): spectrum = jnp.dot(fields, transform, preferred_element_type=jnp.float32)  15.4 us
    all_to_all x1, starting transfers between devices, body(): commands = jnp.sum(lax.all_to_all(partial_commands, 'narrow', 0, 0), axis=0)  6.77 us
  transfers between devices with their start and end apart: 2, of which 1 were waited for; matrix products, arithmetic and copies ran while one was open for 5% of the time, Pallas kernels for 0%

profile of v4, /device:TPU:1, one launch (start us, length us, event | category | flops | bytes accessed | tf_op | source)
XLA Modules:
  0.0 316.4 jit_solution(13882446086356264635)
XLA Ops:
  13.8 5.6 %fusion.50 = (bf16[1,256,4096]{2,1,0:T(8,128)(2,1)S(1)}, bf16[1,256,4096]{2,1,0:T(8,128)(2,1)}, bf16[1,256,4096]{2,1,0:T(8,128)(2,1)}, bf16[1,256,4096]{2,1,0:T(8,128)(2,1)}) fusion(bf16[4,256,4096]{2,1,0:T(8,128)(2,1)} %param.6), kind=kLoop, calls=%fused_computation.106 | loop fusion | bytes 16777216 | tf_op jit(solution)/shard_map/slice | solution.py:82
  24.4 2.3 dynamic-slice_bitcast_fusion
  26.7 2.0 dynamic-slice_bitcast_fusion.2
  28.8 3.2 %fusion.35 = (bf16[1,144,1344]{2,1,0:T(8,128)(2,1)S(1)}, bf16[1,144,1344]{2,1,0:T(8,128)(2,1)S(1)}, bf16[1,144,1344]{2,1,0:T(8,128)(2,1)S(1)}, bf16[1,144,1344]{2,1,0:T(8,128)(2,1)S(1)}) fusion(s32[]{:T(128)S(6)} %min.13, bf16[144,1344]{1,0:T(8,128)(2,1)S(1)} %broadcast_in_dim.6, bf16[256,1344]{1,0:T(8,128)(2,1)S(1)} %get-tuple-element.220, s32[]{:T(128)S(6)} %min.15, ...), kind=kLoop, calls=%fused_computation.80 | loop fusion | flops 4644864 | bytes 4687888 | tf_op jit(solution)/shard_map/stack | solution.py:87
  32.0 1.4 pad_maximum_fusion
  155.5 4.3 %fusion.48 = bf16[256,1024]{1,0:T(8,128)(2,1)S(1)} fusion(s32[1024]{0:T(1024)S(1)} %get-tuple-element.214, s32[256]{0:T(256)S(1)} %get-tuple-element.215, s32[1024]{0:T(1024)S(1)} %get-tuple-element.213, s32[256]{0:T(256)S(1)} %get-tuple-element.216), kind=kLoop, calls=%fused_computation.104 | loop fusion | flops 5242880 | bytes 534528 | tf_op jit(solution)/shard_map/neg | solution.py:37
  159.9 4.8 %sine_convert_fusion.2 = (bf16[256,1024]{1,0:T(8,128)(2,1)S(1)}, bf16[256,1024]{1,0:T(8,128)(2,1)S(1)}) fusion(s32[1024]{0:T(1024)S(1)} %get-tuple-element.214, s32[256]{0:T(256)S(1)} %get-tuple-element.215, s32[1024]{0:T(1024)S(1)} %get-tuple-element.213, s32[256]{0:T(256)S(1)} %get-tuple-element.216), kind=kLoop, calls=%fused_computation.55 | loop fusion | flops 4718592 | bytes 1058816 | tf_op jit(solution)/shard_map/convert_element_type | solution.py:35
  164.6 1.6 maximum_maximum_fusion
  166.2 1.5 fusion.51
  171.4 1.7 copy-done.1
  173.1 98.5 %while.13 = (s32[]{:T(128)}, f32[4,800,2]{1,2,0:T(2,128)S(1)}, f32[4,2,80,1280]{3,2,1,0:T(8,128)}, bf16[512,2048]{1,0:T(8,128)(2,1)}, f32[800,1]{0,1:T(1,128)S(1)}, /*index=5*/s32[]{:T(128)}, s32[]{:T(128)}, s32[]{}, f32[]{:T(128)}) while((s32[]{:T(128)}, f32[4,800,2]{1,2,0:T(2,128)S(1)}, f32[4,2,80,1280]{3,2,1,0:T(8,128)}, ...), condition=%wide.region_6.7_spmd, body=%wide.region_2.6_spmd.sunk | while | flops 1687980416 | bytes 22656888 | solution.py:114
  173.1 5.2 %cosine_convert_fusion.4 = (bf16[1,1,80,1280]{3,2,1,0:T(8,128)(2,1)}, bf16[1,1,80,1280]{3,2,1,0:T(8,128)(2,1)}, bf16[1,1,80,1280]{3,2,1,0:T(8,128)(2,1)S(1)}, bf16[1,1,80,1280]{3,2,1,0:T(8,128)(2,1)S(1)}) fusion(f32[4,2,80,1280]{3,2,1,0:T(8,128)} %get-tuple-element.294, s32[]{:T(128)} %get-tuple-element.283, s32[]{:T(128)S(6)} %add.637), kind=kLoop, calls=%fused_computation.16.clone.1 | loop fusion | flops 409600 | bytes 1638408 | tf_op jit(solution)/shard_map/convert.15
  178.3 1.2 cos.47
  179.5 1.1 copy.35
  180.6 1.0 cos.48
  181.6 2.2 cos.49
  183.8 1.1 copy.37
  184.9 1.0 cos.50
  185.8 2.2 sin.47
  188.1 1.1 copy.34
  190.1 1.2 sin.49
  191.3 1.1 copy.36
  192.7 3.9 %fusion.70 = f32[800,2048]{1,0:T(8,128)S(1)} fusion(bf16[512,2048]{1,0:T(8,128)(2,1)} %get-tuple-element.295, bf16[400,256]{0,1:T(8,128)(2,1)} %sin.48, bf16[400,256]{0,1:T(8,128)(2,1)} %cos.48, bf16[400,256]{0,1:T(8,128)(2,1)S(1)} %sin.50, bf16[400,256]{0,1:T(8,128)(2,1)} %cos.50), kind=kOutput, calls=%fused_computation.5.clone.1 | convolution fusion | flops 1680998400 | bytes 9469952 | tf_op jit(solution)/shard_map/while/body/eval_jaxpr/dot_general | solution.py:53
  196.5 1.1 multiply_reduce_fusion.3
  197.7 5.2 %cosine_convert_fusion.4 = (bf16[1,1,80,1280]{3,2,1,0:T(8,128)(2,1)}, bf16[1,1,80,1280]{3,2,1,0:T(8,128)(2,1)}, bf16[1,1,80,1280]{3,2,1,0:T(8,128)(2,1)S(1)}, bf16[1,1,80,1280]{3,2,1,0:T(8,128)(2,1)S(1)}) fusion(f32[4,2,80,1280]{3,2,1,0:T(8,128)} %get-tuple-element.294, s32[]{:T(128)} %get-tuple-element.283, s32[]{:T(128)S(6)} %add.637), kind=kLoop, calls=%fused_computation.16.clone.1 | loop fusion | flops 409600 | bytes 1638408 | tf_op jit(solution)/shard_map/convert.15
  202.9 1.2 cos.47
  204.2 1.1 copy.35
  205.2 1.0 cos.48
  206.2 2.2 cos.49
  208.4 1.1 copy.37
  210.5 2.2 sin.47
  212.7 1.1 copy.34
  213.8 1.0 sin.48
  214.7 1.2 sin.49
  216.0 1.1 copy.36
  217.3 3.9 %fusion.70 = f32[800,2048]{1,0:T(8,128)S(1)} fusion(bf16[512,2048]{1,0:T(8,128)(2,1)} %get-tuple-element.295, bf16[400,256]{0,1:T(8,128)(2,1)} %sin.48, bf16[400,256]{0,1:T(8,128)(2,1)} %cos.48, bf16[400,256]{0,1:T(8,128)(2,1)S(1)} %sin.50, bf16[400,256]{0,1:T(8,128)(2,1)} %cos.50), kind=kOutput, calls=%fused_computation.5.clone.1 | convolution fusion | flops 1680998400 | bytes 9469952 | tf_op jit(solution)/shard_map/while/body/eval_jaxpr/dot_general | solution.py:53
  221.2 1.1 multiply_reduce_fusion.3
  222.4 5.2 %cosine_convert_fusion.4 = (bf16[1,1,80,1280]{3,2,1,0:T(8,128)(2,1)}, bf16[1,1,80,1280]{3,2,1,0:T(8,128)(2,1)}, bf16[1,1,80,1280]{3,2,1,0:T(8,128)(2,1)S(1)}, bf16[1,1,80,1280]{3,2,1,0:T(8,128)(2,1)S(1)}) fusion(f32[4,2,80,1280]{3,2,1,0:T(8,128)} %get-tuple-element.294, s32[]{:T(128)} %get-tuple-element.283, s32[]{:T(128)S(6)} %add.637), kind=kLoop, calls=%fused_computation.16.clone.1 | loop fusion | flops 409600 | bytes 1638408 | tf_op jit(solution)/shard_map/convert.15
  227.6 1.2 cos.47
  228.8 1.1 copy.35
  229.9 1.0 cos.48
  230.8 2.2 cos.49
  233.1 1.1 copy.37
  235.1 2.2 sin.47
  237.3 1.1 copy.34
  239.4 1.2 sin.49
  240.6 1.1 copy.36
  241.9 3.8 %fusion.70 = f32[800,2048]{1,0:T(8,128)S(1)} fusion(bf16[512,2048]{1,0:T(8,128)(2,1)} %get-tuple-element.295, bf16[400,256]{0,1:T(8,128)(2,1)} %sin.48, bf16[400,256]{0,1:T(8,128)(2,1)} %cos.48, bf16[400,256]{0,1:T(8,128)(2,1)S(1)} %sin.50, bf16[400,256]{0,1:T(8,128)(2,1)} %cos.50), kind=kOutput, calls=%fused_computation.5.clone.1 | convolution fusion | flops 1680998400 | bytes 9469952 | tf_op jit(solution)/shard_map/while/body/eval_jaxpr/dot_general | solution.py:53
  245.8 1.1 multiply_reduce_fusion.3
  247.0 5.2 %cosine_convert_fusion.4 = (bf16[1,1,80,1280]{3,2,1,0:T(8,128)(2,1)}, bf16[1,1,80,1280]{3,2,1,0:T(8,128)(2,1)}, bf16[1,1,80,1280]{3,2,1,0:T(8,128)(2,1)S(1)}, bf16[1,1,80,1280]{3,2,1,0:T(8,128)(2,1)S(1)}) fusion(f32[4,2,80,1280]{3,2,1,0:T(8,128)} %get-tuple-element.294, s32[]{:T(128)} %get-tuple-element.283, s32[]{:T(128)S(6)} %add.637), kind=kLoop, calls=%fused_computation.16.clone.1 | loop fusion | flops 409600 | bytes 1638408 | tf_op jit(solution)/shard_map/convert.15
  252.2 1.2 cos.47
  253.4 1.1 copy.35
  254.5 1.0 cos.48
  255.5 2.2 cos.49
  257.7 1.1 copy.37
  259.7 2.2 sin.47
  261.9 1.1 copy.34
  264.0 1.2 sin.49
  265.2 1.1 copy.36
  266.6 3.9 %fusion.70 = f32[800,2048]{1,0:T(8,128)S(1)} fusion(bf16[512,2048]{1,0:T(8,128)(2,1)} %get-tuple-element.295, bf16[400,256]{0,1:T(8,128)(2,1)} %sin.48, bf16[400,256]{0,1:T(8,128)(2,1)} %cos.48, bf16[400,256]{0,1:T(8,128)(2,1)S(1)} %sin.50, bf16[400,256]{0,1:T(8,128)(2,1)} %cos.50), kind=kOutput, calls=%fused_computation.5.clone.1 | convolution fusion | flops 1680998400 | bytes 9469952 | tf_op jit(solution)/shard_map/while/body/eval_jaxpr/dot_general | solution.py:53
  270.4 1.1 multiply_reduce_fusion.3
  272.4 21.9 %all-gather = bf16[16,4,1600]{2,1,0:T(4,128)(2,1)S(1)} all-gather(bf16[1,4,1600]{2,1,0:T(4,128)(2,1)S(1)} %copy.28), channel_id=1, replica_groups=mesh['wide'=16,'narrow'=16] {'wide'}, dimensions={0}, use_global_device_ids=true | all-gather | bytes 217600 | tf_op jit(solution)/shard_map/all_gather | solution.py:123
  295.5 6.8 %all-to-all-start = ((f32[16,4,320]{2,1,0:T(4,128)}), f32[16,4,320]{2,1,0:T(4,128)S(1)}, u32[]{:S(2)}, u32[]{:S(2)}) async-start(f32[16,4,320]{2,1,0:T(4,128)} %reshape.294), calls=%async_computation | async-start | bytes 196608 | tf_op jit(solution)/shard_map/all_to_all | solution.py:128
  302.9 6.0 %all-to-all-done = f32[16,4,320]{2,1,0:T(4,128)S(1)} async-done(((f32[16,4,320]{2,1,0:T(4,128)}), f32[16,4,320]{2,1,0:T(4,128)S(1)}, u32[]{:S(2)}, u32[]{:S(2)}) %all-to-all-start) | async-done | bytes 81952 | tf_op jit(solution)/shard_map/all_to_all | solution.py:128
  (75 shorter events, 18.7 us)
Async XLA Ops:
  7.2 287.2 %copy-start = (bf16[1600,320]{0,1:T(8,128)(2,1)S(1)}, bf16[1600,320]{0,1:T(8,128)(2,1)}, u32[]{:S(2)}) copy-start(bf16[1600,320]{0,1:T(8,128)(2,1)} %param.9) | copy-start | bytes 3072004
  7.2 159.0 %all-reduce.2.cloned.1.call-start = ((), (), s32[]{:S(2)}) async-start(), calls=%async_computation.1 | async-start | bytes 3244032 | tf_op jit(solution)/shard_map/psum | solution.py:87
  32.0 1.5 copy-start.2
  32.0 83.7 %copy-start.3 = (s32[2,5,80]{2,0,1:T(2,128)S(1)}, s32[2,5,80]{2,0,1:T(2,128)}, u32[]{:S(2)}) copy-start(s32[2,5,80]{2,0,1:T(2,128)} %param.8) | copy-start | bytes 9604
  171.4 1.7 copy-start.1
  295.5 13.4 %all-to-all-start = ((f32[16,4,320]{2,1,0:T(4,128)}), f32[16,4,320]{2,1,0:T(4,128)S(1)}, u32[]{:S(2)}, u32[]{:S(2)}) async-start(f32[16,4,320]{2,1,0:T(4,128)} %reshape.294), calls=%async_computation | async-start | bytes 196608 | tf_op jit(solution)/shard_map/all_to_all | solution.py:128
Sparse Core Ops, SparseCore 0:
  33.6 116.6 all-reduce.1

commit v5 on v4

v5 whole, which is shorter than its diff:
```python
import math

import jax
import jax.numpy as jnp
from jax import lax
from jax.sharding import PartitionSpec as P

L = 4
NSUB = 80
SAMP = 16
NPIX = 32
NSENS = 2
SPREAD = 64
FR_DEV = 4
PUP = 1280
f32 = jnp.float32
bf16 = jnp.bfloat16


def split_hi_lo(x):
    hi = x.astype(bf16)
    return hi, (x - hi.astype(f32)).astype(bf16)

def dft_factors(samp, npix):
    ids = jnp.arange(samp, dtype=jnp.int32)
    pix = jnp.arange(npix, dtype=jnp.int32) - npix // 2
    turns = jnp.mod(pix[:, None] * ids[None, :], npix)
    angles = turns.astype(f32) * f32(-2.0 * math.pi / npix)
    return jnp.cos(angles), jnp.sin(angles)

def block_diag(block, count):
    eye = jnp.eye(count, dtype=block.dtype)
    p, q = block.shape
    return (eye[:, None, :, None] * block[None, :, None, :]).reshape(count * p, count * q)

def centroids_sep(phase, sub_rows):
    items = phase.shape[0]
    rows = sub_rows * SAMP
    lane_subs = 128 // SAMP
    groups = PUP // 128
    cosf, sinf = dft_factors(SAMP, NPIX)
    bc = block_diag(cosf.T, lane_subs)
    bs = block_diag(sinf.T, lane_subs)
    rhs1 = jnp.concatenate([jnp.concatenate([bc, bs], 1), jnp.concatenate([-bs, bc], 1)], 0)
    r1_hi, r1_lo = split_hi_lo(rhs1)
    rhs1 = jnp.concatenate([r1_hi, r1_lo], 0)
    fc = jnp.cos(phase).astype(bf16).reshape(items, rows, groups, 128)
    fs = jnp.sin(phase).astype(bf16).reshape(items, rows, groups, 128)
    lhs1 = jnp.concatenate([fc, fs, fc, fs], axis=-1)
    t = jnp.einsum("irgk,kn->irgn", lhs1, rhs1, preferred_element_type=f32)
    half = lane_subs * NPIX
    tcomb = jnp.concatenate([t[..., :half], t[..., half:]], axis=1).reshape(items, 2 * rows, groups * half)
    t_hi, t_lo = split_hi_lo(tcomb)
    rhs2 = jnp.concatenate([t_hi, t_lo, t_hi], axis=1)
    ac = block_diag(cosf, sub_rows)
    as_ = block_diag(sinf, sub_rows)
    m2 = jnp.concatenate([jnp.concatenate([ac, -as_], 1), jnp.concatenate([as_, ac], 1)], 0)
    m_hi, m_lo = split_hi_lo(m2)
    lhs2 = jnp.concatenate([m_hi, m_hi, m_lo], axis=1)
    s = jnp.einsum("pq,iqn->ipn", lhs2, rhs2, preferred_element_type=f32)
    s_re = s[:, : sub_rows * NPIX]
    s_im = s[:, sub_rows * NPIX :]
    inten = (s_re * s_re + s_im * s_im).reshape(items, sub_rows, NPIX, PUP // SAMP, NPIX)
    w = jnp.arange(NPIX, dtype=f32) - NPIX // 2
    flux = jnp.sum(inten, axis=(2, 4))
    cx = jnp.sum(inten * w, axis=(2, 4)) / flux
    cy = jnp.sum(inten * w[:, None, None], axis=(2, 4)) / flux
    return jnp.stack([cx, cy], axis=-1)


def body(screens, offsets, valid, recon):
    narrow_count = lax.axis_size("narrow")
    wide_index = lax.axis_index("wide")
    narrow_index = lax.axis_index("narrow")
    band_rows = screens.shape[1]
    sub_rows = valid.shape[1]
    pixel_rows = sub_rows * SAMP
    slab_rows = pixel_rows + SPREAD
    union_cols = PUP + SPREAD
    local_items = FR_DEV * NSENS
    own_offsets = lax.dynamic_slice_in_dim(offsets, wide_index * local_items, local_items, 1)
    lowest = jnp.min(offsets, axis=1)
    pad = jnp.zeros((slab_rows, union_cols), screens.dtype)
    slabs = []
    for which_layer in range(L):
        band = lax.dynamic_slice_in_dim(screens[which_layer], lowest[1, which_layer], union_cols, 1)
        padded = jnp.concatenate([pad, band, pad], axis=0)
        group_start = lowest[0, which_layer] + pixel_rows * narrow_index
        row_at = jnp.clip(group_start - wide_index * band_rows + slab_rows, 0, band_rows + slab_rows)
        slabs.append(lax.dynamic_slice_in_dim(padded, row_at, slab_rows, 0))
    slabs = lax.psum(jnp.stack(slabs), "wide")
    rel = own_offsets - lowest[:, None, :]
    phases = []
    for item in range(local_items):
        acc = jnp.zeros((pixel_rows, PUP), jnp.float32)
        for which_layer in range(L):
            window = lax.dynamic_slice(
                slabs[which_layer], (rel[0, item, which_layer], rel[1, item, which_layer]), (pixel_rows, PUP)
            )
            acc = acc + window.astype(jnp.float32)
        phases.append(acc)
    pupil_phase = jnp.stack(phases)
    measured = centroids_sep(pupil_phase, sub_rows)
    measured = measured.reshape(FR_DEV, NSENS, sub_rows, NSUB, 2) * valid[None, :, :, :, None].astype(
        jnp.float32
    )
    slopes = measured.transpose(4, 0, 1, 2, 3)
    slope_vector = (
        measured.transpose(0, 2, 1, 3, 4)
        .reshape(FR_DEV, sub_rows * NSENS * NSUB * 2)
        .astype(jnp.bfloat16)
    )
    partial_commands = jnp.dot(
        lax.all_gather(slope_vector, "wide", axis=0, tiled=True),
        recon,
        preferred_element_type=jnp.float32,
    )
    partial_commands = partial_commands.reshape(narrow_count, -1, partial_commands.shape[1])
    commands = jnp.sum(lax.all_to_all(partial_commands, "narrow", 0, 0), axis=0)
    return (slopes, commands)


def solution(mesh):
    return jax.shard_map(
        body,
        mesh=mesh,
        in_specs=(P(None, "wide", None), P(), P(None, "narrow", None), P("narrow", "wide")),
        out_specs=(P(None, "wide", None, "narrow", None), P("narrow", "wide")),
        check_vma=False,
    )
```

time: 320 us -> 364 us (1.14)
  other arithmetic: 46 us -> 86 us
  matrix products: 15.8 us -> 25.7 us
  local copies, waits for them, and re-layouts: 76 us -> 70.8 us
    reshape x1 -> x2, local copies, waits for them, and re-layouts: 0.1 us -> 41.4 us  [the longest x1 30.1 us: centroids_sep(): (s_re * s_re + s_im * s_im).reshape(items, sub_rows, NPIX, PUP // SAMP, N...]
    cos x24 -> x0, local copies, waits for them, and re-layouts: 30.1 us -> none  [subaperture_fields(): jnp.cos(samples)]
    sin x24 -> x0, local copies, waits for them, and re-layouts: 27.1 us -> none  [subaperture_fields(): jnp.sin(samples)]
    convert_element_type x6 -> x9, other arithmetic: 4.8 us -> 27.5 us  [the longest x3 15.3 us: split_hi_lo(): return (hi, (x - hi.astype(f32)).astype(bf16))]
    another operation x8 -> x0, other arithmetic: 20.9 us -> none
    reduce_sum x4 -> x1, other arithmetic: 4.35 us -> 23.7 us  [centroids_sep(): cx = jnp.sum(inten * w, axis=(2, 4)) / flux]
    add x0 -> x1, other arithmetic: none -> 13.9 us  [centroids_sep(): s_re * s_re + s_im * s_im]
    slice x0 -> x1, local copies, waits for them, and re-layouts: none -> 10.9 us  [centroids_sep(): t[..., :half]]
  transfers between devices with their start and end apart: 2 -> 2, of which waited for: 1 -> 1; matrix products, arithmetic and copies ran while one was open for 5% -> 1% of each run, Pallas kernels for 0% -> 0%
where the time goes in v5:
time: 364 us; the launch traced here: 361 us
  between operations  144 us (40%)
  other arithmetic  86 us (24%)
  local copies, waits for them, and re-layouts  70.8 us (19%)
  matrix products  25.7 us (7%)
  blocking collectives  21.9 us (6%)
  starting transfers between devices  6.79 us (2%)
  waiting for transfers between devices  6.07 us (2%)
    reshape x1, local copies, waits for them, and re-layouts, centroids_sep(): (s_re * s_re + s_im * s_im).reshape(items, sub_rows, NPIX, PUP // SAMP, N...  30.1 us
    reduce_sum x1, other arithmetic, centroids_sep(): cx = jnp.sum(inten * w, axis=(2, 4)) / flux  23.7 us
    all_gather x1, blocking collectives, body(): lax.all_gather(slope_vector, 'wide', axis=0, tiled=True)  21.9 us
    dot_general x1, matrix products, centroids_sep(): s = jnp.einsum('pq,iqn->ipn', lhs2, rhs2, preferred_element_type=f32)  18.8 us
    convert_element_type x3, other arithmetic, split_hi_lo(): return (hi, (x - hi.astype(f32)).astype(bf16))  15.3 us
    add x1, other arithmetic, centroids_sep(): s_re * s_re + s_im * s_im  13.9 us
    unnamed x8, other arithmetic  13.7 us
    convert_element_type x1, other arithmetic, centroids_sep(): fc = jnp.cos(phase).astype(bf16).reshape(items, rows, groups, 128)  12 us
  transfers between devices with their start and end apart: 2, of which 1 were waited for; matrix products, arithmetic and copies ran while one was open for 1% of the time, Pallas kernels for 0%

profile of v5, /device:TPU:1, one launch (start us, length us, event | category | flops | bytes accessed | tf_op | source)
XLA Modules:
  0.0 361.1 jit_solution(5167372941720502513)
XLA Ops:
  7.2 0.0 copy-start
  7.2 0.0 all-reduce.2.cloned.1.call-start
  7.2 0.9 reduce_min.9
  8.1 0.7 fusion.68
  13.7 5.6 %fusion.61 = (bf16[1,256,4096]{2,1,0:T(8,128)(2,1)S(1)}, bf16[1,256,4096]{2,1,0:T(8,128)(2,1)}, bf16[1,256,4096]{2,1,0:T(8,128)(2,1)}, bf16[1,256,4096]{2,1,0:T(8,128)(2,1)}) fusion(bf16[4,256,4096]{2,1,0:T(8,128)(2,1)} %param.4), kind=kLoop, calls=%fused_computation.123 | loop fusion | bytes 16777216 | tf_op jit(solution)/shard_map/slice | solution.py:86
  24.5 2.3 dynamic-slice_bitcast_fusion
  26.7 2.0 dynamic-slice_bitcast_fusion.2
  28.8 3.2 fusion.31
  32.1 0.0 copy-start.1
  32.1 1.4 pad_maximum_fusion
  33.5 0.0 copy-start.2
  33.5 0.0 all-reduce.2.cloned.1.call-update
  33.5 0.0 copy-done.1
  33.5 0.1 fusion.50
  33.6 0.7 fusion.66
  34.4 0.6 fusion.67
  67.6 0.7 fusion.65
  91.8 0.7 fusion.64
  116.1 0.1 fusion.53
  116.2 0.1 fusion.51
  116.2 0.2 broadcast_multiply_fusion
  116.4 0.2 mul.268
  116.6 0.2 mul.265
  116.8 0.1 broadcast_multiply_fusion.2
  116.9 0.1 mul.280
  117.0 0.1 copy.46
  117.1 0.1 mul.277
  117.3 0.1 copy.47
  117.4 0.0 copy-done.2
  157.2 0.1 fusion.37
  157.3 0.2 subtract_convert_fusion.2
  157.5 0.0 all-reduce.2.cloned.1.call-done
  157.6 1.5 fusion.62
  159.1 0.5 bitcast_dynamic-update-slice_fusion.7
  159.5 0.6 bitcast_dynamic-update-slice_fusion.6
  160.1 0.6 bitcast_dynamic-update-slice_fusion.5
  160.7 0.6 bitcast_dynamic-update-slice_fusion.4
  161.2 0.6 bitcast_dynamic-update-slice_fusion.3
  161.8 0.6 bitcast_dynamic-update-slice_fusion.2
  162.4 0.7 bitcast_dynamic-update-slice_fusion.1
  163.1 0.6 bitcast_dynamic-update-slice_fusion
  163.7 12.0 %cosine_convert_fusion = (bf16[8,80,10,128]{3,1,2,0:T(8,128)(2,1)S(1)}, bf16[8,80,10,128]{3,1,2,0:T(8,128)(2,1)S(1)}) fusion(f32[8,80,10,128]{3,1,2,0:T(8,128)S(1)} %bitcast_dynamic-update-slice_fusion), kind=kLoop, calls=%fused_computation.31 | loop fusion | flops 1638400 | bytes 6553600 | tf_op jit(solution)/shard_map/convert_element_type | solution.py:47
  175.7 6.6 %fusion.10 = f32[8,80,10,512]{3,1,2,0:T(8,128)} fusion(bf16[8,80,10,128]{3,1,2,0:T(8,128)(2,1)S(1)} %get-tuple-element.20, bf16[8,80,10,128]{3,1,2,0:T(8,128)(2,1)S(1)} %get-tuple-element.19, bf16[256,512]{1,0:T(8,128)(2,1)S(1)} %subtract_convert_fusion.1, bf16[256,512]{1,0:T(8,128)(2,1)S(1)} %fusion.32), kind=kOutput, calls=%fused_computation.14 | convolution fusion | flops 3382706176 | bytes 16908288 | tf_op jit(solution)/shard_map/irgk,kn->irgn/dot_general | solution.py:50
  182.3 10.9 %fusion.60 = (f32[8,80,10,256]{3,1,2,0:T(8,128)}, f32[8,80,10,256]{3,1,2,0:T(8,128)}) fusion(f32[8,80,10,512]{3,1,2,0:T(8,128)} %fusion.10), kind=kLoop, calls=%fused_computation.122 | loop fusion | bytes 26214400 | tf_op jit(solution)/shard_map/slice | solution.py:52
  193.2 9.7 %maximum_bitcast_fusion = f32[8,10,20,8,256]{4,3,2,1,0:T(8,128)} fusion(f32[8,80,10,256]{3,1,2,0:T(8,128)} %get-tuple-element.14, f32[8,80,10,256]{3,1,2,0:T(8,128)} %get-tuple-element.13), kind=kLoop, calls=%fused_computation.11 | loop fusion | flops 3276800 | bytes 26214400
  202.9 11.2 %copy.64 = f32[8,10,20,8,256]{4,3,1,2,0:T(8,128)} copy(f32[8,10,20,8,256]{4,3,2,1,0:T(8,128)} %maximum_bitcast_fusion) | data formatting | bytes 26214400 | tf_op jit(solution)/shard_map/reshape | solution.py:52
  214.1 15.1 %subtract_convert_fusion = (bf16[8,160,2560]{2,1,0:T(8,128)(2,1)}, bf16[8,160,2560]{2,1,0:T(8,128)(2,1)}) fusion(f32[8,160,2560]{2,1,0:T(8,128)} %bitcast.158), kind=kLoop, calls=%fused_computation.12 | loop fusion | flops 13107200 | bytes 26214400 | tf_op jit(solution)/shard_map/convert_element_type | solution.py:22
  229.3 18.8 %fusion.7 = f32[8,320,2560]{2,1,0:T(8,128)} fusion(bf16[8,160,2560]{2,1,0:T(8,128)(2,1)} %get-tuple-element.12, bf16[8,160,2560]{2,1,0:T(8,128)(2,1)} %get-tuple-element.11, bf16[320,160]{1,0:T(8,128)(2,1)S(1)} %subtract_convert_fusion.2, bf16[320,160]{1,0:T(8,128)(2,1)S(1)} %fusion.37), kind=kOutput, calls=%fused_computation.13 | convolution fusion | flops 6351360000 | bytes 39526400 | tf_op jit(solution)/shard_map/pq,iqn->ipn/dot_general | solution.py:60
  248.0 13.9 %fusion.6 = f32[8,160,2560]{2,1,0:T(8,128)} fusion(f32[8,320,2560]{2,1,0:T(8,128)} %fusion.7), kind=kLoop, calls=%fused_computation.9 | loop fusion | flops 9830400 | bytes 39321600 | tf_op jit(solution)/shard_map/add | solution.py:63
  261.9 30.1 %reshape.264 = f32[8,5,32,80,32]{4,3,2,1,0:T(8,128)} reshape(f32[8,160,2560]{2,1,0:T(8,128)} %fusion.6) | data formatting | bytes 26214400 | tf_op jit(solution)/shard_map/reshape | solution.py:63
  292.0 23.7 %multiply_reduce_fusion.1 = (f32[8,5,80]{2,1,0:T(8,128)S(1)}, f32[8,5,80]{2,1,0:T(8,128)S(1)}, f32[8,5,80]{2,1,0:T(8,128)S(1)}) fusion(f32[8,5,32,80,32]{4,3,2,1,0:T(8,128)} %reshape.264, f32[32]{0:T(128)S(1)} %iota_add_fusion), kind=kLoop, calls=%fused_computation.1 | loop fusion | flops 16374400 | bytes 13145728 | tf_op jit(solution)/shard_map/reduce_sum | solution.py:66
  315.8 1.1 copy.52
  316.9 0.2 copy.53
  317.1 21.9 %all-gather = bf16[16,4,1600]{2,1,0:T(4,128)(2,1)S(1)} all-gather(bf16[1,4,1600]{2,1,0:T(4,128)(2,1)S(1)} %copy.53), channel_id=1, replica_groups=mesh['wide'=16,'narrow'=16] {'wide'}, dimensions={0}, use_global_device_ids=true | all-gather | bytes 217600 | tf_op jit(solution)/shard_map/all_gather | solution.py:114
  339.0 0.1 reshape.267
  339.1 0.0 copy-done
  339.1 0.4 fusion.69
  339.6 0.7 reshape.265
  340.2 6.8 %all-to-all-start = ((f32[16,4,320]{2,1,0:T(4,128)}), f32[16,4,320]{2,1,0:T(4,128)S(1)}, u32[]{:S(2)}, u32[]{:S(2)}) async-start(f32[16,4,320]{2,1,0:T(4,128)} %reshape.265), calls=%async_computation | async-start | bytes 196608 | tf_op jit(solution)/shard_map/all_to_all | solution.py:119
  347.0 0.6 copy.54
  347.6 6.0 %all-to-all-done = f32[16,4,320]{2,1,0:T(4,128)S(1)} async-done(((f32[16,4,320]{2,1,0:T(4,128)}), f32[16,4,320]{2,1,0:T(4,128)S(1)}, u32[]{:S(2)}, u32[]{:S(2)}) %all-to-all-start) | async-done | bytes 81952 | tf_op jit(solution)/shard_map/all_to_all | solution.py:119
  353.6 0.6 reduce_sum.39
  (14 shorter events, 0.2 us)
Async XLA Ops:
  7.2 331.9 %copy-start = (bf16[1600,320]{0,1:T(8,128)(2,1)S(1)}, bf16[1600,320]{0,1:T(8,128)(2,1)}, u32[]{:S(2)}) copy-start(bf16[1600,320]{0,1:T(8,128)(2,1)} %param.7) | copy-start | bytes 3072004
  7.2 150.4 %all-reduce.2.cloned.1.call-start = ((), (), s32[]{:S(2)}) async-start(), calls=%async_computation.1 | async-start | bytes 3244032 | tf_op jit(solution)/shard_map/psum | solution.py:91
  32.1 1.5 copy-start.1
  33.5 83.9 %copy-start.2 = (s32[2,5,80]{2,0,1:T(2,128)S(1)}, s32[2,5,80]{2,0,1:T(2,128)}, u32[]{:S(2)}) copy-start(s32[2,5,80]{2,0,1:T(2,128)} %param.6) | copy-start | bytes 9604
  340.2 13.4 %all-to-all-start = ((f32[16,4,320]{2,1,0:T(4,128)}), f32[16,4,320]{2,1,0:T(4,128)S(1)}, u32[]{:S(2)}, u32[]{:S(2)}) async-start(f32[16,4,320]{2,1,0:T(4,128)} %reshape.265), calls=%async_computation | async-start | bytes 196608 | tf_op jit(solution)/shard_map/all_to_all | solution.py:119
Sparse Core Ops, SparseCore 0:
  33.7 116.6 all-reduce.1

commit v6 on v5

--- a/solution.py
+++ b/solution.py
@@ -3,6 +3,7 @@
 import jax
 import jax.numpy as jnp
 from jax import lax
+from jax.experimental import pallas as pl
 from jax.sharding import PartitionSpec as P
 
 L = 4
@@ -13,13 +14,15 @@
 SPREAD = 64
 FR_DEV = 4
 PUP = 1280
+LANES = 128
 f32 = jnp.float32
 bf16 = jnp.bfloat16
 
 
 def split_hi_lo(x):
-    hi = x.astype(bf16)
-    return hi, (x - hi.astype(f32)).astype(bf16)
+    hi = lax.reduce_precision(x, exponent_bits=8, mantissa_bits=7)
+    return hi.astype(bf16), (x - hi).astype(bf16)
+
 
 def dft_factors(samp, npix):
     ids = jnp.arange(samp, dtype=jnp.int32)
@@ -28,44 +31,92 @@
     angles = turns.astype(f32) * f32(-2.0 * math.pi / npix)
     return jnp.cos(angles), jnp.sin(angles)
 
+
 def block_diag(block, count):
     eye = jnp.eye(count, dtype=block.dtype)
     p, q = block.shape
     return (eye[:, None, :, None] * block[None, :, None, :]).reshape(count * p, count * q)
 
-def centroids_sep(phase, sub_rows):
-    items = phase.shape[0]
-    rows = sub_rows * SAMP
-    lane_subs = 128 // SAMP
-    groups = PUP // 128
+
+def dft_operands(sub_rows):
+    lane_subs = LANES // SAMP
     cosf, sinf = dft_factors(SAMP, NPIX)
     bc = block_diag(cosf.T, lane_subs)
     bs = block_diag(sinf.T, lane_subs)
     rhs1 = jnp.concatenate([jnp.concatenate([bc, bs], 1), jnp.concatenate([-bs, bc], 1)], 0)
     r1_hi, r1_lo = split_hi_lo(rhs1)
     rhs1 = jnp.concatenate([r1_hi, r1_lo], 0)
-    fc = jnp.cos(phase).astype(bf16).reshape(items, rows, groups, 128)
-    fs = jnp.sin(phase).astype(bf16).reshape(items, rows, groups, 128)
-    lhs1 = jnp.concatenate([fc, fs, fc, fs], axis=-1)
-    t = jnp.einsum("irgk,kn->irgn", lhs1, rhs1, preferred_element_type=f32)
-    half = lane_subs * NPIX
-    tcomb = jnp.concatenate([t[..., :half], t[..., half:]], axis=1).reshape(items, 2 * rows, groups * half)
-    t_hi, t_lo = split_hi_lo(tcomb)
-    rhs2 = jnp.concatenate([t_hi, t_lo, t_hi], axis=1)
     ac = block_diag(cosf, sub_rows)
     as_ = block_diag(sinf, sub_rows)
     m2 = jnp.concatenate([jnp.concatenate([ac, -as_], 1), jnp.concatenate([as_, ac], 1)], 0)
     m_hi, m_lo = split_hi_lo(m2)
     lhs2 = jnp.concatenate([m_hi, m_hi, m_lo], axis=1)
-    s = jnp.einsum("pq,iqn->ipn", lhs2, rhs2, preferred_element_type=f32)
-    s_re = s[:, : sub_rows * NPIX]
-    s_im = s[:, sub_rows * NPIX :]
-    inten = (s_re * s_re + s_im * s_im).reshape(items, sub_rows, NPIX, PUP // SAMP, NPIX)
-    w = jnp.arange(NPIX, dtype=f32) - NPIX // 2
-    flux = jnp.sum(inten, axis=(2, 4))
-    cx = jnp.sum(inten * w, axis=(2, 4)) / flux
-    cy = jnp.sum(inten * w[:, None, None], axis=(2, 4)) / flux
-    return jnp.stack([cx, cy], axis=-1)
+    weights = jnp.arange(NPIX, dtype=f32) - NPIX // 2
+    ones = jnp.ones((NPIX,), f32)
+    eye_r = jnp.eye(sub_rows, dtype=f32)
+    wj = jnp.concatenate([(eye_r[:, :, None] * ones).reshape(sub_rows, -1),
+                          (eye_r[:, :, None] * weights).reshape(sub_rows, -1)], 0)
+    wj = jnp.pad(wj, ((0, 16 - 2 * sub_rows), (0, 0))).astype(bf16)
+    eye_c = jnp.eye(lane_subs, dtype=f32)
+    wk = jnp.concatenate([(eye_c[:, None, :] * ones[None, :, None]).reshape(-1, lane_subs),
+                          (eye_c[:, None, :] * weights[None, :, None]).reshape(-1, lane_subs)], 1)
+    return rhs1, lhs2, wj, wk.astype(bf16)
+
+
+def centroid_kernel(phase_ref, rhs1_ref, lhs2_ref, wj_ref, wk_ref, out_ref):
+    ph = phase_ref[0]
+    fc = jnp.cos(ph).astype(bf16)
+    fs = jnp.sin(ph).astype(bf16)
+    rhs1 = rhs1_ref[...]
+    lhs2 = lhs2_ref[...]
+    wj = wj_ref[...]
+    wk = wk_ref[...]
+    rows = ph.shape[0]
+    half = rhs1.shape[1] // 2
+    for g in range(ph.shape[1] // LANES):
+        fcg = fc[:, g * LANES:(g + 1) * LANES]
+        fsg = fs[:, g * LANES:(g + 1) * LANES]
+        lhs = jnp.concatenate([fcg, fsg, fcg, fsg], axis=1)
+        t = jnp.dot(lhs, rhs1, preferred_element_type=f32)
+        tc = jnp.concatenate([t[:, :half], t[:, half:]], axis=0)
+        t_hi = tc.astype(bf16)
+        t_lo = (tc - t_hi.astype(f32)).astype(bf16)
+        s = jnp.dot(lhs2, jnp.concatenate([t_hi, t_lo, t_hi], axis=0), preferred_element_type=f32)
+        sr = s[:rows * 2]
+        si = s[rows * 2:]
+        inten = sr * sr + si * si
+        i_hi = inten.astype(bf16)
+        i_lo = (inten - i_hi.astype(f32)).astype(bf16)
+        pj = jnp.dot(wj, i_hi, preferred_element_type=f32) + jnp.dot(wj, i_lo, preferred_element_type=f32)
+        p_hi = pj.astype(bf16)
+        p_lo = (pj - p_hi.astype(f32)).astype(bf16)
+        q = jnp.dot(p_hi, wk, preferred_element_type=f32) + jnp.dot(p_lo, wk, preferred_element_type=f32)
+        out_ref[0, g] = q
+
+
+def centroids_kernel(phase, sub_rows):
+    items, rows, cols = phase.shape
+    groups = cols // LANES
+    rhs1, lhs2, wj, wk = dft_operands(sub_rows)
+    sums = pl.pallas_call(
+        centroid_kernel,
+        grid=(items,),
+        in_specs=[
+            pl.BlockSpec((1, rows, cols), lambda i: (i, 0, 0)),
+            pl.BlockSpec(rhs1.shape, lambda i: (0, 0)),
+            pl.BlockSpec(lhs2.shape, lambda i: (0, 0)),
+            pl.BlockSpec(wj.shape, lambda i: (0, 0)),
+            pl.BlockSpec(wk.shape, lambda i: (0, 0)),
+        ],
+        out_specs=pl.BlockSpec((1, groups, 16, 16), lambda i: (i, 0, 0, 0)),
+        out_shape=jax.ShapeDtypeStruct((items, groups, 16, 16), f32),
+    )(phase, rhs1, lhs2, wj, wk)
+    lane_subs = LANES // SAMP
+    sums = sums.transpose(0, 2, 1, 3)
+    flux = sums[:, :sub_rows, :, :lane_subs].reshape(items, sub_rows, -1)
+    sum_x = sums[:, :sub_rows, :, lane_subs:2 * lane_subs].reshape(items, sub_rows, -1)
+    sum_y = sums[:, sub_rows:2 * sub_rows, :, :lane_subs].reshape(items, sub_rows, -1)
+    return jnp.stack([sum_x / flux, sum_y / flux], axis=-1)
 
 
 def body(screens, offsets, valid, recon):
@@ -100,7 +151,7 @@
             acc = acc + window.astype(jnp.float32)
         phases.append(acc)
     pupil_phase = jnp.stack(phases)
-    measured = centroids_sep(pupil_phase, sub_rows)
+    measured = centroids_kernel(pupil_phase, sub_rows)
     measured = measured.reshape(FR_DEV, NSENS, sub_rows, NSUB, 2) * valid[None, :, :, :, None].astype(
         jnp.float32
     )

time: 364 us -> 284 us (0.78)
  other arithmetic: 86 us -> 20.7 us
  Pallas kernels: 0 us -> 61.3 us
  local copies, waits for them, and re-layouts: 70.8 us -> 20.2 us
  matrix products: 25.7 us -> 0.43 us
    pallas_call x0 -> x1, Pallas kernels: none -> 61.3 us  [centroids_kernel(): pl.pallas_call(centroid_kernel, grid=(items,), in_specs=[pl.BlockSpec((1,...]
    reshape x2, local copies, waits for them, and re-layouts: 41.4 us -> 0.15 us  [the longest x1 0.08 us: dft_operands(): (eye_c[:, None, :] * ones[None, :, None]).reshape(-1, lane_subs)]
    convert_element_type x6 -> x2, other arithmetic: 27.5 us -> 0.2 us  [split_hi_lo(): return (hi.astype(bf16), (x - hi).astype(bf16))]
    dot_general x2 -> x0, matrix products: 25.3 us -> none  [the longest x1 18.8 us: centroids_sep(): s = jnp.einsum('pq,iqn->ipn', lhs2, rhs2, preferred_element_type=f32)]
    reduce_sum x1 -> x0, other arithmetic: 23.7 us -> none  [centroids_sep(): cx = jnp.sum(inten * w, axis=(2, 4)) / flux]
    add x1 -> x0, other arithmetic: 13.9 us -> none  [centroids_sep(): s_re * s_re + s_im * s_im]
    slice x1 -> x0, local copies, waits for them, and re-layouts: 10.9 us -> none  [centroids_sep(): t[..., :half]]
    unnamed x8 -> x7, other arithmetic: 13.7 us -> 8.46 us
  transfers between devices with their start and end apart: 2 -> 2, of which waited for: 1 -> 1; matrix products, arithmetic and copies ran while one was open for 1% -> 3% of each run, Pallas kernels for 0% -> 0%
where the time goes in v6:
time: 284 us; the launch traced here: 281 us
  between operations  144 us (51%)
  Pallas kernels  61.3 us (22%)
  blocking collectives  21.9 us (8%)
  other arithmetic  20.7 us (7%)
  local copies, waits for them, and re-layouts  20.2 us (7%)
  starting transfers between devices  6.8 us (2%)
  waiting for transfers between devices  6.05 us (2%)
    pallas_call x1, Pallas kernels, centroids_kernel(): pl.pallas_call(centroid_kernel, grid=(items,), in_specs=[pl.BlockSpec((1,...  61.3 us
    all_gather x1, blocking collectives, body(): lax.all_gather(slope_vector, 'wide', axis=0, tiled=True)  21.9 us
    unnamed x7, other arithmetic  8.46 us
    all_to_all x1, starting transfers between devices, body(): commands = jnp.sum(lax.all_to_all(partial_commands, 'narrow', 0, 0), axis=0)  6.76 us
    all_to_all x1, waiting for transfers between devices, body(): commands = jnp.sum(lax.all_to_all(partial_commands, 'narrow', 0, 0), axis=0)  6.03 us
  transfers between devices with their start and end apart: 2, of which 1 were waited for; matrix products, arithmetic and copies ran while one was open for 3% of the time, Pallas kernels for 0%

profile of v6, /device:TPU:1, one launch (start us, length us, event | category | flops | bytes accessed | tf_op | source)
XLA Modules:
  0.0 281.4 jit_solution(5945753822900132759)
XLA Ops:
  7.2 0.0 copy-start
  7.2 0.0 all-reduce.3.cloned.1.call-start
  7.2 0.9 reduce_min.9
  8.1 0.7 fusion.45
  13.9 5.6 %fusion.37 = (bf16[1,256,4096]{2,1,0:T(8,128)(2,1)S(1)}, bf16[1,256,4096]{2,1,0:T(8,128)(2,1)}, bf16[1,256,4096]{2,1,0:T(8,128)(2,1)}, bf16[1,256,4096]{2,1,0:T(8,128)(2,1)}) fusion(bf16[4,256,4096]{2,1,0:T(8,128)(2,1)} %param.4), kind=kLoop, calls=%fused_computation.93 | loop fusion | bytes 16777216 | tf_op jit(solution)/shard_map/slice | solution.py:137
  24.6 2.3 dynamic-slice_bitcast_fusion
  26.9 2.0 dynamic-slice_bitcast_fusion.2
  29.0 3.2 %fusion.12 = (bf16[1,144,1344]{2,1,0:T(8,128)(2,1)S(1)}, bf16[1,144,1344]{2,1,0:T(8,128)(2,1)S(1)}, bf16[1,144,1344]{2,1,0:T(8,128)(2,1)S(1)}, bf16[1,144,1344]{2,1,0:T(8,128)(2,1)S(1)}) fusion(s32[]{:T(128)S(6)} %min.13, bf16[144,1344]{1,0:T(8,128)(2,1)S(1)} %broadcast_in_dim.2, bf16[256,1344]{1,0:T(8,128)(2,1)S(1)} %get-tuple-element.115, s32[]{:T(128)S(6)} %min.15, ...), kind=kLoop, calls=%fused_computation.43 | loop fusion | flops 4644864 | bytes 4687888 | tf_op jit(solution)/shard_map/stack | solution.py:142
  32.2 1.4 pad_maximum_fusion
  33.7 0.0 all-reduce.3.cloned.1.call-update
  33.7 0.1 fusion.29
  33.8 0.7 fusion.43
  34.5 0.6 fusion.44
  67.7 0.7 fusion.42
  92.0 0.7 fusion.41
  116.4 0.1 fusion.32
  116.4 0.1 fusion.30
  116.5 0.1 copy.30
  116.6 0.2 broadcast_multiply_fusion
  116.8 0.2 mul.292
  117.0 0.2 mul.289
  117.1 0.1 copy.29
  117.2 0.1 broadcast_multiply_fusion.2
  117.4 0.1 mul.304
  117.5 0.1 copy.25
  117.6 0.1 mul.301
  117.7 0.1 copy.26
  117.8 0.1 mul.310
  117.9 0.1 reshape.275
  118.0 0.1 mul.312
  118.1 0.7 copy.31.wk_ref
  118.8 0.1 mul.305
  118.9 0.1 reshape.274
  118.9 0.1 mul.307
  158.9 0.6 fusion.22.wj_ref
  159.5 0.2 reduce-precision_convert_fusion.1
  159.7 0.9 pad_maximum_fusion.2.lhs2_ref
  160.6 0.1 reduce-precision_convert_fusion
  160.7 0.8 pad_maximum_fusion.1.rhs1_ref
  161.5 1.5 fusion.38
  163.0 1.2 add_dynamic-update-slice_fusion.7
  164.2 1.2 add_dynamic-update-slice_fusion.6
  165.4 1.2 add_dynamic-update-slice_fusion.5
  166.6 1.2 add_dynamic-update-slice_fusion.4
  167.8 1.2 add_dynamic-update-slice_fusion.3
  169.0 1.2 add_dynamic-update-slice_fusion.2
  170.2 1.2 add_dynamic-update-slice_fusion.1
  171.5 1.4 add_dynamic-update-slice_fusion.phase_ref
  172.8 61.3 %shard_map.59 = f32[8,10,16,16]{3,2,1,0:T(8,128)} custom-call(f32[8,80,1280]{2,1,0:T(8,128)} %add_dynamic-update-slice_fusion.phase_ref, bf16[512,512]{1,0:T(8,128)(2,1)} %pad_maximum_fusion.1.rhs1_ref, bf16[320,480]{1,0:T(8,128)(2,1)} %pad_maximum_fusion.2.lhs2_ref, bf16[16,160]{1,0:T(8,128)(2,1)} %fusion.22.wj_ref, bf16[256,16]{1,0:T(8,128)(2,1)} %copy.31.wk_ref), custom_call_target="tpu_custom_call" | custom-call | tf_op jit(solution)/shard_map/pallas_call | solution.py:101
  234.1 1.5 slice_divide_fusion.1
  235.6 0.1 copy.32
  235.7 0.1 div.29
  235.8 0.1 copy.33
  235.9 0.1 div.31
  236.1 1.1 copy.34
  237.2 0.2 copy.35
  237.4 21.9 %all-gather = bf16[16,4,1600]{2,1,0:T(4,128)(2,1)S(1)} all-gather(bf16[1,4,1600]{2,1,0:T(4,128)(2,1)S(1)} %copy.35), channel_id=1, replica_groups=mesh['wide'=16,'narrow'=16] {'wide'}, dimensions={0}, use_global_device_ids=true | all-gather | bytes 217600 | tf_op jit(solution)/shard_map/all_gather | solution.py:165
  259.3 0.1 reshape.278
  259.4 0.4 fusion.46
  259.8 0.7 reshape.276
  260.5 6.8 %all-to-all-start = ((f32[16,4,320]{2,1,0:T(4,128)}), f32[16,4,320]{2,1,0:T(4,128)S(1)}, u32[]{:S(2)}, u32[]{:S(2)}) async-start(f32[16,4,320]{2,1,0:T(4,128)} %reshape.276), calls=%async_computation | async-start | bytes 196608 | tf_op jit(solution)/shard_map/all_to_all | solution.py:170
  267.3 0.6 copy.36
  267.9 6.0 %all-to-all-done = f32[16,4,320]{2,1,0:T(4,128)S(1)} async-done(((f32[16,4,320]{2,1,0:T(4,128)}), f32[16,4,320]{2,1,0:T(4,128)S(1)}, u32[]{:S(2)}, u32[]{:S(2)}) %all-to-all-start) | async-done | bytes 81952 | tf_op jit(solution)/shard_map/all_to_all | solution.py:170
  273.9 0.6 reduce_sum.9
  (20 shorter events, 0.1 us)
Async XLA Ops:
  7.2 252.2 %copy-start = (bf16[1600,320]{0,1:T(8,128)(2,1)S(1)}, bf16[1600,320]{0,1:T(8,128)(2,1)}, u32[]{:S(2)}) copy-start(bf16[1600,320]{0,1:T(8,128)(2,1)} %param.7) | copy-start | bytes 3072004
  7.2 154.3 %all-reduce.3.cloned.1.call-start = ((), (), s32[]{:S(2)}) async-start(), calls=%async_computation.1 | async-start | bytes 3244032 | tf_op jit(solution)/shard_map/psum | solution.py:142
  32.2 1.5 copy-start.1
  116.7 2.3 copy-start.2
  260.5 13.4 %all-to-all-start = ((f32[16,4,320]{2,1,0:T(4,128)}), f32[16,4,320]{2,1,0:T(4,128)S(1)}, u32[]{:S(2)}, u32[]{:S(2)}) async-start(f32[16,4,320]{2,1,0:T(4,128)} %reshape.276), calls=%async_computation | async-start | bytes 196608 | tf_op jit(solution)/shard_map/all_to_all | solution.py:170
Sparse Core Ops, SparseCore 0:
  33.8 116.7 all-reduce.2

commit v7 on v6

--- a/solution.py
+++ b/solution.py
@@ -4,6 +4,7 @@
 import jax.numpy as jnp
 from jax import lax
 from jax.experimental import pallas as pl
+from jax.experimental.pallas import tpu as pltpu
 from jax.sharding import PartitionSpec as P
 
 L = 4
@@ -53,51 +54,55 @@
     lhs2 = jnp.concatenate([m_hi, m_hi, m_lo], axis=1)
     weights = jnp.arange(NPIX, dtype=f32) - NPIX // 2
     ones = jnp.ones((NPIX,), f32)
-    eye_r = jnp.eye(sub_rows, dtype=f32)
-    wj = jnp.concatenate([(eye_r[:, :, None] * ones).reshape(sub_rows, -1),
-                          (eye_r[:, :, None] * weights).reshape(sub_rows, -1)], 0)
-    wj = jnp.pad(wj, ((0, 16 - 2 * sub_rows), (0, 0))).astype(bf16)
     eye_c = jnp.eye(lane_subs, dtype=f32)
     wk = jnp.concatenate([(eye_c[:, None, :] * ones[None, :, None]).reshape(-1, lane_subs),
                           (eye_c[:, None, :] * weights[None, :, None]).reshape(-1, lane_subs)], 1)
-    return rhs1, lhs2, wj, wk.astype(bf16)
+    return rhs1, lhs2, wk.astype(bf16)
 
 
-def centroid_kernel(phase_ref, rhs1_ref, lhs2_ref, wj_ref, wk_ref, out_ref):
+def centroid_kernel(phase_ref, rhs1_ref, lhs2_ref, wk_ref, out_ref, acc_ref):
     ph = phase_ref[0]
     fc = jnp.cos(ph).astype(bf16)
     fs = jnp.sin(ph).astype(bf16)
     rhs1 = rhs1_ref[...]
     lhs2 = lhs2_ref[...]
-    wj = wj_ref[...]
     wk = wk_ref[...]
     rows = ph.shape[0]
+    sub_rows = rows // SAMP
+    groups = ph.shape[1] // LANES
     half = rhs1.shape[1] // 2
-    for g in range(ph.shape[1] // LANES):
-        fcg = fc[:, g * LANES:(g + 1) * LANES]
-        fsg = fs[:, g * LANES:(g + 1) * LANES]
-        lhs = jnp.concatenate([fcg, fsg, fcg, fsg], axis=1)
-        t = jnp.dot(lhs, rhs1, preferred_element_type=f32)
+    lhs = jnp.concatenate(
+        [
+            jnp.concatenate([fc[:, g * LANES:(g + 1) * LANES], fs[:, g * LANES:(g + 1) * LANES]] * 2, axis=1)
+            for g in range(groups)
+        ],
+        axis=0,
+    )
+    t_all = jnp.dot(lhs, rhs1, preferred_element_type=f32)
+    weights = (lax.broadcasted_iota(jnp.int32, (sub_rows, NPIX, 2 * half), 1) - NPIX // 2).astype(f32)
+    for g in range(groups):
+        t = t_all[g * rows:(g + 1) * rows]
         tc = jnp.concatenate([t[:, :half], t[:, half:]], axis=0)
         t_hi = tc.astype(bf16)
         t_lo = (tc - t_hi.astype(f32)).astype(bf16)
         s = jnp.dot(lhs2, jnp.concatenate([t_hi, t_lo, t_hi], axis=0), preferred_element_type=f32)
         sr = s[:rows * 2]
         si = s[rows * 2:]
-        inten = sr * sr + si * si
-        i_hi = inten.astype(bf16)
-        i_lo = (inten - i_hi.astype(f32)).astype(bf16)
-        pj = jnp.dot(wj, i_hi, preferred_element_type=f32) + jnp.dot(wj, i_lo, preferred_element_type=f32)
-        p_hi = pj.astype(bf16)
-        p_lo = (pj - p_hi.astype(f32)).astype(bf16)
-        q = jnp.dot(p_hi, wk, preferred_element_type=f32) + jnp.dot(p_lo, wk, preferred_element_type=f32)
-        out_ref[0, g] = q
+        inten = (sr * sr + si * si).reshape(sub_rows, NPIX, half)
+        acc_ref[g, 0:sub_rows, :] = jnp.sum(inten, axis=1)
+        acc_ref[g, sub_rows:2 * sub_rows, :] = jnp.sum(inten * weights[:, :, :half], axis=1)
+        acc_ref[g, 2 * sub_rows:, :] = jnp.zeros((acc_ref.shape[1] - 2 * sub_rows, half), f32)
+    pj = acc_ref[...].reshape(groups * acc_ref.shape[1], half)
+    p_hi = pj.astype(bf16)
+    p_lo = (pj - p_hi.astype(f32)).astype(bf16)
+    q = jnp.dot(p_hi, wk, preferred_element_type=f32) + jnp.dot(p_lo, wk, preferred_element_type=f32)
+    out_ref[0] = q.reshape(groups, acc_ref.shape[1], wk.shape[1])
 
 
 def centroids_kernel(phase, sub_rows):
     items, rows, cols = phase.shape
     groups = cols // LANES
-    rhs1, lhs2, wj, wk = dft_operands(sub_rows)
+    rhs1, lhs2, wk = dft_operands(sub_rows)
     sums = pl.pallas_call(
         centroid_kernel,
         grid=(items,),
@@ -105,12 +110,12 @@
             pl.BlockSpec((1, rows, cols), lambda i: (i, 0, 0)),
             pl.BlockSpec(rhs1.shape, lambda i: (0, 0)),
             pl.BlockSpec(lhs2.shape, lambda i: (0, 0)),
-            pl.BlockSpec(wj.shape, lambda i: (0, 0)),
             pl.BlockSpec(wk.shape, lambda i: (0, 0)),
         ],
         out_specs=pl.BlockSpec((1, groups, 16, 16), lambda i: (i, 0, 0, 0)),
         out_shape=jax.ShapeDtypeStruct((items, groups, 16, 16), f32),
-    )(phase, rhs1, lhs2, wj, wk)
+        scratch_shapes=[pltpu.VMEM((groups, 16, rhs1.shape[1] // 2), f32)],
+    )(phase, rhs1, lhs2, wk)
     lane_subs = LANES // SAMP
     sums = sums.transpose(0, 2, 1, 3)
     flux = sums[:, :sub_rows, :, :lane_subs].reshape(items, sub_rows, -1)

time: 284 us -> 246 us (0.87)
  Pallas kernels: 61.3 us -> 25.1 us
    pallas_call x1, Pallas kernels: 61.3 us -> 25.1 us  [centroids_kernel(): pl.pallas_call(centroid_kernel, grid=(items,), in_specs=[pl.BlockSpec((1,...]
where the time goes in v7:
time: 246 us; the launch traced here: 244 us
  between operations  144 us (59%)
  Pallas kernels  25.1 us (10%)
  blocking collectives  21.9 us (9%)
  other arithmetic  20.1 us (8%)
  local copies, waits for them, and re-layouts  19.9 us (8%)
  starting transfers between devices  6.8 us (3%)
  waiting for transfers between devices  6.05 us (2%)
    pallas_call x1, Pallas kernels, centroids_kernel(): pl.pallas_call(centroid_kernel, grid=(items,), in_specs=[pl.BlockSpec((1,...  25.1 us
    all_gather x1, blocking collectives, body(): lax.all_gather(slope_vector, 'wide', axis=0, tiled=True)  21.9 us
    unnamed x7, other arithmetic  8.46 us
    all_to_all x1, starting transfers between devices, body(): commands = jnp.sum(lax.all_to_all(partial_commands, 'narrow', 0, 0), axis=0)  6.76 us
    all_to_all x1, waiting for transfers between devices, body(): commands = jnp.sum(lax.all_to_all(partial_commands, 'narrow', 0, 0), axis=0)  6.03 us
    slice x1, local copies, waits for them, and re-layouts, body(): screens[which_layer]  5.64 us
  transfers between devices with their start and end apart: 2, of which 1 were waited for; matrix products, arithmetic and copies ran while one was open for 3% of the time, Pallas kernels for 0%

profile of v7, /device:TPU:1, one launch (start us, length us, event | category | flops | bytes accessed | tf_op | source)
XLA Modules:
  0.0 244.0 jit_solution(17065208612866054014)
XLA Ops:
  7.2 0.0 copy-start
  7.2 0.0 all-reduce.2.cloned.1.call-start
  7.2 0.9 reduce_min.9
  8.1 0.7 fusion.41
  14.0 5.6 %fusion.34 = (bf16[1,256,4096]{2,1,0:T(8,128)(2,1)S(1)}, bf16[1,256,4096]{2,1,0:T(8,128)(2,1)}, bf16[1,256,4096]{2,1,0:T(8,128)(2,1)}, bf16[1,256,4096]{2,1,0:T(8,128)(2,1)}) fusion(bf16[4,256,4096]{2,1,0:T(8,128)(2,1)} %param.4), kind=kLoop, calls=%fused_computation.88 | loop fusion | bytes 16777216 | tf_op jit(solution)/shard_map/slice | solution.py:142
  24.8 2.3 dynamic-slice_bitcast_fusion
  27.0 2.0 dynamic-slice_bitcast_fusion.2
  29.1 3.2 %fusion.12 = (bf16[1,144,1344]{2,1,0:T(8,128)(2,1)S(1)}, bf16[1,144,1344]{2,1,0:T(8,128)(2,1)S(1)}, bf16[1,144,1344]{2,1,0:T(8,128)(2,1)S(1)}, bf16[1,144,1344]{2,1,0:T(8,128)(2,1)S(1)}) fusion(s32[]{:T(128)S(6)} %min.13, bf16[144,1344]{1,0:T(8,128)(2,1)S(1)} %broadcast_in_dim.2, bf16[256,1344]{1,0:T(8,128)(2,1)S(1)} %get-tuple-element.113, s32[]{:T(128)S(6)} %min.15, ...), kind=kLoop, calls=%fused_computation.43 | loop fusion | flops 4644864 | bytes 4687888 | tf_op jit(solution)/shard_map/stack | solution.py:147
  32.3 0.0 copy-start.1
  32.3 1.4 pad_maximum_fusion
  33.8 0.0 all-reduce.2.cloned.1.call-update
  33.8 0.0 copy-done.1
  33.8 0.1 fusion.26
  33.9 0.7 fusion.39
  34.6 0.6 fusion.40
  67.5 0.7 fusion.38
  92.0 0.7 fusion.37
  116.2 0.1 fusion.29
  116.3 0.1 fusion.27
  116.4 0.1 copy.27
  116.4 0.2 broadcast_multiply_fusion
  116.6 0.0 copy-start.2
  116.6 0.2 mul.269
  116.8 0.2 mul.266
  117.0 0.1 broadcast_multiply_fusion.2
  117.1 0.1 mul.281
  117.2 0.1 copy.23
  117.4 0.1 mul.278
  117.5 0.1 copy.24
  117.6 0.1 mul.282
  117.6 0.1 reshape.254
  117.7 0.1 mul.284
  117.8 0.7 copy.28.wk_ref
  118.6 0.0 copy-done.2
  158.3 0.2 reduce-precision_convert_fusion.1
  158.5 0.9 pad_maximum_fusion.2.lhs2_ref
  159.4 0.1 reduce-precision_convert_fusion
  159.5 0.8 pad_maximum_fusion.1.rhs1_ref
  160.3 1.5 fusion.35
  161.8 1.2 add_dynamic-update-slice_fusion.7
  163.0 1.2 add_dynamic-update-slice_fusion.6
  164.2 1.2 add_dynamic-update-slice_fusion.5
  165.4 1.2 add_dynamic-update-slice_fusion.4
  166.6 1.2 add_dynamic-update-slice_fusion.3
  167.8 1.2 add_dynamic-update-slice_fusion.2
  169.0 1.2 add_dynamic-update-slice_fusion.1
  170.2 1.4 add_dynamic-update-slice_fusion.phase_ref
  171.6 25.1 %shard_map.59 = f32[8,10,16,16]{3,2,1,0:T(8,128)} custom-call(f32[8,80,1280]{2,1,0:T(8,128)} %add_dynamic-update-slice_fusion.phase_ref, bf16[512,512]{1,0:T(8,128)(2,1)} %pad_maximum_fusion.1.rhs1_ref, bf16[320,480]{1,0:T(8,128)(2,1)} %pad_maximum_fusion.2.lhs2_ref, bf16[256,16]{1,0:T(8,128)(2,1)} %copy.28.wk_ref), custom_call_target="tpu_custom_call" | custom-call | tf_op jit(solution)/shard_map/pallas_call | solution.py:106
  196.7 1.5 slice_divide_fusion.1
  198.2 0.1 copy.29
  198.3 0.1 div.29
  198.4 0.1 copy.30
  198.5 0.1 div.31
  198.7 1.1 copy.31
  199.8 0.2 copy.32
  200.0 21.9 %all-gather = bf16[16,4,1600]{2,1,0:T(4,128)(2,1)S(1)} all-gather(bf16[1,4,1600]{2,1,0:T(4,128)(2,1)S(1)} %copy.32), channel_id=1, replica_groups=mesh['wide'=16,'narrow'=16] {'wide'}, dimensions={0}, use_global_device_ids=true | all-gather | bytes 217600 | tf_op jit(solution)/shard_map/all_gather | solution.py:170
  221.9 0.1 reshape.257
  222.0 0.0 copy-done
  222.0 0.4 fusion.42
  222.4 0.7 reshape.255
  223.1 6.8 %all-to-all-start = ((f32[16,4,320]{2,1,0:T(4,128)}), f32[16,4,320]{2,1,0:T(4,128)S(1)}, u32[]{:S(2)}, u32[]{:S(2)}) async-start(f32[16,4,320]{2,1,0:T(4,128)} %reshape.255), calls=%async_computation | async-start | bytes 196608 | tf_op jit(solution)/shard_map/all_to_all | solution.py:175
  229.8 0.6 copy.33
  230.5 6.0 %all-to-all-done = f32[16,4,320]{2,1,0:T(4,128)S(1)} async-done(((f32[16,4,320]{2,1,0:T(4,128)}), f32[16,4,320]{2,1,0:T(4,128)S(1)}, u32[]{:S(2)}, u32[]{:S(2)}) %all-to-all-start) | async-done | bytes 81952 | tf_op jit(solution)/shard_map/all_to_all | solution.py:175
  236.5 0.6 reduce_sum.9
  (13 shorter events, 0.1 us)
Async XLA Ops:
  7.2 214.8 %copy-start = (bf16[1600,320]{0,1:T(8,128)(2,1)S(1)}, bf16[1600,320]{0,1:T(8,128)(2,1)}, u32[]{:S(2)}) copy-start(bf16[1600,320]{0,1:T(8,128)(2,1)} %param.7) | copy-start | bytes 3072004
  7.2 153.1 %all-reduce.2.cloned.1.call-start = ((), (), s32[]{:S(2)}) async-start(), calls=%async_computation.1 | async-start | bytes 3244032 | tf_op jit(solution)/shard_map/psum | solution.py:147
  32.3 1.5 copy-start.1
  116.6 2.0 copy-start.2
  223.1 13.4 %all-to-all-start = ((f32[16,4,320]{2,1,0:T(4,128)}), f32[16,4,320]{2,1,0:T(4,128)S(1)}, u32[]{:S(2)}, u32[]{:S(2)}) async-start(f32[16,4,320]{2,1,0:T(4,128)} %reshape.255), calls=%async_computation | async-start | bytes 196608 | tf_op jit(solution)/shard_map/all_to_all | solution.py:175
Sparse Core Ops, SparseCore 0:
  33.9 116.7 all-reduce.1

commit v8 on v7

--- a/solution.py
+++ b/solution.py
@@ -126,6 +126,7 @@
 
 def body(screens, offsets, valid, recon):
     narrow_count = lax.axis_size("narrow")
+    wide_count = lax.axis_size("wide")
     wide_index = lax.axis_index("wide")
     narrow_index = lax.axis_index("narrow")
     band_rows = screens.shape[1]
@@ -144,7 +145,14 @@
         group_start = lowest[0, which_layer] + pixel_rows * narrow_index
         row_at = jnp.clip(group_start - wide_index * band_rows + slab_rows, 0, band_rows + slab_rows)
         slabs.append(lax.dynamic_slice_in_dim(padded, row_at, slab_rows, 0))
-    slabs = lax.psum(jnp.stack(slabs), "wide")
+    chunks = jnp.stack(slabs).reshape(wide_count, L * slab_rows // wide_count, union_cols)
+    chunk = jnp.sum(lax.all_to_all(chunks, "wide", 0, 0), axis=0, dtype=chunks.dtype)
+    gathered = [chunk]
+    for shift in range(1, wide_count):
+        pairs = [(source, (source + shift) % wide_count) for source in range(wide_count)]
+        gathered.append(lax.ppermute(chunk, "wide", pairs))
+    order = (wide_index - jnp.arange(wide_count)) % wide_count
+    slabs = jnp.stack(gathered)[order].reshape(L, slab_rows, union_cols)
     rel = own_offsets - lowest[:, None, :]
     phases = []
     for item in range(local_items):

time: 246 us -> 309 us (1.26)
  starting transfers between devices: 6.8 us -> 59.9 us
  local copies, waits for them, and re-layouts: 19.9 us -> 41.8 us
  between operations: 144 us -> 130 us
  blocking collectives: 21.9 us -> 17.6 us
  waiting for transfers between devices: 6.05 us -> 10 us
    ppermute x0 -> x15, starting transfers between devices: none -> 43 us  [body(): gathered.append(lax.ppermute(chunk, 'wide', pairs))]
    all_to_all x0 -> x1, starting transfers between devices: none -> 10.1 us  [body(): lax.all_to_all(chunks, 'wide', 0, 0)]
    unnamed x9 -> x34, local copies, waits for them, and re-layouts: 0.95 us -> 10.8 us
    mul x6, local copies, waits for them, and re-layouts: 0.78 us -> 5.58 us  [block_diag(): eye[:, None, :, None] * block[None, :, None, :]]
    all_gather x1, blocking collectives: 21.9 us -> 17.6 us  [body(): lax.all_gather(slope_vector, 'wide', axis=0, tiled=True)]
    ppermute x0 -> x15, waiting for transfers between devices: none -> 3.99 us  [body(): gathered.append(lax.ppermute(chunk, 'wide', pairs))]
  transfers between devices with their start and end apart: 2 -> 17, of which waited for: 1 -> 4; matrix products, arithmetic and copies ran while one was open for 3% -> 8% of each run, Pallas kernels for 0% -> 0%
where the time goes in v8:
time: 309 us; the launch traced here: 306 us
  between operations  130 us (42%)
  starting transfers between devices  59.9 us (19%)
  local copies, waits for them, and re-layouts  41.8 us (14%)
  Pallas kernels  25.1 us (8%)
  other arithmetic  22 us (7%)
  blocking collectives  17.6 us (6%)
  waiting for transfers between devices  10 us (3%)
    ppermute x15, starting transfers between devices, body(): gathered.append(lax.ppermute(chunk, 'wide', pairs))  43 us
    pallas_call x1, Pallas kernels, centroids_kernel(): pl.pallas_call(centroid_kernel, grid=(items,), in_specs=[pl.BlockSpec((1,...  25.1 us
    all_gather x1, blocking collectives, body(): lax.all_gather(slope_vector, 'wide', axis=0, tiled=True)  17.6 us
    unnamed x34, local copies, waits for them, and re-layouts  10.8 us
    all_to_all x1, starting transfers between devices, body(): lax.all_to_all(chunks, 'wide', 0, 0)  10.1 us
    unnamed x7, other arithmetic  8.46 us
    all_to_all x1, starting transfers between devices, body(): commands = jnp.sum(lax.all_to_all(partial_commands, 'narrow', 0, 0), axis=0)  6.75 us
  transfers between devices with their start and end apart: 17, of which 4 were waited for; matrix products, arithmetic and copies ran while one was open for 8% of the time, Pallas kernels for 0%

profile of v8, /device:TPU:1, one launch (start us, length us, event | category | flops | bytes accessed | tf_op | source)
XLA Modules:
  0.0 306.3 jit_solution(10445286664905152200)
XLA Ops:
  0.6 0.9 reduce_min.9
  1.5 0.7 fusion.43
  7.1 6.1 %fusion.36 = (bf16[1,256,4096]{2,1,0:T(8,128)(2,1)}, bf16[1,256,4096]{2,1,0:T(8,128)(2,1)}, bf16[1,256,4096]{2,1,0:T(8,128)(2,1)}, bf16[1,256,4096]{2,1,0:T(8,128)(2,1)}) fusion(bf16[4,256,4096]{2,1,0:T(8,128)(2,1)} %param.4), kind=kLoop, calls=%fused_computation.112 | loop fusion | bytes 16777216 | tf_op jit(solution)/shard_map/slice | solution.py:143
  18.1 2.3 dynamic-slice_bitcast_fusion
  20.4 2.3 dynamic-slice_bitcast_fusion.2
  22.7 3.2 %fusion.12 = (bf16[1,144,1344]{2,1,0:T(8,128)(2,1)S(1)}, bf16[1,144,1344]{2,1,0:T(8,128)(2,1)S(1)}, bf16[1,144,1344]{2,1,0:T(8,128)(2,1)S(1)}, bf16[1,144,1344]{2,1,0:T(8,128)(2,1)S(1)}) fusion(s32[]{:T(128)S(6)} %min.13, bf16[144,1344]{1,0:T(8,128)(2,1)S(1)} %broadcast_in_dim.2, bf16[256,1344]{1,0:T(8,128)(2,1)S(1)} %get-tuple-element.113, s32[]{:T(128)S(6)} %min.15, ...), kind=kLoop, calls=%fused_computation.44 | loop fusion | flops 4644864 | bytes 4687888 | tf_op jit(solution)/shard_map/stack | solution.py:148
  26.2 1.5 reshape.283
  27.7 10.1 %all-to-all-start = ((bf16[16,36,1344]{2,1,0:T(8,128)(2,1)}), bf16[16,36,1344]{2,1,0:T(8,128)(2,1)S(1)}, u32[]{:S(2)}, u32[]{:S(2)}) async-start(bf16[16,36,1344]{2,1,0:T(8,128)(2,1)} %reshape.283), calls=%async_computation | async-start | bytes 3604480 | tf_op jit(solution)/shard_map/all_to_all | solution.py:149
  39.6 0.7 fusion.41
  71.4 0.7 fusion.40
  95.7 0.7 fusion.39
  120.1 1.0 broadcast_multiply_fusion
  121.0 1.2 mul.269
  122.3 0.7 neg.6
  123.0 0.8 mul.266
  124.0 0.8 mul.281
  124.8 1.0 copy.23
  126.4 0.7 mul.278
  127.2 1.0 copy.24
  128.5 0.7 copy.28.wk_ref
  168.8 1.0 reduce-precision_convert_fusion.1
  169.9 0.9 pad_maximum_fusion.2.lhs2_ref
  170.8 0.8 pad_maximum_fusion.1.rhs1_ref
  172.0 1.6 collective-permute-start
  174.3 1.2 collective-permute-start.1
  175.5 1.3 collective-permute-start.2
  176.8 2.4 collective-permute-start.3
  179.6 3.2 %collective-permute-start.5 = (bf16[36,1344]{1,0:T(8,128)(2,1)S(1)}, bf16[36,1344]{1,0:T(8,128)(2,1)S(1)}, u32[]{:S(2)}, u32[]{:S(2)}) collective-permute-start(bf16[36,1344]{1,0:T(8,128)(2,1)S(1)} %reduce_sum.18), channel_id=1, source_target_pairs={{0,96},{16,112},{32,128},{48,144},{64,160},{80,176},{96,192},{112,... | collective-permute-start | bytes 290312 | tf_op jit(solution)/shard_map/ppermute | solution.py:153
  183.5 2.5 collective-permute-start.6
  186.7 4.2 %collective-permute-start.7 = (bf16[36,1344]{1,0:T(8,128)(2,1)S(1)}, bf16[36,1344]{1,0:T(8,128)(2,1)S(1)}, u32[]{:S(2)}, u32[]{:S(2)}) collective-permute-start(bf16[36,1344]{1,0:T(8,128)(2,1)S(1)} %reduce_sum.18), channel_id=1, source_target_pairs={{0,128},{16,144},{32,160},{48,176},{64,192},{80,208},{96,224},{112... | collective-permute-start | bytes 290312 | tf_op jit(solution)/shard_map/ppermute | solution.py:153
  190.9 0.7 bitcast_dynamic-update-slice_fusion.20
  191.6 3.6 %collective-permute-start.8 = (bf16[36,1344]{1,0:T(8,128)(2,1)S(1)}, bf16[36,1344]{1,0:T(8,128)(2,1)S(1)}, u32[]{:S(2)}, u32[]{:S(2)}) collective-permute-start(bf16[36,1344]{1,0:T(8,128)(2,1)S(1)} %reduce_sum.18), channel_id=1, source_target_pairs={{0,144},{16,160},{32,176},{48,192},{64,208},{80,224},{96,240},{112... | collective-permute-start | bytes 290312 | tf_op jit(solution)/shard_map/ppermute | solution.py:153
  195.2 0.7 bitcast_dynamic-update-slice_fusion.19
  196.5 5.7 %collective-permute-start.9 = (bf16[36,1344]{1,0:T(8,128)(2,1)S(1)}, bf16[36,1344]{1,0:T(8,128)(2,1)S(1)}, u32[]{:S(2)}, u32[]{:S(2)}) collective-permute-start(bf16[36,1344]{1,0:T(8,128)(2,1)S(1)} %reduce_sum.18), channel_id=1, source_target_pairs={{0,160},{16,176},{32,192},{48,208},{64,224},{80,240},{96,0},{112,1... | collective-permute-start | bytes 290312 | tf_op jit(solution)/shard_map/ppermute | solution.py:153
  202.2 0.7 bitcast_dynamic-update-slice_fusion.18
  202.8 3.5 %collective-permute-start.10 = (bf16[36,1344]{1,0:T(8,128)(2,1)S(1)}, bf16[36,1344]{1,0:T(8,128)(2,1)S(1)}, u32[]{:S(2)}, u32[]{:S(2)}) collective-permute-start(bf16[36,1344]{1,0:T(8,128)(2,1)S(1)} %reduce_sum.18), channel_id=1, source_target_pairs={{0,176},{16,192},{32,208},{48,224},{64,240},{80,0},{96,16},{112,32... | collective-permute-start | bytes 290312 | tf_op jit(solution)/shard_map/ppermute | solution.py:153
  206.3 0.7 bitcast_dynamic-update-slice_fusion.17
  207.0 12.8 %collective-permute-start.11 = (bf16[36,1344]{1,0:T(8,128)(2,1)S(1)}, bf16[36,1344]{1,0:T(8,128)(2,1)S(1)}, u32[]{:S(2)}, u32[]{:S(2)}) collective-permute-start(bf16[36,1344]{1,0:T(8,128)(2,1)S(1)} %reduce_sum.18), channel_id=1, source_target_pairs={{0,192},{16,208},{32,224},{48,240},{64,0},{80,16},{96,32},{112,48}... | collective-permute-start | bytes 290312 | tf_op jit(solution)/shard_map/ppermute | solution.py:153
  219.8 0.7 bitcast_dynamic-update-slice_fusion.16
  222.2 0.7 bitcast_dynamic-update-slice_fusion.13
  222.8 0.7 bitcast_dynamic-update-slice_fusion.12
  223.5 0.7 bitcast_dynamic-update-slice_fusion.11
  224.2 2.4 collective-permute-done.12
  227.2 1.0 collective-permute-done.13
  228.2 0.7 bitcast_dynamic-update-slice_fusion.9
  229.5 2.3 gather_fusion
  231.8 1.1 fusion.37
  233.0 1.2 squeeze.268
  234.2 1.1 squeeze.271
  235.6 1.2 bitcast_dynamic-update-slice_fusion.7
  236.8 1.2 bitcast_dynamic-update-slice_fusion.6
  238.0 1.2 bitcast_dynamic-update-slice_fusion.5
  239.2 1.2 bitcast_dynamic-update-slice_fusion.4
  240.4 1.2 bitcast_dynamic-update-slice_fusion.3
  241.6 1.2 bitcast_dynamic-update-slice_fusion.2
  242.8 1.2 bitcast_dynamic-update-slice_fusion.1
  244.0 1.2 bitcast_dynamic-update-slice_fusion.phase_ref
  245.2 25.1 %shard_map.59 = f32[8,10,16,16]{3,2,1,0:T(8,128)} custom-call(f32[8,80,1280]{2,1,0:T(8,128)} %bitcast_dynamic-update-slice_fusion.phase_ref, bf16[512,512]{1,0:T(8,128)(2,1)} %pad_maximum_fusion.1.rhs1_ref, bf16[320,480]{1,0:T(8,128)(2,1)} %pad_maximum_fusion.2.lhs2_ref, bf16[256,16]{1,0:T(8,128)(2,1)} %copy.28.wk_ref), custom_call_target="tpu_custom_call" | custom-call | tf_op jit(solution)/shard_map/pallas_call | solution.py:106
  270.3 1.4 slice_divide_fusion.1
  272.2 1.1 copy.31
  273.5 17.6 %all-gather = bf16[16,4,1600]{2,1,0:T(4,128)(2,1)S(1)} all-gather(bf16[1,4,1600]{2,1,0:T(4,128)(2,1)S(1)} %copy.32), channel_id=1, replica_groups=mesh['wide'=16,'narrow'=16] {'wide'}, dimensions={0}, use_global_device_ids=true | all-gather | bytes 217600 | tf_op jit(solution)/shard_map/all_gather | solution.py:178
  291.6 0.7 reshape.285
  292.3 6.8 %all-to-all-start.1 = ((f32[16,4,320]{2,1,0:T(4,128)}), f32[16,4,320]{2,1,0:T(4,128)S(1)}, u32[]{:S(2)}, u32[]{:S(2)}) async-start(f32[16,4,320]{2,1,0:T(4,128)} %reshape.285), calls=%async_computation.1 | async-start | bytes 196608 | tf_op jit(solution)/shard_map/all_to_all | solution.py:183
  299.7 6.0 %all-to-all-done.1 = f32[16,4,320]{2,1,0:T(4,128)S(1)} async-done(((f32[16,4,320]{2,1,0:T(4,128)}), f32[16,4,320]{2,1,0:T(4,128)S(1)}, u32[]{:S(2)}, u32[]{:S(2)}) %all-to-all-start.1) | async-done | bytes 81952 | tf_op jit(solution)/shard_map/all_to_all | solution.py:183
  (77 shorter events, 11.3 us)
Async XLA Ops:
  0.6 290.6 %copy-start = (bf16[1600,320]{0,1:T(8,128)(2,1)S(1)}, bf16[1600,320]{0,1:T(8,128)(2,1)}, u32[]{:S(2)}) copy-start(bf16[1600,320]{0,1:T(8,128)(2,1)} %param.7) | copy-start | bytes 3072004
  27.7 10.1 %copy-start.6 = (s32[2,128,4]{1,2,0:T(4,128)S(1)}, s32[2,128,4]{1,2,0:T(4,128)}, u32[]{:S(2)}) copy-start(s32[2,128,4]{1,2,0:T(4,128)} %param.5) | copy-start | bytes 12292
  27.7 144.0 %all-to-all-start = ((bf16[16,36,1344]{2,1,0:T(8,128)(2,1)}), bf16[16,36,1344]{2,1,0:T(8,128)(2,1)S(1)}, u32[]{:S(2)}, u32[]{:S(2)}) async-start(bf16[16,36,1344]{2,1,0:T(8,128)(2,1)} %reshape.283), calls=%async_computation | async-start | bytes 3604480 | tf_op jit(solution)/shard_map/all_to_all | solution.py:149
  121.0 8.1 %copy-start.7 = (s32[2,5,80]{2,0,1:T(2,128)S(1)}, s32[2,5,80]{2,0,1:T(2,128)}, u32[]{:S(2)}) copy-start(s32[2,5,80]{2,0,1:T(2,128)} %param.6) | copy-start | bytes 9604
  122.3 1.6 copy-start.2
  124.8 46.0 %copy-start.3 = (f32[128,256]{1,0:T(8,128)S(1)}, f32[128,256]{1,0:T(8,128)}, u32[]{:S(2)}) copy-start(f32[128,256]{1,0:T(8,128)} %copy-done.2) | copy-start | bytes 393220
  124.8 46.0 %copy-start.4 = (f32[128,256]{1,0:T(8,128)S(1)}, f32[128,256]{1,0:T(8,128)}, u32[]{:S(2)}) copy-start(f32[128,256]{1,0:T(8,128)} %mul.266) | copy-start | bytes 393220
  127.2 43.6 %copy-start.5 = (f32[128,256]{1,0:T(8,128)S(1)}, f32[128,256]{1,0:T(8,128)}, u32[]{:S(2)}) copy-start(f32[128,256]{1,0:T(8,128)} %neg.6) | copy-start | bytes 393220
  172.0 7.7 %collective-permute-start = (bf16[36,1344]{1,0:T(8,128)(2,1)S(1)}, bf16[36,1344]{1,0:T(8,128)(2,1)S(1)}, u32[]{:S(2)}, u32[]{:S(2)}) collective-permute-start(bf16[36,1344]{1,0:T(8,128)(2,1)S(1)} %reduce_sum.18), channel_id=1, source_target_pairs={{0,16},{16,32},{32,48},{48,64},{64,80},{80,96},{96,112},{112,128},... | collective-permute-start | bytes 290312 | tf_op jit(solution)/shard_map/ppermute | solution.py:153
  174.3 9.2 %collective-permute-start.1 = (bf16[36,1344]{1,0:T(8,128)(2,1)S(1)}, bf16[36,1344]{1,0:T(8,128)(2,1)S(1)}, u32[]{:S(2)}, u32[]{:S(2)}) collective-permute-start(bf16[36,1344]{1,0:T(8,128)(2,1)S(1)} %reduce_sum.18), channel_id=1, source_target_pairs={{0,32},{16,48},{32,64},{48,80},{64,96},{80,112},{96,128},{112,144}... | collective-permute-start | bytes 290312 | tf_op jit(solution)/shard_map/ppermute | solution.py:153
  175.5 11.3 %collective-permute-start.2 = (bf16[36,1344]{1,0:T(8,128)(2,1)S(1)}, bf16[36,1344]{1,0:T(8,128)(2,1)S(1)}, u32[]{:S(2)}, u32[]{:S(2)}) collective-permute-start(bf16[36,1344]{1,0:T(8,128)(2,1)S(1)} %reduce_sum.18), channel_id=1, source_target_pairs={{0,48},{16,64},{32,80},{48,96},{64,112},{80,128},{96,144},{112,160... | collective-permute-start | bytes 290312 | tf_op jit(solution)/shard_map/ppermute | solution.py:153
  176.8 14.8 %collective-permute-start.3 = (bf16[36,1344]{1,0:T(8,128)(2,1)S(1)}, bf16[36,1344]{1,0:T(8,128)(2,1)S(1)}, u32[]{:S(2)}, u32[]{:S(2)}) collective-permute-start(bf16[36,1344]{1,0:T(8,128)(2,1)S(1)} %reduce_sum.18), channel_id=1, source_target_pairs={{0,64},{16,80},{32,96},{48,112},{64,128},{80,144},{96,160},{112,17... | collective-permute-start | bytes 290312 | tf_op jit(solution)/shard_map/ppermute | solution.py:153
  179.2 17.3 %collective-permute-start.4 = (bf16[36,1344]{1,0:T(8,128)(2,1)S(1)}, bf16[36,1344]{1,0:T(8,128)(2,1)S(1)}, u32[]{:S(2)}, u32[]{:S(2)}) collective-permute-start(bf16[36,1344]{1,0:T(8,128)(2,1)S(1)} %reduce_sum.18), channel_id=1, source_target_pairs={{0,80},{16,96},{32,112},{48,128},{64,144},{80,160},{96,176},{112,1... | collective-permute-start | bytes 290312 | tf_op jit(solution)/shard_map/ppermute | solution.py:153
  179.6 23.2 %collective-permute-start.5 = (bf16[36,1344]{1,0:T(8,128)(2,1)S(1)}, bf16[36,1344]{1,0:T(8,128)(2,1)S(1)}, u32[]{:S(2)}, u32[]{:S(2)}) collective-permute-start(bf16[36,1344]{1,0:T(8,128)(2,1)S(1)} %reduce_sum.18), channel_id=1, source_target_pairs={{0,96},{16,112},{32,128},{48,144},{64,160},{80,176},{96,192},{112,... | collective-permute-start | bytes 290312 | tf_op jit(solution)/shard_map/ppermute | solution.py:153
  183.5 23.5 %collective-permute-start.6 = (bf16[36,1344]{1,0:T(8,128)(2,1)S(1)}, bf16[36,1344]{1,0:T(8,128)(2,1)S(1)}, u32[]{:S(2)}, u32[]{:S(2)}) collective-permute-start(bf16[36,1344]{1,0:T(8,128)(2,1)S(1)} %reduce_sum.18), channel_id=1, source_target_pairs={{0,112},{16,128},{32,144},{48,160},{64,176},{80,192},{96,208},{112... | collective-permute-start | bytes 290312 | tf_op jit(solution)/shard_map/ppermute | solution.py:153
  186.7 33.7 %collective-permute-start.7 = (bf16[36,1344]{1,0:T(8,128)(2,1)S(1)}, bf16[36,1344]{1,0:T(8,128)(2,1)S(1)}, u32[]{:S(2)}, u32[]{:S(2)}) collective-permute-start(bf16[36,1344]{1,0:T(8,128)(2,1)S(1)} %reduce_sum.18), channel_id=1, source_target_pairs={{0,128},{16,144},{32,160},{48,176},{64,192},{80,208},{96,224},{112... | collective-permute-start | bytes 290312 | tf_op jit(solution)/shard_map/ppermute | solution.py:153
  191.6 29.5 %collective-permute-start.8 = (bf16[36,1344]{1,0:T(8,128)(2,1)S(1)}, bf16[36,1344]{1,0:T(8,128)(2,1)S(1)}, u32[]{:S(2)}, u32[]{:S(2)}) collective-permute-start(bf16[36,1344]{1,0:T(8,128)(2,1)S(1)} %reduce_sum.18), channel_id=1, source_target_pairs={{0,144},{16,160},{32,176},{48,192},{64,208},{80,224},{96,240},{112... | collective-permute-start | bytes 290312 | tf_op jit(solution)/shard_map/ppermute | solution.py:153
  196.5 25.3 %collective-permute-start.9 = (bf16[36,1344]{1,0:T(8,128)(2,1)S(1)}, bf16[36,1344]{1,0:T(8,128)(2,1)S(1)}, u32[]{:S(2)}, u32[]{:S(2)}) collective-permute-start(bf16[36,1344]{1,0:T(8,128)(2,1)S(1)} %reduce_sum.18), channel_id=1, source_target_pairs={{0,160},{16,176},{32,192},{48,208},{64,224},{80,240},{96,0},{112,1... | collective-permute-start | bytes 290312 | tf_op jit(solution)/shard_map/ppermute | solution.py:153
  202.8 20.0 %collective-permute-start.10 = (bf16[36,1344]{1,0:T(8,128)(2,1)S(1)}, bf16[36,1344]{1,0:T(8,128)(2,1)S(1)}, u32[]{:S(2)}, u32[]{:S(2)}) collective-permute-start(bf16[36,1344]{1,0:T(8,128)(2,1)S(1)} %reduce_sum.18), channel_id=1, source_target_pairs={{0,176},{16,192},{32,208},{48,224},{64,240},{80,0},{96,16},{112,32... | collective-permute-start | bytes 290312 | tf_op jit(solution)/shard_map/ppermute | solution.py:153
  207.0 16.5 %collective-permute-start.11 = (bf16[36,1344]{1,0:T(8,128)(2,1)S(1)}, bf16[36,1344]{1,0:T(8,128)(2,1)S(1)}, u32[]{:S(2)}, u32[]{:S(2)}) collective-permute-start(bf16[36,1344]{1,0:T(8,128)(2,1)S(1)} %reduce_sum.18), channel_id=1, source_target_pairs={{0,192},{16,208},{32,224},{48,240},{64,0},{80,16},{96,32},{112,48}... | collective-permute-start | bytes 290312 | tf_op jit(solution)/shard_map/ppermute | solution.py:153
  220.5 6.1 %collective-permute-start.12 = (bf16[36,1344]{1,0:T(8,128)(2,1)S(1)}, bf16[36,1344]{1,0:T(8,128)(2,1)S(1)}, u32[]{:S(2)}, u32[]{:S(2)}) collective-permute-start(bf16[36,1344]{1,0:T(8,128)(2,1)S(1)} %reduce_sum.18), channel_id=1, source_target_pairs={{0,208},{16,224},{32,240},{48,0},{64,16},{80,32},{96,48},{112,64},... | collective-permute-start | bytes 290312 | tf_op jit(solution)/shard_map/ppermute | solution.py:153
  221.1 7.1 %collective-permute-start.13 = (bf16[36,1344]{1,0:T(8,128)(2,1)S(1)}, bf16[36,1344]{1,0:T(8,128)(2,1)S(1)}, u32[]{:S(2)}, u32[]{:S(2)}) collective-permute-start(bf16[36,1344]{1,0:T(8,128)(2,1)S(1)} %reduce_sum.18), channel_id=1, source_target_pairs={{0,224},{16,240},{32,0},{48,16},{64,32},{80,48},{96,64},{112,80},{... | collective-permute-start | bytes 290312 | tf_op jit(solution)/shard_map/ppermute | solution.py:153
  221.8 7.1 %collective-permute-start.14 = (bf16[36,1344]{1,0:T(8,128)(2,1)S(1)}, bf16[36,1344]{1,0:T(8,128)(2,1)S(1)}, u32[]{:S(2)}, u32[]{:S(2)}) collective-permute-start(bf16[36,1344]{1,0:T(8,128)(2,1)S(1)} %reduce_sum.18), channel_id=1, source_target_pairs={{0,240},{16,0},{32,16},{48,32},{64,48},{80,64},{96,80},{112,96},{1... | collective-permute-start | bytes 290312 | tf_op jit(solution)/shard_map/ppermute | solution.py:153
  233.0 2.3 copy-start.1
  292.3 13.4 %all-to-all-start.1 = ((f32[16,4,320]{2,1,0:T(4,128)}), f32[16,4,320]{2,1,0:T(4,128)S(1)}, u32[]{:S(2)}, u32[]{:S(2)}) async-start(f32[16,4,320]{2,1,0:T(4,128)} %reshape.285), calls=%async_computation.1 | async-start | bytes 196608 | tf_op jit(solution)/shard_map/all_to_all | solution.py:183

commit v9 on v7

--- a/solution.py
+++ b/solution.py
@@ -139,7 +139,9 @@
     pad = jnp.zeros((slab_rows, union_cols), screens.dtype)
     slabs = []
     for which_layer in range(L):
-        band = lax.dynamic_slice_in_dim(screens[which_layer], lowest[1, which_layer], union_cols, 1)
+        band = lax.dynamic_slice(
+            screens, (which_layer, 0, lowest[1, which_layer]), (1, band_rows, union_cols)
+        )[0]
         padded = jnp.concatenate([pad, band, pad], axis=0)
         group_start = lowest[0, which_layer] + pixel_rows * narrow_index
         row_at = jnp.clip(group_start - wide_index * band_rows + slab_rows, 0, band_rows + slab_rows)

time: 246 us -> 239 us (0.972)
  local copies, waits for them, and re-layouts: 19.9 us -> 13.2 us
    slice x1 -> x0, local copies, waits for them, and re-layouts: 5.64 us -> none  [body(): screens[which_layer]]
    dynamic_slice x2 -> x0, local copies, waits for them, and re-layouts: 4.32 us -> none  [body(): lax.dynamic_slice_in_dim(screens[which_layer], lowest[1, which_layer], un...]
    squeeze x0 -> x1, local copies, waits for them, and re-layouts: none -> 3.27 us  [body(): lax.dynamic_slice(screens, (which_layer, 0, lowest[1, which_layer]), (1,...]
where the time goes in v9:
time: 239 us; the launch traced here: 237 us
  between operations  143 us (60%)
  Pallas kernels  25 us (10%)
  blocking collectives  21.9 us (9%)
  other arithmetic  20 us (8%)
  local copies, waits for them, and re-layouts  13.2 us (6%)
  starting transfers between devices  6.78 us (3%)
  waiting for transfers between devices  6.05 us (3%)
    pallas_call x1, Pallas kernels, centroids_kernel(): pl.pallas_call(centroid_kernel, grid=(items,), in_specs=[pl.BlockSpec((1,...  25 us
    all_gather x1, blocking collectives, body(): lax.all_gather(slope_vector, 'wide', axis=0, tiled=True)  21.9 us
    unnamed x7, other arithmetic  8.45 us
    all_to_all x1, starting transfers between devices, body(): commands = jnp.sum(lax.all_to_all(partial_commands, 'narrow', 0, 0), axis=0)  6.74 us
    all_to_all x1, waiting for transfers between devices, body(): commands = jnp.sum(lax.all_to_all(partial_commands, 'narrow', 0, 0), axis=0)  6.03 us
  transfers between devices with their start and end apart: 2, of which 1 were waited for; matrix products, arithmetic and copies ran while one was open for 3% of the time, Pallas kernels for 0%

profile of v9, /device:TPU:1, one launch (start us, length us, event | category | flops | bytes accessed | tf_op | source)
XLA Modules:
  0.0 236.6 jit_solution(12864889653485733324)
XLA Ops:
  7.2 0.0 copy-start
  7.2 0.0 all-reduce.2.cloned.1.call-start
  7.2 0.9 reduce_min.9
  8.1 0.7 fusion.40
  18.9 3.3 %dynamic-slice_bitcast_fusion.3 = (bf16[256,1344]{1,0:T(8,128)(2,1)S(1)}, bf16[256,1344]{1,0:T(8,128)(2,1)S(1)}, bf16[256,1344]{1,0:T(8,128)(2,1)S(1)}, bf16[256,1344]{1,0:T(8,128)(2,1)S(1)}) fusion(bf16[4,256,4096]{2,1,0:T(8,128)(2,1)} %param.4, s32[]{:T(128)S(6)} %select_n.248, s32[]{:T(128)S(6)} %select_n.249, s32[]{:T(128)S(6)} %select_n.251, ...), kind=kLoop, calls=%fused_computation.18 | loop fusion | bytes 5505040 | tf_op jit(solution)/shard_map/squeeze | solution.py:142
  22.2 3.2 %fusion.12 = (bf16[1,144,1344]{2,1,0:T(8,128)(2,1)S(1)}, bf16[1,144,1344]{2,1,0:T(8,128)(2,1)S(1)}, bf16[1,144,1344]{2,1,0:T(8,128)(2,1)S(1)}, bf16[1,144,1344]{2,1,0:T(8,128)(2,1)S(1)}) fusion(s32[]{:T(128)S(6)} %min.13, bf16[144,1344]{1,0:T(8,128)(2,1)S(1)} %broadcast_in_dim.2, bf16[256,1344]{1,0:T(8,128)(2,1)S(1)} %get-tuple-element.8, s32[]{:T(128)S(6)} %min.15, ...), kind=kLoop, calls=%fused_computation.43 | loop fusion | flops 4644864 | bytes 4687888 | tf_op jit(solution)/shard_map/stack | solution.py:149
  25.4 0.0 copy-start.1
  25.4 1.4 pad_maximum_fusion
  26.9 0.0 copy-start.2
  26.9 0.0 all-reduce.2.cloned.1.call-update
  26.9 0.0 copy-done.1
  26.9 0.1 fusion.26
  27.0 0.7 fusion.38
  27.7 0.6 fusion.39
  60.4 0.7 fusion.37
  84.8 0.7 fusion.36
  109.1 0.1 fusion.29
  109.1 0.1 fusion.27
  109.2 0.1 copy.27
  109.3 0.2 broadcast_multiply_fusion
  109.5 0.2 mul.269
  109.7 0.2 mul.266
  109.9 0.1 broadcast_multiply_fusion.2
  110.0 0.1 mul.281
  110.1 0.1 copy.23
  110.2 0.1 mul.278
  110.3 0.1 copy.24
  110.4 0.1 mul.282
  110.5 0.1 reshape.250
  110.6 0.1 mul.284
  110.7 0.7 copy.28.wk_ref
  111.4 0.0 copy-done.2
  151.0 0.2 reduce-precision_convert_fusion.1
  151.2 0.9 pad_maximum_fusion.2.lhs2_ref
  152.1 0.1 reduce-precision_convert_fusion
  152.2 0.8 pad_maximum_fusion.1.rhs1_ref
  153.0 0.0 all-reduce.2.cloned.1.call-done
  153.0 1.5 fusion.34
  154.5 1.2 add_dynamic-update-slice_fusion.7
  155.7 1.2 add_dynamic-update-slice_fusion.6
  156.9 1.2 add_dynamic-update-slice_fusion.5
  158.1 1.2 add_dynamic-update-slice_fusion.4
  159.3 1.2 add_dynamic-update-slice_fusion.3
  160.5 1.2 add_dynamic-update-slice_fusion.2
  161.7 1.2 add_dynamic-update-slice_fusion.1
  162.9 1.4 add_dynamic-update-slice_fusion.phase_ref
  164.3 25.0 %shard_map.59 = f32[8,10,16,16]{3,2,1,0:T(8,128)} custom-call(f32[8,80,1280]{2,1,0:T(8,128)} %add_dynamic-update-slice_fusion.phase_ref, bf16[512,512]{1,0:T(8,128)(2,1)} %pad_maximum_fusion.1.rhs1_ref, bf16[320,480]{1,0:T(8,128)(2,1)} %pad_maximum_fusion.2.lhs2_ref, bf16[256,16]{1,0:T(8,128)(2,1)} %copy.28.wk_ref), custom_call_target="tpu_custom_call" | custom-call | tf_op jit(solution)/shard_map/pallas_call | solution.py:106
  189.4 1.5 slice_divide_fusion.1
  190.9 0.1 copy.29
  191.0 0.1 div.29
  191.1 0.1 copy.30
  191.2 0.1 div.31
  191.3 1.1 copy.31
  192.4 0.2 copy.32
  192.6 21.9 %all-gather = bf16[16,4,1600]{2,1,0:T(4,128)(2,1)S(1)} all-gather(bf16[1,4,1600]{2,1,0:T(4,128)(2,1)S(1)} %copy.32), channel_id=1, replica_groups=mesh['wide'=16,'narrow'=16] {'wide'}, dimensions={0}, use_global_device_ids=true | all-gather | bytes 217600 | tf_op jit(solution)/shard_map/all_gather | solution.py:172
  214.5 0.1 reshape.253
  214.6 0.0 copy-done
  214.6 0.4 fusion.41
  215.1 0.7 reshape.251
  215.7 6.7 %all-to-all-start = ((f32[16,4,320]{2,1,0:T(4,128)}), f32[16,4,320]{2,1,0:T(4,128)S(1)}, u32[]{:S(2)}, u32[]{:S(2)}) async-start(f32[16,4,320]{2,1,0:T(4,128)} %reshape.251), calls=%async_computation | async-start | bytes 196608 | tf_op jit(solution)/shard_map/all_to_all | solution.py:177
  222.5 0.6 copy.33
  223.1 6.0 %all-to-all-done = f32[16,4,320]{2,1,0:T(4,128)S(1)} async-done(((f32[16,4,320]{2,1,0:T(4,128)}), f32[16,4,320]{2,1,0:T(4,128)S(1)}, u32[]{:S(2)}, u32[]{:S(2)}) %all-to-all-start) | async-done | bytes 81952 | tf_op jit(solution)/shard_map/all_to_all | solution.py:177
  229.2 0.6 reduce_sum.9
  (12 shorter events, 0.1 us)
Async XLA Ops:
  7.2 207.5 %copy-start = (bf16[1600,320]{0,1:T(8,128)(2,1)S(1)}, bf16[1600,320]{0,1:T(8,128)(2,1)}, u32[]{:S(2)}) copy-start(bf16[1600,320]{0,1:T(8,128)(2,1)} %param.7) | copy-start | bytes 3072004
  7.2 145.8 %all-reduce.2.cloned.1.call-start = ((), (), s32[]{:S(2)}) async-start(), calls=%async_computation.1 | async-start | bytes 3244032 | tf_op jit(solution)/shard_map/psum | solution.py:149
  25.4 1.5 copy-start.1
  26.9 84.5 %copy-start.2 = (s32[2,5,80]{2,0,1:T(2,128)S(1)}, s32[2,5,80]{2,0,1:T(2,128)}, u32[]{:S(2)}) copy-start(s32[2,5,80]{2,0,1:T(2,128)} %param.6) | copy-start | bytes 9604
  215.7 13.4 %all-to-all-start = ((f32[16,4,320]{2,1,0:T(4,128)}), f32[16,4,320]{2,1,0:T(4,128)S(1)}, u32[]{:S(2)}, u32[]{:S(2)}) async-start(f32[16,4,320]{2,1,0:T(4,128)} %reshape.251), calls=%async_computation | async-start | bytes 196608 | tf_op jit(solution)/shard_map/all_to_all | solution.py:177
Sparse Core Ops, SparseCore 0:
  27.0 116.7 all-reduce.1

commit v10 on v9

--- a/solution.py
+++ b/solution.py
@@ -60,8 +60,20 @@
     return rhs1, lhs2, wk.astype(bf16)
 
 
-def centroid_kernel(phase_ref, rhs1_ref, lhs2_ref, wk_ref, out_ref, acc_ref):
-    ph = phase_ref[0]
+def centroid_kernel(rel_ref, slab_ref, rhs1_ref, lhs2_ref, wk_ref, out_ref, acc_ref):
+    item = pl.program_id(0)
+    items = pl.num_programs(0)
+    layers, slab_rows, width = slab_ref.shape
+    rows = slab_rows - SPREAD - 8
+    ph = jnp.zeros((rows, PUP), f32)
+    for which_layer in range(layers):
+        row_at = rel_ref[item * layers + which_layer]
+        col_at = rel_ref[(items + item) * layers + which_layer]
+        base = pl.multiple_of((row_at // 8) * 8, 8)
+        window = slab_ref[which_layer, pl.ds(base, rows + 8), :]
+        window = pltpu.roll(window, (rows + 8 - (row_at - base)) % (rows + 8), 0)
+        window = pltpu.roll(window, (width - col_at) % width, 1)
+        ph = ph + window[:rows, :PUP]
     fc = jnp.cos(ph).astype(bf16)
     fs = jnp.sin(ph).astype(bf16)
     rhs1 = rhs1_ref[...]
@@ -99,23 +111,28 @@
     out_ref[0] = q.reshape(groups, acc_ref.shape[1], wk.shape[1])
 
 
-def centroids_kernel(phase, sub_rows):
-    items, rows, cols = phase.shape
-    groups = cols // LANES
+def centroids_kernel(slabs, rel, sub_rows, items):
+    rows = sub_rows * SAMP
+    groups = PUP // LANES
+    width = -(-slabs.shape[2] // LANES) * LANES
+    slabs = jnp.pad(slabs.astype(f32), ((0, 0), (0, 8), (0, width - slabs.shape[2])))
     rhs1, lhs2, wk = dft_operands(sub_rows)
     sums = pl.pallas_call(
         centroid_kernel,
-        grid=(items,),
-        in_specs=[
-            pl.BlockSpec((1, rows, cols), lambda i: (i, 0, 0)),
-            pl.BlockSpec(rhs1.shape, lambda i: (0, 0)),
-            pl.BlockSpec(lhs2.shape, lambda i: (0, 0)),
-            pl.BlockSpec(wk.shape, lambda i: (0, 0)),
-        ],
-        out_specs=pl.BlockSpec((1, groups, 16, 16), lambda i: (i, 0, 0, 0)),
+        grid_spec=pltpu.PrefetchScalarGridSpec(
+            num_scalar_prefetch=1,
+            grid=(items,),
+            in_specs=[
+                pl.BlockSpec(slabs.shape, lambda i, r: (0, 0, 0)),
+                pl.BlockSpec(rhs1.shape, lambda i, r: (0, 0)),
+                pl.BlockSpec(lhs2.shape, lambda i, r: (0, 0)),
+                pl.BlockSpec(wk.shape, lambda i, r: (0, 0)),
+            ],
+            out_specs=pl.BlockSpec((1, groups, 16, 16), lambda i, r: (i, 0, 0, 0)),
+            scratch_shapes=[pltpu.VMEM((groups, 16, rhs1.shape[1] // 2), f32)],
+        ),
         out_shape=jax.ShapeDtypeStruct((items, groups, 16, 16), f32),
-        scratch_shapes=[pltpu.VMEM((groups, 16, rhs1.shape[1] // 2), f32)],
-    )(phase, rhs1, lhs2, wk)
+    )(rel.reshape(-1), slabs, rhs1, lhs2, wk)
     lane_subs = LANES // SAMP
     sums = sums.transpose(0, 2, 1, 3)
     flux = sums[:, :sub_rows, :, :lane_subs].reshape(items, sub_rows, -1)
@@ -148,17 +165,7 @@
         slabs.append(lax.dynamic_slice_in_dim(padded, row_at, slab_rows, 0))
     slabs = lax.psum(jnp.stack(slabs), "wide")
     rel = own_offsets - lowest[:, None, :]
-    phases = []
-    for item in range(local_items):
-        acc = jnp.zeros((pixel_rows, PUP), jnp.float32)
-        for which_layer in range(L):
-            window = lax.dynamic_slice(
-                slabs[which_layer], (rel[0, item, which_layer], rel[1, item, which_layer]), (pixel_rows, PUP)
-            )
-            acc = acc + window.astype(jnp.float32)
-        phases.append(acc)
-    pupil_phase = jnp.stack(phases)
-    measured = centroids_kernel(pupil_phase, sub_rows)
+    measured = centroids_kernel(slabs, rel, sub_rows, local_items)
     measured = measured.reshape(FR_DEV, NSENS, sub_rows, NSUB, 2) * valid[None, :, :, :, None].astype(
         jnp.float32
     )

time: 239 us -> 225 us (0.941)
  between operations: 143 us -> 24.2 us
  waiting for transfers between devices: 6.05 us -> 118 us
  Pallas kernels: 25 us -> 36.3 us
  other arithmetic: 20 us -> 13.6 us
  blocking collectives: 21.9 us -> 16 us
  local copies, waits for them, and re-layouts: 13.2 us -> 9.56 us
    psum x1, waiting for transfers between devices: 0.01 us -> 112 us  [body(): slabs = lax.psum(jnp.stack(slabs), 'wide')]
    pallas_call x1, Pallas kernels: 25 us -> 36.3 us  [centroids_kernel(): pl.pallas_call(centroid_kernel, grid_spec=pltpu.PrefetchScalarGridSpec(nu...]
    unnamed x7 -> x0, other arithmetic: 8.45 us -> none
    all_gather x1, blocking collectives: 21.9 us -> 16 us  [body(): lax.all_gather(slope_vector, 'wide', axis=0, tiled=True)]
    slice x5 -> x0, local copies, waits for them, and re-layouts: 4.29 us -> none  [the longest x4 2.81 us: body(): rel[1, item, which_layer]]
    pad x0 -> x1, other arithmetic: none -> 3.38 us  [centroids_kernel(): jnp.pad(slabs.astype(f32), ((0, 0), (0, 8), (0, width - slabs.shape[2])))]
  transfers between devices with their start and end apart: 2 -> 2, of which waited for: 1 -> 2; matrix products, arithmetic and copies ran while one was open for 3% -> 3% of each run, Pallas kernels for 0% -> 0%
where the time goes in v10:
time: 225 us; the launch traced here: 224 us
  waiting for transfers between devices  118 us (52%)
  Pallas kernels  36.3 us (16%)
  between operations  24.2 us (11%)
  blocking collectives  16 us (7%)
  other arithmetic  13.6 us (6%)
  local copies, waits for them, and re-layouts  9.56 us (4%)
  starting transfers between devices  6.57 us (3%)
    psum x1, waiting for transfers between devices, body(): slabs = lax.psum(jnp.stack(slabs), 'wide')  112 us
    pallas_call x1, Pallas kernels, centroids_kernel(): pl.pallas_call(centroid_kernel, grid_spec=pltpu.PrefetchScalarGridSpec(nu...  36.3 us
    all_gather x1, blocking collectives, body(): lax.all_gather(slope_vector, 'wide', axis=0, tiled=True)  16 us
    all_to_all x1, starting transfers between devices, body(): commands = jnp.sum(lax.all_to_all(partial_commands, 'narrow', 0, 0), axis=0)  6.53 us
    all_to_all x1, waiting for transfers between devices, body(): commands = jnp.sum(lax.all_to_all(partial_commands, 'narrow', 0, 0), axis=0)  6.03 us
    another operation x2, other arithmetic, body(): slabs = lax.psum(jnp.stack(slabs), 'wide')  4.66 us
  transfers between devices with their start and end apart: 2, of which 2 were waited for; matrix products, arithmetic and copies ran while one was open for 3% of the time, Pallas kernels for 0%

profile of v10, /device:TPU:1, one launch (start us, length us, event | category | flops | bytes accessed | tf_op | source)
XLA Modules:
  0.0 224.4 jit_solution(9529648651846710270)
XLA Ops:
  7.2 0.0 copy-start
  7.2 0.0 all-reduce.3.cloned.1.call-start
  7.2 0.9 reduce_min.9
  8.1 0.7 fusion.35
  18.7 3.3 %dynamic-slice_bitcast_fusion.3 = (bf16[256,1344]{1,0:T(8,128)(2,1)S(1)}, bf16[256,1344]{1,0:T(8,128)(2,1)S(1)}, bf16[256,1344]{1,0:T(8,128)(2,1)S(1)}, bf16[256,1344]{1,0:T(8,128)(2,1)S(1)}) fusion(bf16[4,256,4096]{2,1,0:T(8,128)(2,1)} %param.4, s32[]{:T(128)S(6)} %select_n.57, s32[]{:T(128)S(6)} %select_n.58, s32[]{:T(128)S(6)} %select_n.60, s32[]{:T(128)S(6)} %select_n.59), kind=kLoop, calls=%fused_computation.19 | loop fusion | bytes 5505040 | tf_op jit(solution)/shard_map/squeeze | solution.py:159
  22.0 3.2 %fusion.12 = (bf16[1,144,1344]{2,1,0:T(8,128)(2,1)S(1)}, bf16[1,144,1344]{2,1,0:T(8,128)(2,1)S(1)}, bf16[1,144,1344]{2,1,0:T(8,128)(2,1)S(1)}, bf16[1,144,1344]{2,1,0:T(8,128)(2,1)S(1)}) fusion(s32[]{:T(128)S(6)} %min.13, bf16[144,1344]{1,0:T(8,128)(2,1)S(1)} %broadcast_in_dim.2, bf16[256,1344]{1,0:T(8,128)(2,1)S(1)} %get-tuple-element.8, s32[]{:T(128)S(6)} %min.15, ...), kind=kLoop, calls=%fused_computation.36 | loop fusion | flops 4644864 | bytes 4687888 | tf_op jit(solution)/shard_map/stack | solution.py:166
  25.2 1.5 pad_maximum_fusion
  26.7 0.0 all-reduce.3.cloned.1.call-update
  26.7 0.1 fusion.29
  26.8 0.1 fusion.27
  26.9 0.1 copy.31
  27.0 0.2 broadcast_multiply_fusion
  27.1 0.2 mul.269
  27.3 0.0 copy-start.1
  27.3 0.0 copy-start.2
  27.3 0.2 mul.266
  27.5 0.1 broadcast_multiply_fusion.2
  27.7 0.1 mul.281
  27.8 0.1 copy.27
  27.9 0.1 mul.278
  28.0 0.1 copy.28
  28.1 0.0 copy-done.1
  28.1 0.1 fusion.26
  28.2 0.1 copy.26
  28.3 0.6 reshape.221.rel_ref
  28.9 0.1 mul.282
  28.9 0.1 reshape.222
  29.0 0.1 mul.284
  29.1 0.7 copy.32.wk_ref
  29.9 0.0 copy-done.2
  29.9 0.2 reduce-precision_convert_fusion.1
  30.0 0.9 pad_maximum_fusion.2.lhs2_ref
  31.0 0.1 reduce-precision_convert_fusion
  31.0 0.8 pad_maximum_fusion.1.rhs1_ref
  31.9 111.7 %all-reduce.3.cloned.1.call-done = bf16[4,144,1344]{2,1,0:T(8,128)(2,1)} async-done(((bf16[4,144,1344]{2,1,0:T(8,128)(2,1)}), bf16[4,144,1344]{2,1,0:T(8,128)(2,1)}) %all-reduce.3.cloned.1.call-update) | async-done | bytes 1548304 | tf_op jit(solution)/shard_map/psum | solution.py:166
  143.5 3.4 %pad_convert_fusion.slab_ref = f32[4,152,1408]{2,1,0:T(8,128)} fusion(bf16[4,144,1344]{2,1,0:T(8,128)(2,1)} %all-reduce.3.cloned.1.call-done), kind=kLoop, calls=%fused_computation.8 | loop fusion | flops 856064 | bytes 4972544 | tf_op jit(solution)/shard_map/jit(_pad)/pad | solution.py:118
  146.9 36.3 %shard_map.59 = f32[8,10,16,16]{3,2,1,0:T(8,128)} custom-call(s32[64]{0:T(128)} %reshape.221.rel_ref, f32[4,152,1408]{2,1,0:T(8,128)} %pad_convert_fusion.slab_ref, bf16[512,512]{1,0:T(8,128)(2,1)} %pad_maximum_fusion.1.rhs1_ref, bf16[320,480]{1,0:T(8,128)(2,1)} %pad_maximum_fusion.2.lhs2_ref, bf16[256,16]{1,0:T(8,128)(2,1)} %copy.32.wk_ref), custom_call_target="tpu_custom_call" | custom-call | tf_op jit(solution)/shard_map/pallas_call | solution.py:120
  183.2 1.5 slice_divide_fusion.1
  184.8 0.1 copy.33
  184.8 0.1 div.29
  185.0 0.1 copy.34
  185.0 0.1 div.31
  185.2 1.1 copy.35
  186.3 0.2 copy.36
  186.5 16.0 %all-gather = bf16[16,4,1600]{2,1,0:T(4,128)(2,1)S(1)} all-gather(bf16[1,4,1600]{2,1,0:T(4,128)(2,1)S(1)} %copy.36), channel_id=1, replica_groups=mesh['wide'=16,'narrow'=16] {'wide'}, dimensions={0}, use_global_device_ids=true | all-gather | bytes 217600 | tf_op jit(solution)/shard_map/all_gather | solution.py:179
  202.5 0.1 reshape.225
  202.6 0.0 copy-done
  202.6 0.4 fusion.36
  203.1 0.7 reshape.223
  203.7 6.5 %all-to-all-start = ((f32[16,4,320]{2,1,0:T(4,128)}), f32[16,4,320]{2,1,0:T(4,128)S(1)}, u32[]{:S(2)}, u32[]{:S(2)}) async-start(f32[16,4,320]{2,1,0:T(4,128)} %reshape.223), calls=%async_computation | async-start | bytes 196608 | tf_op jit(solution)/shard_map/all_to_all | solution.py:184
  210.3 0.6 copy.37
  210.9 6.0 %all-to-all-done = f32[16,4,320]{2,1,0:T(4,128)S(1)} async-done(((f32[16,4,320]{2,1,0:T(4,128)}), f32[16,4,320]{2,1,0:T(4,128)S(1)}, u32[]{:S(2)}, u32[]{:S(2)}) %all-to-all-start) | async-done | bytes 81952 | tf_op jit(solution)/shard_map/all_to_all | solution.py:184
  216.9 0.6 reduce_sum.9
  (12 shorter events, 0.1 us)
Async XLA Ops:
  7.2 195.4 %copy-start = (bf16[1600,320]{0,1:T(8,128)(2,1)S(1)}, bf16[1600,320]{0,1:T(8,128)(2,1)}, u32[]{:S(2)}) copy-start(bf16[1600,320]{0,1:T(8,128)(2,1)} %param.7) | copy-start | bytes 3072004
  7.2 136.3 %all-reduce.3.cloned.1.call-start = ((), (), s32[]{:S(2)}) async-start(), calls=%async_computation.1 | async-start | bytes 3244032 | tf_op jit(solution)/shard_map/psum | solution.py:166
  27.3 0.8 copy-start.1
  27.3 2.5 %copy-start.2 = (s32[2,5,80]{2,0,1:T(2,128)S(1)}, s32[2,5,80]{2,0,1:T(2,128)}, u32[]{:S(2)}) copy-start(s32[2,5,80]{2,0,1:T(2,128)} %param.6) | copy-start | bytes 9604
  203.7 13.2 %all-to-all-start = ((f32[16,4,320]{2,1,0:T(4,128)}), f32[16,4,320]{2,1,0:T(4,128)S(1)}, u32[]{:S(2)}, u32[]{:S(2)}) async-start(f32[16,4,320]{2,1,0:T(4,128)} %reshape.223), calls=%async_computation | async-start | bytes 196608 | tf_op jit(solution)/shard_map/all_to_all | solution.py:184
Sparse Core Ops, SparseCore 0:
  26.8 116.6 all-reduce.2

commit v11 on v10

--- a/solution.py
+++ b/solution.py
@@ -64,15 +64,17 @@
     item = pl.program_id(0)
     items = pl.num_programs(0)
     layers, slab_rows, width = slab_ref.shape
-    rows = slab_rows - SPREAD - 8
+    rows = slab_rows - SPREAD - 16
+    span = PUP + SPREAD + LANES - SPREAD
     ph = jnp.zeros((rows, PUP), f32)
     for which_layer in range(layers):
         row_at = rel_ref[item * layers + which_layer]
         col_at = rel_ref[(items + item) * layers + which_layer]
-        base = pl.multiple_of((row_at // 8) * 8, 8)
-        window = slab_ref[which_layer, pl.ds(base, rows + 8), :]
-        window = pltpu.roll(window, (rows + 8 - (row_at - base)) % (rows + 8), 0)
-        window = pltpu.roll(window, (width - col_at) % width, 1)
+        base = pl.multiple_of((row_at // 16) * 16, 16)
+        col_base = pl.multiple_of((col_at // LANES) * LANES, LANES)
+        window = slab_ref[which_layer, pl.ds(base, rows + 16), pl.ds(col_base, span)].astype(f32)
+        window = pltpu.roll(window, (rows + 16 - (row_at - base)) % (rows + 16), 0)
+        window = pltpu.roll(window, (span - (col_at - col_base)) % span, 1)
         ph = ph + window[:rows, :PUP]
     fc = jnp.cos(ph).astype(bf16)
     fs = jnp.sin(ph).astype(bf16)
@@ -114,8 +116,6 @@
 def centroids_kernel(slabs, rel, sub_rows, items):
     rows = sub_rows * SAMP
     groups = PUP // LANES
-    width = -(-slabs.shape[2] // LANES) * LANES
-    slabs = jnp.pad(slabs.astype(f32), ((0, 0), (0, 8), (0, width - slabs.shape[2])))
     rhs1, lhs2, wk = dft_operands(sub_rows)
     sums = pl.pallas_call(
         centroid_kernel,
@@ -153,18 +153,17 @@
     local_items = FR_DEV * NSENS
     own_offsets = lax.dynamic_slice_in_dim(offsets, wide_index * local_items, local_items, 1)
     lowest = jnp.min(offsets, axis=1)
-    pad = jnp.zeros((slab_rows, union_cols), screens.dtype)
+    picked = slab_rows + 16
+    local_row = jnp.arange(band_rows, dtype=jnp.int32)
     slabs = []
     for which_layer in range(L):
-        band = lax.dynamic_slice(
-            screens, (which_layer, 0, lowest[1, which_layer]), (1, band_rows, union_cols)
-        )[0]
-        padded = jnp.concatenate([pad, band, pad], axis=0)
-        group_start = lowest[0, which_layer] + pixel_rows * narrow_index
-        row_at = jnp.clip(group_start - wide_index * band_rows + slab_rows, 0, band_rows + slab_rows)
-        slabs.append(lax.dynamic_slice_in_dim(padded, row_at, slab_rows, 0))
+        first = lowest[0, which_layer] + pixel_rows * narrow_index - wide_index * band_rows
+        wanted = first + jnp.arange(picked, dtype=jnp.int32)
+        select = (wanted[:, None] == local_row[None, :]).astype(screens.dtype)
+        rows_of = jnp.dot(select, screens[which_layer], preferred_element_type=f32)
+        slabs.append(rows_of.astype(screens.dtype))
     slabs = lax.psum(jnp.stack(slabs), "wide")
-    rel = own_offsets - lowest[:, None, :]
+    rel = jnp.stack([own_offsets[0] - lowest[0][None, :], own_offsets[1]])
     measured = centroids_kernel(slabs, rel, sub_rows, local_items)
     measured = measured.reshape(FR_DEV, NSENS, sub_rows, NSUB, 2) * valid[None, :, :, :, None].astype(
         jnp.float32

time: 225 us -> 233 us (1.036)
  waiting for transfers between devices: 118 us -> 129 us
  matrix products: 0.43 us -> 11.3 us
  between operations: 24.2 us -> 16.9 us
  other arithmetic: 13.6 us -> 8.91 us
  local copies, waits for them, and re-layouts: 9.56 us -> 6.24 us
    psum x1, waiting for transfers between devices: 112 us -> 123 us  [body(): slabs = lax.psum(jnp.stack(slabs), 'wide')]
    dot_general x0 -> x4, matrix products: none -> 10.9 us  [body(): rows_of = jnp.dot(select, screens[which_layer], preferred_element_type=f32)]
    pad x1 -> x0, other arithmetic: 3.38 us -> none  [centroids_kernel(): jnp.pad(slabs.astype(f32), ((0, 0), (0, 8), (0, width - slabs.shape[2])))]
    squeeze x1 -> x0, local copies, waits for them, and re-layouts: 3.27 us -> none  [body(): lax.dynamic_slice(screens, (which_layer, 0, lowest[1, which_layer]), (1,...]
    another operation x2 -> x1, other arithmetic: 4.66 us -> 3.31 us  [body(): slabs = lax.psum(jnp.stack(slabs), 'wide')]
  transfers between devices with their start and end apart: 2 -> 2, of which waited for: 2 -> 2; matrix products, arithmetic and copies ran while one was open for 3% -> 2% of each run, Pallas kernels for 0% -> 0%
where the time goes in v11:
time: 233 us
  waiting for transfers between devices  129 us (55%)
  Pallas kernels  37.8 us (16%)
  between operations  16.9 us (7%)
  blocking collectives  16.3 us (7%)
  matrix products  11.3 us (5%)
  other arithmetic  8.91 us (4%)
  starting transfers between devices  6.57 us (3%)
  local copies, waits for them, and re-layouts  6.24 us (3%)
    psum x1, waiting for transfers between devices, body(): slabs = lax.psum(jnp.stack(slabs), 'wide')  123 us
    pallas_call x1, Pallas kernels, centroids_kernel(): pl.pallas_call(centroid_kernel, grid_spec=pltpu.PrefetchScalarGridSpec(nu...  37.8 us
    all_gather x1, blocking collectives, body(): lax.all_gather(slope_vector, 'wide', axis=0, tiled=True)  16.3 us
    dot_general x4, matrix products, body(): rows_of = jnp.dot(select, screens[which_layer], preferred_element_type=f32)  10.9 us
    all_to_all x1, starting transfers between devices, body(): commands = jnp.sum(lax.all_to_all(partial_commands, 'narrow', 0, 0), axis=0)  6.53 us
    all_to_all x1, waiting for transfers between devices, body(): commands = jnp.sum(lax.all_to_all(partial_commands, 'narrow', 0, 0), axis=0)  6.03 us
  transfers between devices with their start and end apart: 2, of which 2 were waited for; matrix products, arithmetic and copies ran while one was open for 2% of the time, Pallas kernels for 0%

profile of v11, /device:TPU:1, one launch (start us, length us, event | category | flops | bytes accessed | tf_op | source)
XLA Modules:
  0.0 232.9 jit_solution(6208105899993795591)
XLA Ops:
  7.2 0.0 copy-start
  7.2 0.0 all-reduce.2.cloned.1.call-start
  7.2 0.9 reduce_min.9
  8.1 0.6 fusion.38
  10.1 2.1 fusion
  12.2 3.2 %fusion.1 = bf16[1,160,4096]{2,1,0:T(8,128)(2,1)} fusion(bf16[4,256,4096]{2,1,0:T(8,128)(2,1)} %param.4, s32[160]{0:T(256)S(1)} %iota_add_fusion.2), kind=kOutput, calls=%fused_computation.6 | convolution fusion | flops 336240640 | bytes 3408512 | tf_op jit(solution)/shard_map/dot_general | solution.py:163
  16.1 3.2 %fusion.2 = bf16[1,160,4096]{2,1,0:T(8,128)(2,1)} fusion(bf16[4,256,4096]{2,1,0:T(8,128)(2,1)} %param.4, s32[160]{0:T(256)S(1)} %iota_add_fusion.1), kind=kOutput, calls=%fused_computation.7 | convolution fusion | flops 336240640 | bytes 3408512 | tf_op jit(solution)/shard_map/dot_general | solution.py:163
  19.9 0.0 copy-start.1
  20.0 0.0 copy-start.2
  20.0 2.3 fusion.3
  22.3 0.0 copy-done.1
  22.3 0.0 copy-done.2
  22.3 3.3 %pad_maximum_fusion = bf16[4,160,4096]{2,1,0:T(8,128)(2,1)} fusion(bf16[1,160,4096]{2,1,0:T(8,128)(2,1)S(1)} %fusion.3, bf16[1,160,4096]{2,1,0:T(8,128)(2,1)S(1)} %copy-done.2, bf16[1,160,4096]{2,1,0:T(8,128)(2,1)S(1)} %copy-done.1, bf16[1,160,4096]{2,1,0:T(8,128)(2,1)S(1)} %fusion), kind=kLoop, calls=%fused_computation | loop fusion | flops 7864320 | bytes 10485760 | tf_op jit(solution)/shard_map/stack | solution.py:165
  25.6 0.0 all-reduce.2.cloned.1.call-update
  25.6 0.1 copy.31
  25.7 0.1 fusion.32
  25.8 0.0 copy-start.3
  25.8 0.2 broadcast_multiply_fusion
  26.0 0.0 copy-start.4
  26.0 0.2 mul.269
  26.2 0.2 mul.266
  26.4 0.1 fusion.30
  26.4 0.1 broadcast_multiply_fusion.2
  26.6 0.1 mul.281
  26.7 0.1 copy.27
  26.8 0.1 mul.278
  26.9 0.1 copy.28
  27.0 0.0 copy-done.3
  27.0 0.1 dynamic-slice_subtract_fusion
  27.1 0.1 copy.26
  27.2 0.6 reshape.242.rel_ref
  27.8 0.1 mul.282
  27.9 0.1 reshape.243
  28.0 0.1 mul.284
  28.1 0.7 copy.32.wk_ref
  28.8 0.0 copy-done.4
  28.8 0.2 reduce-precision_convert_fusion.1
  29.0 0.9 pad_maximum_fusion.2.lhs2_ref
  29.9 0.1 reduce-precision_convert_fusion
  30.0 0.8 pad_maximum_fusion.1.rhs1_ref
  30.8 123.0 %all-reduce.2.cloned.1.call-done.slab_ref = bf16[4,160,4096]{2,1,0:T(8,128)(2,1)} async-done(((bf16[4,160,4096]{2,1,0:T(8,128)(2,1)}), bf16[4,160,4096]{2,1,0:T(8,128)(2,1)}) %all-reduce.2.cloned.1.call-update) | async-done | bytes 5242896 | tf_op jit(solution)/shard_map/psum | solution.py:165
  153.8 37.8 %shard_map.59 = f32[8,10,16,16]{3,2,1,0:T(8,128)} custom-call(s32[64]{0:T(128)} %reshape.242.rel_ref, bf16[4,160,4096]{2,1,0:T(8,128)(2,1)} %all-reduce.2.cloned.1.call-done.slab_ref, bf16[512,512]{1,0:T(8,128)(2,1)} %pad_maximum_fusion.1.rhs1_ref, bf16[320,480]{1,0:T(8,128)(2,1)} %pad_maximum_fusion.2.lhs2_ref, bf16[256,16]{1,0:T(8,128)(2,1)} %copy.32.wk_ref), custom_call_target="tpu_custom_call" | custom-call | tf_op jit(solution)/shard_map/pallas_call | solution.py:120
  191.5 1.5 slice_divide_fusion.1
  193.1 0.1 copy.33
  193.1 0.1 div.29
  193.3 0.1 copy.34
  193.3 0.1 div.31
  193.5 1.1 copy.35
  194.6 0.2 copy.36
  194.8 16.3 %all-gather = bf16[16,4,1600]{2,1,0:T(4,128)(2,1)S(1)} all-gather(bf16[1,4,1600]{2,1,0:T(4,128)(2,1)S(1)} %copy.36), channel_id=1, replica_groups=mesh['wide'=16,'narrow'=16] {'wide'}, dimensions={0}, use_global_device_ids=true | all-gather | bytes 217600 | tf_op jit(solution)/shard_map/all_gather | solution.py:178
  211.1 0.1 reshape.246
  211.2 0.0 copy-done
  211.2 0.4 fusion.39
  211.6 0.7 reshape.244
  212.3 6.5 %all-to-all-start = ((f32[16,4,320]{2,1,0:T(4,128)}), f32[16,4,320]{2,1,0:T(4,128)S(1)}, u32[]{:S(2)}, u32[]{:S(2)}) async-start(f32[16,4,320]{2,1,0:T(4,128)} %reshape.244), calls=%async_computation | async-start | bytes 196608 | tf_op jit(solution)/shard_map/all_to_all | solution.py:183
  218.8 0.6 copy.37
  219.4 6.0 %all-to-all-done = f32[16,4,320]{2,1,0:T(4,128)S(1)} async-done(((f32[16,4,320]{2,1,0:T(4,128)}), f32[16,4,320]{2,1,0:T(4,128)S(1)}, u32[]{:S(2)}, u32[]{:S(2)}) %all-to-all-start) | async-done | bytes 81952 | tf_op jit(solution)/shard_map/all_to_all | solution.py:183
  225.5 0.6 reduce_sum.9
  (17 shorter events, 0.1 us)
Async XLA Ops:
  7.2 204.0 %copy-start = (bf16[1600,320]{0,1:T(8,128)(2,1)S(1)}, bf16[1600,320]{0,1:T(8,128)(2,1)}, u32[]{:S(2)}) copy-start(bf16[1600,320]{0,1:T(8,128)(2,1)} %param.7) | copy-start | bytes 3072004
  7.2 146.6 %all-reduce.2.cloned.1.call-start = ((), (), s32[]{:S(2)}) async-start(), calls=%async_computation.1 | async-start | bytes 10485760 | tf_op jit(solution)/shard_map/psum | solution.py:165
  19.9 2.3 %copy-start.1 = (bf16[1,160,4096]{2,1,0:T(8,128)(2,1)S(1)}, bf16[1,160,4096]{2,1,0:T(8,128)(2,1)}, u32[]{:S(2)}) copy-start(bf16[1,160,4096]{2,1,0:T(8,128)(2,1)} %fusion.1) | copy-start | bytes 3932164
  20.0 2.3 %copy-start.2 = (bf16[1,160,4096]{2,1,0:T(8,128)(2,1)S(1)}, bf16[1,160,4096]{2,1,0:T(8,128)(2,1)}, u32[]{:S(2)}) copy-start(bf16[1,160,4096]{2,1,0:T(8,128)(2,1)} %fusion.2) | copy-start | bytes 3932164
  25.8 1.2 copy-start.3
  26.0 2.9 %copy-start.4 = (s32[2,5,80]{2,0,1:T(2,128)S(1)}, s32[2,5,80]{2,0,1:T(2,128)}, u32[]{:S(2)}) copy-start(s32[2,5,80]{2,0,1:T(2,128)} %param.6) | copy-start | bytes 9604
  212.3 13.2 %all-to-all-start = ((f32[16,4,320]{2,1,0:T(4,128)}), f32[16,4,320]{2,1,0:T(4,128)S(1)}, u32[]{:S(2)}, u32[]{:S(2)}) async-start(f32[16,4,320]{2,1,0:T(4,128)} %reshape.244), calls=%async_computation | async-start | bytes 196608 | tf_op jit(solution)/shard_map/all_to_all | solution.py:183
Sparse Core Ops, SparseCore 0:
  25.8 127.9 all-reduce.1

commit v12 on v10

--- a/solution.py
+++ b/solution.py
@@ -64,14 +64,14 @@
     item = pl.program_id(0)
     items = pl.num_programs(0)
     layers, slab_rows, width = slab_ref.shape
-    rows = slab_rows - SPREAD - 8
+    rows = slab_rows - SPREAD - 16
     ph = jnp.zeros((rows, PUP), f32)
     for which_layer in range(layers):
         row_at = rel_ref[item * layers + which_layer]
         col_at = rel_ref[(items + item) * layers + which_layer]
-        base = pl.multiple_of((row_at // 8) * 8, 8)
-        window = slab_ref[which_layer, pl.ds(base, rows + 8), :]
-        window = pltpu.roll(window, (rows + 8 - (row_at - base)) % (rows + 8), 0)
+        base = pl.multiple_of((row_at // 16) * 16, 16)
+        window = slab_ref[which_layer, pl.ds(base, rows + 16), :].astype(f32)
+        window = pltpu.roll(window, (rows + 16 - (row_at - base)) % (rows + 16), 0)
         window = pltpu.roll(window, (width - col_at) % width, 1)
         ph = ph + window[:rows, :PUP]
     fc = jnp.cos(ph).astype(bf16)
@@ -114,8 +114,6 @@
 def centroids_kernel(slabs, rel, sub_rows, items):
     rows = sub_rows * SAMP
     groups = PUP // LANES
-    width = -(-slabs.shape[2] // LANES) * LANES
-    slabs = jnp.pad(slabs.astype(f32), ((0, 0), (0, 8), (0, width - slabs.shape[2])))
     rhs1, lhs2, wk = dft_operands(sub_rows)
     sums = pl.pallas_call(
         centroid_kernel,
@@ -148,8 +146,8 @@
     band_rows = screens.shape[1]
     sub_rows = valid.shape[1]
     pixel_rows = sub_rows * SAMP
-    slab_rows = pixel_rows + SPREAD
-    union_cols = PUP + SPREAD
+    slab_rows = pixel_rows + SPREAD + 16
+    union_cols = PUP + LANES
     local_items = FR_DEV * NSENS
     own_offsets = lax.dynamic_slice_in_dim(offsets, wide_index * local_items, local_items, 1)
     lowest = jnp.min(offsets, axis=1)

time: 225 us -> 223 us (level)
  other arithmetic: 13.6 us -> 10.5 us
    pad x1 -> x0, other arithmetic: 3.38 us -> none  [centroids_kernel(): jnp.pad(slabs.astype(f32), ((0, 0), (0, 8), (0, width - slabs.shape[2])))]
where the time goes in v12:
time: 223 us
  waiting for transfers between devices  119 us (53%)
  Pallas kernels  36.9 us (17%)
  between operations  24.2 us (11%)
  blocking collectives  15.9 us (7%)
  other arithmetic  10.5 us (5%)
  local copies, waits for them, and re-layouts  9.56 us (4%)
  starting transfers between devices  6.56 us (3%)
    psum x1, waiting for transfers between devices, body(): slabs = lax.psum(jnp.stack(slabs), 'wide')  113 us
    pallas_call x1, Pallas kernels, centroids_kernel(): pl.pallas_call(centroid_kernel, grid_spec=pltpu.PrefetchScalarGridSpec(nu...  36.9 us
    all_gather x1, blocking collectives, body(): lax.all_gather(slope_vector, 'wide', axis=0, tiled=True)  15.9 us
    all_to_all x1, starting transfers between devices, body(): commands = jnp.sum(lax.all_to_all(partial_commands, 'narrow', 0, 0), axis=0)  6.53 us
    all_to_all x1, waiting for transfers between devices, body(): commands = jnp.sum(lax.all_to_all(partial_commands, 'narrow', 0, 0), axis=0)  6.03 us
    another operation x2, other arithmetic, body(): slabs = lax.psum(jnp.stack(slabs), 'wide')  5.03 us
  transfers between devices with their start and end apart: 2, of which 2 were waited for; matrix products, arithmetic and copies ran while one was open for 3% of the time, Pallas kernels for 0%

profile of v12, /device:TPU:1, one launch (start us, length us, event | category | flops | bytes accessed | tf_op | source)
XLA Modules:
  0.0 222.9 jit_solution(4147071483627341456)
XLA Ops:
  7.2 0.0 copy-start
  7.2 0.0 all-reduce.2.cloned.1.call-start
  7.2 0.9 reduce_min.9
  8.1 0.7 fusion.35
  18.7 3.3 %dynamic-slice_bitcast_fusion.3 = (bf16[256,1408]{1,0:T(8,128)(2,1)S(1)}, bf16[256,1408]{1,0:T(8,128)(2,1)S(1)}, bf16[256,1408]{1,0:T(8,128)(2,1)S(1)}, bf16[256,1408]{1,0:T(8,128)(2,1)S(1)}) fusion(bf16[4,256,4096]{2,1,0:T(8,128)(2,1)} %param.4, s32[]{:T(128)S(6)} %select_n.57, s32[]{:T(128)S(6)} %select_n.58, s32[]{:T(128)S(6)} %select_n.60, s32[]{:T(128)S(6)} %select_n.59), kind=kLoop, calls=%fused_computation.18 | loop fusion | bytes 5767184 | tf_op jit(solution)/shard_map/squeeze | solution.py:157
  22.0 3.5 %fusion.12 = (bf16[1,160,1408]{2,1,0:T(8,128)(2,1)S(1)}, bf16[1,160,1408]{2,1,0:T(8,128)(2,1)S(1)}, bf16[1,160,1408]{2,1,0:T(8,128)(2,1)S(1)}, bf16[1,160,1408]{2,1,0:T(8,128)(2,1)S(1)}) fusion(s32[]{:T(128)S(6)} %min.13, bf16[160,1408]{1,0:T(8,128)(2,1)S(1)} %broadcast_in_dim.2, bf16[256,1408]{1,0:T(8,128)(2,1)S(1)} %get-tuple-element.8, s32[]{:T(128)S(6)} %min.15, ...), kind=kLoop, calls=%fused_computation.35 | loop fusion | flops 5406720 | bytes 5136400 | tf_op jit(solution)/shard_map/stack | solution.py:164
  25.6 1.5 pad_maximum_fusion
  27.1 0.0 all-reduce.2.cloned.1.call-update
  27.1 0.1 fusion.29
  27.2 0.1 fusion.27
  27.2 0.1 copy.31
  27.3 0.2 broadcast_multiply_fusion
  27.5 0.2 mul.269
  27.7 0.0 copy-start.1
  27.7 0.0 copy-start.2
  27.7 0.2 mul.266
  27.9 0.1 broadcast_multiply_fusion.2
  28.0 0.1 mul.281
  28.1 0.1 copy.27
  28.2 0.1 mul.278
  28.4 0.1 copy.28
  28.5 0.0 copy-done.1
  28.5 0.1 fusion.26
  28.5 0.1 copy.26
  28.6 0.6 reshape.221.rel_ref
  29.2 0.1 mul.282
  29.3 0.1 reshape.222
  29.4 0.1 mul.284
  29.5 0.7 copy.32.wk_ref
  30.2 0.0 copy-done.2
  30.2 0.2 reduce-precision_convert_fusion.1
  30.4 0.9 pad_maximum_fusion.2.lhs2_ref
  31.3 0.1 reduce-precision_convert_fusion
  31.4 0.8 pad_maximum_fusion.1.rhs1_ref
  32.2 112.8 %all-reduce.2.cloned.1.call-done.slab_ref = bf16[4,160,1408]{2,1,0:T(8,128)(2,1)} async-done(((bf16[4,160,1408]{2,1,0:T(8,128)(2,1)}), bf16[4,160,1408]{2,1,0:T(8,128)(2,1)}) %all-reduce.2.cloned.1.call-update) | async-done | bytes 1802256 | tf_op jit(solution)/shard_map/psum | solution.py:164
  145.0 36.9 %shard_map.59 = f32[8,10,16,16]{3,2,1,0:T(8,128)} custom-call(s32[64]{0:T(128)} %reshape.221.rel_ref, bf16[4,160,1408]{2,1,0:T(8,128)(2,1)} %all-reduce.2.cloned.1.call-done.slab_ref, bf16[512,512]{1,0:T(8,128)(2,1)} %pad_maximum_fusion.1.rhs1_ref, bf16[320,480]{1,0:T(8,128)(2,1)} %pad_maximum_fusion.2.lhs2_ref, bf16[256,16]{1,0:T(8,128)(2,1)} %copy.32.wk_ref), custom_call_target="tpu_custom_call" | custom-call | tf_op jit(solution)/shard_map/pallas_call | solution.py:118
  181.9 1.4 slice_divide_fusion.1
  183.4 0.1 copy.33
  183.4 0.1 div.29
  183.6 0.1 copy.34
  183.6 0.1 div.31
  183.8 1.1 copy.35
  184.9 0.2 copy.36
  185.1 15.9 %all-gather = bf16[16,4,1600]{2,1,0:T(4,128)(2,1)S(1)} all-gather(bf16[1,4,1600]{2,1,0:T(4,128)(2,1)S(1)} %copy.36), channel_id=1, replica_groups=mesh['wide'=16,'narrow'=16] {'wide'}, dimensions={0}, use_global_device_ids=true | all-gather | bytes 217600 | tf_op jit(solution)/shard_map/all_gather | solution.py:177
  201.0 0.1 reshape.225
  201.1 0.0 copy-done
  201.2 0.4 fusion.36
  201.6 0.7 reshape.223
  202.3 6.5 %all-to-all-start = ((f32[16,4,320]{2,1,0:T(4,128)}), f32[16,4,320]{2,1,0:T(4,128)S(1)}, u32[]{:S(2)}, u32[]{:S(2)}) async-start(f32[16,4,320]{2,1,0:T(4,128)} %reshape.223), calls=%async_computation | async-start | bytes 196608 | tf_op jit(solution)/shard_map/all_to_all | solution.py:182
  208.8 0.6 copy.37
  209.4 6.0 %all-to-all-done = f32[16,4,320]{2,1,0:T(4,128)S(1)} async-done(((f32[16,4,320]{2,1,0:T(4,128)}), f32[16,4,320]{2,1,0:T(4,128)S(1)}, u32[]{:S(2)}, u32[]{:S(2)}) %all-to-all-start) | async-done | bytes 81952 | tf_op jit(solution)/shard_map/all_to_all | solution.py:182
  215.5 0.6 reduce_sum.9
  (12 shorter events, 0.1 us)
Async XLA Ops:
  7.2 194.0 %copy-start = (bf16[1600,320]{0,1:T(8,128)(2,1)S(1)}, bf16[1600,320]{0,1:T(8,128)(2,1)}, u32[]{:S(2)}) copy-start(bf16[1600,320]{0,1:T(8,128)(2,1)} %param.7) | copy-start | bytes 3072004
  7.2 137.8 %all-reduce.2.cloned.1.call-start = ((), (), s32[]{:S(2)}) async-start(), calls=%async_computation.1 | async-start | bytes 3604480 | tf_op jit(solution)/shard_map/psum | solution.py:164
  27.7 0.8 copy-start.1
  27.7 2.6 %copy-start.2 = (s32[2,5,80]{2,0,1:T(2,128)S(1)}, s32[2,5,80]{2,0,1:T(2,128)}, u32[]{:S(2)}) copy-start(s32[2,5,80]{2,0,1:T(2,128)} %param.6) | copy-start | bytes 9604
  202.3 13.2 %all-to-all-start = ((f32[16,4,320]{2,1,0:T(4,128)}), f32[16,4,320]{2,1,0:T(4,128)S(1)}, u32[]{:S(2)}, u32[]{:S(2)}) async-start(f32[16,4,320]{2,1,0:T(4,128)} %reshape.223), calls=%async_computation | async-start | bytes 196608 | tf_op jit(solution)/shard_map/all_to_all | solution.py:182
Sparse Core Ops, SparseCore 0:
  27.2 117.7 all-reduce.1

commit v13 on v12

--- a/solution.py
+++ b/solution.py
@@ -151,16 +151,16 @@
     local_items = FR_DEV * NSENS
     own_offsets = lax.dynamic_slice_in_dim(offsets, wide_index * local_items, local_items, 1)
     lowest = jnp.min(offsets, axis=1)
-    pad = jnp.zeros((slab_rows, union_cols), screens.dtype)
+    local_row = jnp.arange(band_rows, dtype=jnp.int32)
     slabs = []
     for which_layer in range(L):
         band = lax.dynamic_slice(
             screens, (which_layer, 0, lowest[1, which_layer]), (1, band_rows, union_cols)
         )[0]
-        padded = jnp.concatenate([pad, band, pad], axis=0)
-        group_start = lowest[0, which_layer] + pixel_rows * narrow_index
-        row_at = jnp.clip(group_start - wide_index * band_rows + slab_rows, 0, band_rows + slab_rows)
-        slabs.append(lax.dynamic_slice_in_dim(padded, row_at, slab_rows, 0))
+        first = lowest[0, which_layer] + pixel_rows * narrow_index - wide_index * band_rows
+        wanted = first + jnp.arange(slab_rows, dtype=jnp.int32)
+        select = (wanted[:, None] == local_row[None, :]).astype(screens.dtype)
+        slabs.append(jnp.dot(select, band, preferred_element_type=f32).astype(screens.dtype))
     slabs = lax.psum(jnp.stack(slabs), "wide")
     rel = own_offsets - lowest[:, None, :]
     measured = centroids_kernel(slabs, rel, sub_rows, local_items)

time: 223 us -> 223 us (level)
  matrix products: 0.43 us -> 6.95 us
  other arithmetic: 10.5 us -> 6.97 us
  local copies, waits for them, and re-layouts: 9.56 us -> 6.26 us
    dot_general x0 -> x4, matrix products: none -> 6.52 us  [body(): jnp.dot(select, band, preferred_element_type=f32).astype(screens.dtype)]
    another operation x2 -> x1, other arithmetic: 5.03 us -> 1.5 us  [body(): slabs = lax.psum(jnp.stack(slabs), 'wide')]
    squeeze x1 -> x0, local copies, waits for them, and re-layouts: 3.27 us -> none  [body(): lax.dynamic_slice(screens, (which_layer, 0, lowest[1, which_layer]), (1,...]
where the time goes in v13:
time: 223 us
  waiting for transfers between devices  119 us (53%)
  Pallas kernels  36.8 us (17%)
  between operations  24.4 us (11%)
  blocking collectives  15.9 us (7%)
  other arithmetic  6.97 us (3%)
  matrix products  6.95 us (3%)
  starting transfers between devices  6.57 us (3%)
  local copies, waits for them, and re-layouts  6.26 us (3%)
    psum x1, waiting for transfers between devices, body(): slabs = lax.psum(jnp.stack(slabs), 'wide')  113 us
    pallas_call x1, Pallas kernels, centroids_kernel(): pl.pallas_call(centroid_kernel, grid_spec=pltpu.PrefetchScalarGridSpec(nu...  36.8 us
    all_gather x1, blocking collectives, body(): lax.all_gather(slope_vector, 'wide', axis=0, tiled=True)  15.9 us
    all_to_all x1, starting transfers between devices, body(): commands = jnp.sum(lax.all_to_all(partial_commands, 'narrow', 0, 0), axis=0)  6.53 us
    dot_general x4, matrix products, body(): jnp.dot(select, band, preferred_element_type=f32).astype(screens.dtype)  6.52 us
    all_to_all x1, waiting for transfers between devices, body(): commands = jnp.sum(lax.all_to_all(partial_commands, 'narrow', 0, 0), axis=0)  6.03 us
  transfers between devices with their start and end apart: 2, of which 2 were waited for; matrix products, arithmetic and copies ran while one was open for 3% of the time, Pallas kernels for 0%

profile of v13, /device:TPU:1, one launch (start us, length us, event | category | flops | bytes accessed | tf_op | source)
XLA Modules:
  0.0 222.7 jit_solution(11723778506520317781)
XLA Ops:
  7.2 0.0 copy-start
  7.2 0.0 all-reduce.2.cloned.1.call-start
  7.2 0.9 reduce_min.9
  8.1 0.7 fusion.45
  17.7 1.6 fusion
  19.3 1.6 fusion.1
  21.6 1.6 fusion.2
  23.9 1.6 fusion.3
  25.5 1.5 pad_maximum_fusion
  27.0 0.0 all-reduce.2.cloned.1.call-update
  27.0 0.1 fusion.32
  27.1 0.1 fusion.30
  27.2 0.1 copy.31
  27.3 0.2 broadcast_multiply_fusion
  27.4 0.0 copy-start.1
  27.4 0.0 copy-start.2
  27.4 0.2 mul.269
  27.6 0.2 mul.266
  27.8 0.1 broadcast_multiply_fusion.2
  28.0 0.1 mul.281
  28.1 0.1 copy.27
  28.2 0.1 mul.278
  28.3 0.1 copy.28
  28.4 0.0 copy-done.1
  28.4 0.1 dynamic-slice_subtract_fusion
  28.5 0.1 copy.26
  28.6 0.6 reshape.237.rel_ref
  29.2 0.1 mul.282
  29.3 0.1 reshape.238
  29.3 0.1 mul.284
  29.4 0.7 copy.32.wk_ref
  30.2 0.0 copy-done.2
  30.2 0.2 reduce-precision_convert_fusion.1
  30.3 0.9 pad_maximum_fusion.2.lhs2_ref
  31.3 0.1 reduce-precision_convert_fusion
  31.3 0.8 pad_maximum_fusion.1.rhs1_ref
  32.1 112.8 %all-reduce.2.cloned.1.call-done.slab_ref = bf16[4,160,1408]{2,1,0:T(8,128)(2,1)} async-done(((bf16[4,160,1408]{2,1,0:T(8,128)(2,1)}), bf16[4,160,1408]{2,1,0:T(8,128)(2,1)}) %all-reduce.2.cloned.1.call-update) | async-done | bytes 1802256 | tf_op jit(solution)/shard_map/psum | solution.py:164
  144.9 36.8 %shard_map.59 = f32[8,10,16,16]{3,2,1,0:T(8,128)} custom-call(s32[64]{0:T(128)} %reshape.237.rel_ref, bf16[4,160,1408]{2,1,0:T(8,128)(2,1)} %all-reduce.2.cloned.1.call-done.slab_ref, bf16[512,512]{1,0:T(8,128)(2,1)} %pad_maximum_fusion.1.rhs1_ref, bf16[320,480]{1,0:T(8,128)(2,1)} %pad_maximum_fusion.2.lhs2_ref, bf16[256,16]{1,0:T(8,128)(2,1)} %copy.32.wk_ref), custom_call_target="tpu_custom_call" | custom-call | tf_op jit(solution)/shard_map/pallas_call | solution.py:118
  181.7 1.4 slice_divide_fusion.1
  183.1 0.1 copy.33
  183.2 0.1 div.29
  183.3 0.1 copy.34
  183.4 0.1 div.31
  183.6 1.1 copy.35
  184.7 0.2 copy.36
  184.9 15.9 %all-gather = bf16[16,4,1600]{2,1,0:T(4,128)(2,1)S(1)} all-gather(bf16[1,4,1600]{2,1,0:T(4,128)(2,1)S(1)} %copy.36), channel_id=1, replica_groups=mesh['wide'=16,'narrow'=16] {'wide'}, dimensions={0}, use_global_device_ids=true | all-gather | bytes 217600 | tf_op jit(solution)/shard_map/all_gather | solution.py:177
  200.8 0.1 reshape.241
  200.9 0.0 copy-done
  200.9 0.4 fusion.46
  201.4 0.7 reshape.239
  202.0 6.5 %all-to-all-start = ((f32[16,4,320]{2,1,0:T(4,128)}), f32[16,4,320]{2,1,0:T(4,128)S(1)}, u32[]{:S(2)}, u32[]{:S(2)}) async-start(f32[16,4,320]{2,1,0:T(4,128)} %reshape.239), calls=%async_computation | async-start | bytes 196608 | tf_op jit(solution)/shard_map/all_to_all | solution.py:182
  208.6 0.6 copy.37
  209.2 6.0 %all-to-all-done = f32[16,4,320]{2,1,0:T(4,128)S(1)} async-done(((f32[16,4,320]{2,1,0:T(4,128)}), f32[16,4,320]{2,1,0:T(4,128)S(1)}, u32[]{:S(2)}, u32[]{:S(2)}) %all-to-all-start) | async-done | bytes 81952 | tf_op jit(solution)/shard_map/all_to_all | solution.py:182
  215.2 0.6 reduce_sum.9
  (15 shorter events, 0.1 us)
Async XLA Ops:
  7.2 193.8 %copy-start = (bf16[1600,320]{0,1:T(8,128)(2,1)S(1)}, bf16[1600,320]{0,1:T(8,128)(2,1)}, u32[]{:S(2)}) copy-start(bf16[1600,320]{0,1:T(8,128)(2,1)} %param.7) | copy-start | bytes 3072004
  7.2 137.8 %all-reduce.2.cloned.1.call-start = ((), (), s32[]{:S(2)}) async-start(), calls=%async_computation.1 | async-start | bytes 3604480 | tf_op jit(solution)/shard_map/psum | solution.py:164
  27.4 1.0 copy-start.1
  27.4 2.7 %copy-start.2 = (s32[2,5,80]{2,0,1:T(2,128)S(1)}, s32[2,5,80]{2,0,1:T(2,128)}, u32[]{:S(2)}) copy-start(s32[2,5,80]{2,0,1:T(2,128)} %param.6) | copy-start | bytes 9604
  202.0 13.2 %all-to-all-start = ((f32[16,4,320]{2,1,0:T(4,128)}), f32[16,4,320]{2,1,0:T(4,128)S(1)}, u32[]{:S(2)}, u32[]{:S(2)}) async-start(f32[16,4,320]{2,1,0:T(4,128)} %reshape.239), calls=%async_computation | async-start | bytes 196608 | tf_op jit(solution)/shard_map/all_to_all | solution.py:182
Sparse Core Ops, SparseCore 0:
  27.1 117.7 all-reduce.1
